TPU v7x, 128 devices: a whole 4x4x4 slice. The times are simulated.
128 devices in a mesh: visit: 4 (over x), patch: 32 (over y, z, core).
Axes of the slice: x: 4, y: 4, z: 4, core: 2. Of those that a mesh axis runs over, the one named last changes fastest.
Arguments:
- pixels: bfloat16 [8192, 128, 128], P(('visit', 'patch')), may hold values from -6 to 6
- mask_bits: int32 [8192, 128, 128], P(('visit', 'patch')), may hold values from 0 to 15, as said below
- inv_var: float32 [8192], P(('visit', 'patch')), may hold values from 0.05 to 1
- owner: int32 [8192], P(('visit', 'patch')), may hold values from 0 to 31, as said below
- cell: int32 [8192], P(('visit', 'patch')), may hold values from 0 to 63
- coef_index: int32 [8192], P(('visit', 'patch')), may hold values from 0 to 63
- coef_table: float32 [64, 9], replicated, may hold values from -4 to 4
Outputs:
- coadd: float32 [2048, 128, 128], P('patch', 'visit')
- difference: bfloat16 [8192, 128, 128], P(('visit', 'patch'))
Inputs may be any that keep to these rules, and one draw needn't show every extreme that they name: `owner`: within each device's 64 blocks (aligned runs of 64 in order) no patch is named more than 8 times; one patch, the same for all devices, is named exactly 8 times in every such run. `mask_bits`: each value is a sum of the bit flags 1, 2, 4 and 8.
All inputs are finite; a program needn't handle non-finite values.
Results may differ from a plain program's by a relative error of at most 0.0071.
Values may be sent and summed in bfloat16 or wider, within the bound.
No kernel may reach another device: no remote copies, remote signals or barrier semaphores. Data moves between devices by JAX's collectives and lax.ppermute only.
A program may use at most 128 MiB of HBM per device.

v0:
```python
import jax
import jax.numpy as jnp
from jax import lax
from jax.sharding import PartitionSpec as P

CELLS = 64
KSIZE = 21


gauss_widths = (1.0, 2.0, 3.5)


def band_tables(side_len):
    tap_reach = KSIZE // 2
    position = jnp.arange(side_len).astype(jnp.float32)
    offset = position[:, None] - position[None, :]
    inside = jnp.abs(offset) <= tap_reach
    tap_offsets = jnp.arange(-tap_reach, tap_reach + 1).astype(jnp.float32)
    tables = []
    for spread in gauss_widths:
        profile_sum = jnp.sum(jnp.exp(-tap_offsets * tap_offsets / (2.0 * spread * spread)))
        even_band = jnp.where(
            inside, jnp.exp(-offset * offset / (2.0 * spread * spread)) / profile_sum, 0.0
        )
        tables.append(even_band)
        tables.append(even_band * offset / spread)
    return jnp.stack(tables)


def match_group(blocks, coefficients, tables, right_bands):
    number = blocks.shape[0]
    side_len = blocks.shape[1]
    columns = jnp.dot(
        blocks.reshape(number * side_len, side_len), right_bands, preferred_element_type=jnp.float32
    )
    columns = columns.astype(jnp.bfloat16).reshape(number, side_len, 6, side_len)
    left_parts = []
    for sigma_pos in range(3):
        even_band = tables[2 * sigma_pos]
        odd_band = tables[2 * sigma_pos + 1]
        left_parts.append(
            coefficients[:, 3 * sigma_pos, None, None] * even_band
            + coefficients[:, 3 * sigma_pos + 1, None, None] * odd_band
        )
        left_parts.append(coefficients[:, 3 * sigma_pos + 2, None, None] * even_band)
    left_bands = jnp.stack(left_parts, axis=2).astype(jnp.bfloat16)
    result = jnp.einsum("nisp,npsj->nij", left_bands, columns, preferred_element_type=jnp.float32)
    return result.astype(jnp.bfloat16)


def match_blocks(blocks, coefficients, tables, right_bands):
    number = blocks.shape[0]
    side_len = blocks.shape[1]
    batch_blocks = 16
    rounds = -(-number // batch_blocks)

    def one_batch(bundle):
        return match_group(bundle[0], bundle[1], tables, right_bands)

    matched = lax.map(
        one_batch,
        (
            blocks.reshape(rounds, batch_blocks, side_len, side_len),
            coefficients.reshape(rounds, batch_blocks, coefficients.shape[1]),
        ),
    )
    return matched.reshape(rounds * batch_blocks, side_len, side_len)[:number]


def shards(pixels, mask_bits, inv_var, owner, cell, coef_index, coef_table):
    blocks_here = pixels.shape[0]
    side_len = pixels.shape[1]
    kernel_sets = coef_table.shape[0]
    patches = lax.axis_size("patch")
    visits = lax.axis_size("visit")
    capacity = 4 * blocks_here // patches
    slot_total = patches * capacity
    tables = band_tables(side_len)
    right_bands = (
        jnp.transpose(tables, (2, 0, 1)).reshape(side_len, 6 * side_len).astype(jnp.bfloat16)
    )
    usable = (mask_bits % 2 == 0) & (mask_bits // 2 % 2 == 0) & (mask_bits // 4 % 2 == 0)
    masked = jnp.where(usable, pixels, jnp.zeros((), jnp.bfloat16))
    weight = inv_var.astype(jnp.bfloat16)
    cell_weight = jnp.where(
        cell[:, None] == jnp.arange(CELLS)[None, :], weight[:, None], jnp.zeros((), jnp.bfloat16)
    )
    chosen = (coef_index[:, None] == jnp.arange(kernel_sets)[None, :]).astype(jnp.bfloat16)
    dest_onehot = (owner[:, None] == jnp.arange(patches)[None, :]).astype(jnp.int32)
    slot_rank = jnp.sum((jnp.cumsum(dest_onehot, axis=0) - dest_onehot) * dest_onehot, axis=1)
    slot_of_block = owner * capacity + slot_rank
    matches = slot_of_block[None, :] == jnp.arange(slot_total)[:, None]
    source_row = jnp.sum(jnp.where(matches, jnp.arange(blocks_here)[None, :], 0), axis=1)
    filled = jnp.any(matches, axis=1)

    def pack_slots(values):
        picked = values[source_row]
        keep_rows = filled.reshape((slot_total,) + (1,) * (values.ndim - 1))
        picked = jnp.where(keep_rows, picked, jnp.zeros((), values.dtype))
        return picked.reshape((patches, capacity) + values.shape[1:])

    pieces = lax.all_to_all(pack_slots(masked), "patch", split_axis=0, concat_axis=0, tiled=True)
    weights = lax.all_to_all(
        pack_slots(cell_weight), "patch", split_axis=0, concat_axis=0, tiled=True
    )
    kernel_picks = lax.all_to_all(
        pack_slots(chosen), "patch", split_axis=0, concat_axis=0, tiled=True
    )
    flat_blocks = pieces.reshape((-1, side_len, side_len))
    coefficients = jnp.dot(
        kernel_picks.reshape(-1, kernel_sets).astype(jnp.float32),
        coef_table,
        precision=lax.Precision.HIGHEST,
    )
    matched = match_blocks(flat_blocks, coefficients, tables, right_bands)
    matched_slots = matched.reshape(pieces.shape)
    flat_weights = weights.reshape(slot_total, CELLS)
    flat_matched = matched_slots.reshape(slot_total, side_len * side_len)
    numerator = jnp.einsum(
        "sc,sk->ck", flat_weights, flat_matched, preferred_element_type=jnp.float32
    ).reshape(CELLS, side_len, side_len)
    weight_sum = jnp.sum(flat_weights.astype(jnp.float32), axis=0)
    rows_here = side_len // visits
    numerator, weight_sum = lax.psum((numerator, weight_sum), "visit")
    coadd_full = numerator / jnp.maximum(weight_sum, 1.0)[:, None, None]
    coadd_part = lax.dynamic_slice_in_dim(
        coadd_full, lax.axis_index("visit") * rows_here, rows_here, 1
    )
    template = coadd_full.astype(jnp.bfloat16)
    live_slots = (flat_weights > 0).astype(jnp.bfloat16)
    slot_template = jnp.einsum(
        "sc,ck->sk",
        live_slots,
        template.reshape(CELLS, side_len * side_len),
        preferred_element_type=jnp.float32,
    )
    difference_slots = (flat_matched.astype(jnp.float32) - slot_template).astype(jnp.bfloat16)
    returned = lax.all_to_all(
        difference_slots.reshape(patches, capacity, side_len, side_len),
        "patch",
        split_axis=0,
        concat_axis=0,
        tiled=True,
    )
    difference = returned.reshape(slot_total, side_len, side_len)[slot_of_block]
    return (coadd_part, difference)


def solution(mesh):
    placed = (
        P(("visit", "patch"), None, None),
        P(("visit", "patch"), None, None),
        P(("visit", "patch")),
        P(("visit", "patch")),
        P(("visit", "patch")),
        P(("visit", "patch")),
        P(),
    )
    return jax.shard_map(
        shards,
        mesh=mesh,
        in_specs=placed,
        out_specs=(P("patch", "visit", None), P(("visit", "patch"), None, None)),
        check_vma=False,
    )
```

profile of v0, /device:TPU:32, one launch (start us, length us, event | category | flops | bytes accessed | tf_op | source)
XLA Modules:
  0.0 747.2 jit_solution(13335053271318663736)
XLA Ops:
  14.5 8.2 %all-to-all-start.1 = ((bf16[32,2,256]{2,1,0:T(2,128)(2,1)}), bf16[32,2,256]{2,1,0:T(2,128)(2,1)S(1)}, u32[]{:S(2)}, u32[]{:S(2)}) async-start(bf16[32,2,256]{2,1,0:T(2,128)(2,1)} %reshape.477), calls=%async_computation.1 | async-start | bytes 65536 | tf_op jit(solution)/shard_map/all_to_all | solution.py:106
  22.7 10.7 %fusion.62 = bf16[64,128,128]{2,1,0:T(8,128)(2,1)S(1)} fusion(bf16[64,128,128]{2,1,0:T(8,128)(2,1)} %param.9, s32[64,128,128]{2,1,0:T(8,128)} %param.10), kind=kLoop, calls=%fused_computation.94 | loop fusion | flops 59768832 | bytes 8388608 | tf_op jit(solution)/shard_map/jit(_where)/select_n | solution.py:83
  33.4 8.4 %gather_fusion.2 = bf16[256,128,128]{2,1,0:T(8,128)(2,1)} fusion(bf16[64,128,128]{2,1,0:T(8,128)(2,1)S(1)} %fusion.62, s32[1024]{0:T(1024)S(1)} %pad_clamp_fusion.1), kind=kCustom, calls=%fused_computation.2 | custom fusion | bytes 16778240 | tf_op jit(solution)/shard_map/gather | solution.py:97
  42.5 7.4 all-to-all-start
  49.9 7.2 broadcast_select_fusion
  57.1 7.4 all-to-all-start.2
  72.4 116.4 %all-to-all-done.2 = bf16[32,8,128,128]{3,2,1,0:T(8,128)(2,1)} async-done(((bf16[32,8,128,128]{3,2,1,0:T(8,128)(2,1)}), bf16[32,8,128,128]{3,2,1,0:T(8,128)(2,1)}, u32[]{:S(2)}, u32[]{:S(2)}) %all-to-all-start.2) | async-done | bytes 8388640 | tf_op jit(solution)/shard_map/all_to_all | solution.py:102
  188.8 252.1 %while.12 = (s32[]{:T(128)}, bf16[16,16,128,128]{3,2,1,0:T(8,128)(2,1)}, f32[16,16,9]{1,2,0:T(8,128)S(1)}, bf16[16,16,128,128]{3,2,1,0:T(8,128)(2,1)}, bf16[128,...) while((s32[]{:T(128)}, ...), condition=%wide.region_8.9_spmd.clone.clone, body=%wide.region_7.8_spmd.clone.clone.sunk | while | flops 812171264 | bytes 35789844 | solution.py:60
  231.1 4.9 fusion.129
  246.9 4.9 fusion.129
  309.9 4.9 fusion.129
  341.4 4.9 fusion.129
  404.5 4.9 fusion.129
  440.9 23.1 %copy.59 = bf16[32,8,128,128]{3,1,2,0:T(8,128)(2,1)} copy(bf16[32,8,128,128]{3,2,1,0:T(8,128)(2,1)} %bitcast.114) | data formatting | bytes 16777216
  464.1 11.9 %copy.36 = bf16[16384,256]{1,0:T(8,128)(2,1)} copy(bf16[16384,256]{0,1:T(8,128)(2,1)} %bitcast.117) | data formatting | bytes 16777216 | tf_op jit(solution)/shard_map/sc,sk->ck/dot_general | solution.py:119
  475.9 8.0 %fusion.88 = f32[64,128,128]{2,0,1:T(8,128)} fusion(bf16[128,128,256]{2,1,0:T(8,128)(2,1)} %bitcast.116, bf16[32,8,64]{2,1,0:T(8,128)(2,1)S(1)} %reshape.480), kind=kOutput, calls=%fused_computation.129 | convolution fusion | flops 536870912 | bytes 12615680 | tf_op jit(solution)/shard_map/sc,sk->ck/dot_general | solution.py:119
  484.0 10.7 %psum.15 = f32[64]{0:T(128)S(1)} all-reduce(f32[64]{0:T(128)S(1)} %convert_reduce_fusion), channel_id=1, replica_groups=mesh['visit'=4,'patch'=32] {'visit'}, use_global_device_ids=true, to_apply=%region_11.12 | all-reduce | flops 64 | bytes 512 | tf_op jit(solution)/shard_map/psum | solution.py:124
  494.7 81.7 %all-reduce.2.cloned.1.call-done = f32[64,128,128]{2,0,1:T(8,128)} async-done(((f32[64,128,128]{2,0,1:T(8,128)}), f32[64,128,128]{2,0,1:T(8,128)}) %all-reduce.2.cloned.1.call-update) | async-done | bytes 4194320 | tf_op jit(solution)/shard_map/psum | solution.py:124
  576.4 5.3 convert_bitcast_fusion
  581.7 11.9 %fusion.54 = bf16[32,8,128,128]{3,1,2,0:T(8,128)(2,1)} fusion(bf16[32,8,128,128]{3,2,1,0:T(8,128)(2,1)} %bitcast.115, bf16[128,8,8,128]{3,2,1,0:T(8,128)(2,1)S(1)} %get-tuple-element.195, bf16[32,8,64]{2,1,0:T(8,128)(2,1)S(1)} %reshape.480), kind=kOutput, calls=%fused_computation.85 | convolution fusion | flops 549470208 | bytes 18907136 | tf_op jit(solution)/shard_map/sc,ck->sk/dot_general | solution.py:131
  593.6 9.2 %copy.30 = bf16[32,8,128,128]{3,2,1,0:T(8,128)(2,1)} copy(bf16[32,8,128,128]{3,1,2,0:T(8,128)(2,1)} %fusion.54) | data formatting | bytes 16777216 | tf_op jit(solution)/shard_map/reshape | solution.py:139
  602.7 7.6 %all-to-all-start.3 = ((bf16[32,8,128,128]{3,2,1,0:T(8,128)(2,1)}), bf16[32,8,128,128]{3,2,1,0:T(8,128)(2,1)}, u32[]{:S(2)}, u32[]{:S(2)}) async-start(bf16[32,8,128,128]{3,2,1,0:T(8,128)(2,1)} %copy.30), calls=%async_computation.3 | async-start | bytes 16777216 | tf_op jit(solution)/shard_map/all_to_all | solution.py:138
  613.3 121.3 %all-to-all-done.3 = bf16[32,8,128,128]{3,2,1,0:T(8,128)(2,1)} async-done(((bf16[32,8,128,128]{3,2,1,0:T(8,128)(2,1)}), bf16[32,8,128,128]{3,2,1,0:T(8,128)(2,1)}, u32[]{:S(2)}, u32[]{:S(2)}) %all-to-all-start.3) | async-done | bytes 8388640 | tf_op jit(solution)/shard_map/all_to_all | solution.py:138
  734.6 5.5 gather_fusion.3
  (280 shorter events, 245.1 us)
Async XLA Ops:
  7.2 64.7 %copy-start = (f32[64,9]{0,1:T(8,128)S(1)}, f32[64,9]{0,1:T(8,128)}, u32[]{:S(2)}) copy-start(f32[64,9]{0,1:T(8,128)} %param.15) | copy-start | bytes 6916
  14.5 28.0 %all-to-all-start.1 = ((bf16[32,2,256]{2,1,0:T(2,128)(2,1)}), bf16[32,2,256]{2,1,0:T(2,128)(2,1)S(1)}, u32[]{:S(2)}, u32[]{:S(2)}) async-start(bf16[32,2,256]{2,1,0:T(2,128)(2,1)} %reshape.477), calls=%async_computation.1 | async-start | bytes 65536 | tf_op jit(solution)/shard_map/all_to_all | solution.py:106
  42.5 14.6 %all-to-all-start = ((bf16[32,2,256]{2,1,0:T(2,128)(2,1)}), bf16[32,2,256]{2,1,0:T(2,128)(2,1)S(1)}, u32[]{:S(2)}, u32[]{:S(2)}) async-start(bf16[32,2,256]{2,1,0:T(2,128)(2,1)} %reshape.479), calls=%async_computation | async-start | bytes 65536 | tf_op jit(solution)/shard_map/all_to_all | solution.py:103
  57.1 131.7 %all-to-all-start.2 = ((bf16[32,8,128,128]{3,2,1,0:T(8,128)(2,1)}), bf16[32,8,128,128]{3,2,1,0:T(8,128)(2,1)}, u32[]{:S(2)}, u32[]{:S(2)}) async-start(bf16[32,8,128,128]{3,2,1,0:T(8,128)(2,1)} %broadcast_select_fusion), calls=%async_computation.2 | async-start | bytes 16777216 | tf_op jit(solution)/shard_map/all_to_all | solution.py:102
  64.6 511.8 %all-reduce.2.cloned.1.call-start = ((), (), s32[]{:S(2)}) async-start(), calls=%async_computation.4 | async-start | bytes 8388608 | tf_op jit(solution)/shard_map/psum | solution.py:124
  192.3 1.7 copy-start.2
  208.1 1.7 copy-start.2
  223.8 1.7 copy-start.2
  239.6 1.7 copy-start.2
  255.4 1.7 copy-start.2
  271.1 1.7 copy-start.2
  286.9 1.7 copy-start.2
  302.6 1.7 copy-start.2
  318.4 1.7 copy-start.2
  334.1 1.7 copy-start.2
  349.9 1.7 copy-start.2
  365.7 1.7 copy-start.2
  381.4 1.7 copy-start.2
  397.2 1.7 copy-start.2
  413.0 1.7 copy-start.2
  428.7 1.7 copy-start.2
  602.7 131.8 %all-to-all-start.3 = ((bf16[32,8,128,128]{3,2,1,0:T(8,128)(2,1)}), bf16[32,8,128,128]{3,2,1,0:T(8,128)(2,1)}, u32[]{:S(2)}, u32[]{:S(2)}) async-start(bf16[32,8,128,128]{3,2,1,0:T(8,128)(2,1)} %copy.30), calls=%async_computation.3 | async-start | bytes 16777216 | tf_op jit(solution)/shard_map/all_to_all | solution.py:138
  610.3 129.8 %copy-start.1 = (f32[64,9]{0,1:T(8,128)S(1)}, f32[64,9]{0,1:T(8,128)}, u32[]{:S(2)}) copy-start(f32[64,9]{0,1:T(8,128)} %param.15) | copy-start | bytes 6916
Sparse Core Ops, SparseCore 0:
  484.1 92.2 all-reduce.1
where the time goes:
time: 755 us; the launch traced here: 747 us
  waiting for transfers between devices  319 us (42%)
  local copies, waits for them, and re-layouts  166 us (22%)
  matrix products  115 us (15%)
  other arithmetic  89.4 us (12%)
  starting transfers between devices  31.1 us (4%)
  between operations  14.4 us (2%)
  blocking collectives  10.7 us (1%)
    all_to_all x1, waiting for transfers between devices, shards(): lax.all_to_all(difference_slots.reshape(patches, capacity, side_len, side...  121 us
    all_to_all x1, waiting for transfers between devices, shards(): lax.all_to_all(pack_slots(masked), 'patch', split_axis=0, concat_axis=0,...  116 us
    psum x1, waiting for transfers between devices, shards(): numerator, weight_sum = lax.psum((numerator, weight_sum), 'visit')  81.7 us
    dot_general x16, matrix products, match_group(): jnp.einsum('nisp,npsj->nij', left_bands, columns, preferred_element_type=...  78.8 us
    reshape x16, local copies, waits for them, and re-layouts, match_group(): columns.astype(jnp.bfloat16).reshape(number, side_len, 6, side_len)  74.8 us
    mul x16, other arithmetic, match_group(): coefficients[:, 3 * sigma_pos, None, None] * even_band  32.3 us
    unnamed x11, local copies, waits for them, and re-layouts  26.5 us
    dynamic_slice x16, local copies, waits for them, and re-layouts, match_blocks(): lax.map(one_batch, (blocks.reshape(rounds, batch_blocks, side_len, side_l...  23.8 us
  transfers between devices with their start and end apart: 5, of which 3 were waited for; matrix products, arithmetic and copies ran while one was open for 5% of the time, Pallas kernels for 0%

commit v1 on v0

v1 whole, which is shorter than its diff:
```python
import functools

import jax
import jax.numpy as jnp
from jax import lax
from jax.experimental import pallas as pl
from jax.experimental.pallas import tpu as pltpu
from jax.sharding import PartitionSpec as P

CELLS = 64
KSIZE = 21
GROUP = 8


gauss_widths = (1.0, 2.0, 3.5)


def band_tables(side_len):
    tap_reach = KSIZE // 2
    position = jnp.arange(side_len).astype(jnp.float32)
    offset = position[:, None] - position[None, :]
    inside = jnp.abs(offset) <= tap_reach
    tap_offsets = jnp.arange(-tap_reach, tap_reach + 1).astype(jnp.float32)
    tables = []
    for spread in gauss_widths:
        profile_sum = jnp.sum(jnp.exp(-tap_offsets * tap_offsets / (2.0 * spread * spread)))
        even_band = jnp.where(
            inside, jnp.exp(-offset * offset / (2.0 * spread * spread)) / profile_sum, 0.0
        )
        tables.append(even_band)
        tables.append(even_band * offset / spread)
    return jnp.stack(tables)


def match_kernel(coef_ref, pix_ref, mask_ref, tab_ref, right_ref, out_ref):
    step = pl.program_id(0)
    group, side_len, _ = pix_ref.shape
    bits = mask_ref[...]
    masked = jnp.where((bits & 7) == 0, pix_ref[...], jnp.zeros((), jnp.bfloat16))
    columns = jnp.dot(
        masked.reshape(group * side_len, side_len),
        right_ref[...],
        preferred_element_type=jnp.float32,
    ).astype(jnp.bfloat16)
    for g in range(group):
        base = (step * group + g) * 9
        rows = columns[g * side_len:(g + 1) * side_len]
        acc = jnp.zeros((side_len, side_len), jnp.float32)
        for m in range(3):
            even_band = tab_ref[2 * m]
            odd_band = tab_ref[2 * m + 1]
            left_a = (coef_ref[base + 3 * m] * even_band
                      + coef_ref[base + 3 * m + 1] * odd_band).astype(jnp.bfloat16)
            left_b = (coef_ref[base + 3 * m + 2] * even_band).astype(jnp.bfloat16)
            acc = acc + jnp.dot(
                left_a, rows[:, (2 * m) * side_len:(2 * m + 1) * side_len],
                preferred_element_type=jnp.float32,
            )
            acc = acc + jnp.dot(
                left_b, rows[:, (2 * m + 1) * side_len:(2 * m + 2) * side_len],
                preferred_element_type=jnp.float32,
            )
        out_ref[g] = acc.astype(jnp.bfloat16)


def match_blocks(pixels, mask_bits, coefficients, tables, right_bands):
    number, side_len, _ = pixels.shape
    steps = number // GROUP
    flops = number * 4 * side_len * side_len * 6 * side_len
    return pl.pallas_call(
        match_kernel,
        out_shape=jax.ShapeDtypeStruct(pixels.shape, jnp.bfloat16),
        grid=(steps,),
        in_specs=[
            pl.BlockSpec(memory_space=pltpu.SMEM),
            pl.BlockSpec((GROUP, side_len, side_len), lambda i: (i, 0, 0)),
            pl.BlockSpec((GROUP, side_len, side_len), lambda i: (i, 0, 0)),
            pl.BlockSpec(tables.shape, lambda i: (0, 0, 0)),
            pl.BlockSpec(right_bands.shape, lambda i: (0, 0)),
        ],
        out_specs=pl.BlockSpec((GROUP, side_len, side_len), lambda i: (i, 0, 0)),
        cost_estimate=pl.CostEstimate(
            flops=flops, transcendentals=0, bytes_accessed=number * side_len * side_len * 8
        ),
    )(coefficients.reshape(-1), pixels, mask_bits, tables, right_bands)


def shards(pixels, mask_bits, inv_var, owner, cell, coef_index, coef_table):
    blocks_here = pixels.shape[0]
    side_len = pixels.shape[1]
    patches = lax.axis_size("patch")
    visits = lax.axis_size("visit")
    capacity = 4 * blocks_here // patches
    slot_total = patches * capacity
    tables = band_tables(side_len)
    right_bands = (
        jnp.transpose(tables, (2, 0, 1)).reshape(side_len, 6 * side_len).astype(jnp.bfloat16)
    )
    coefficients = coef_table[coef_index]
    matched_home = match_blocks(pixels, mask_bits, coefficients, tables, right_bands)
    weight = inv_var.astype(jnp.bfloat16)
    cell_weight = jnp.where(
        cell[:, None] == jnp.arange(CELLS)[None, :], weight[:, None], jnp.zeros((), jnp.bfloat16)
    )
    dest_onehot = (owner[:, None] == jnp.arange(patches)[None, :]).astype(jnp.int32)
    slot_rank = jnp.sum((jnp.cumsum(dest_onehot, axis=0) - dest_onehot) * dest_onehot, axis=1)
    slot_of_block = owner * capacity + slot_rank
    matches = slot_of_block[None, :] == jnp.arange(slot_total)[:, None]
    source_row = jnp.sum(jnp.where(matches, jnp.arange(blocks_here)[None, :], 0), axis=1)
    filled = jnp.any(matches, axis=1)

    def pack_slots(values):
        picked = values[source_row]
        keep_rows = filled.reshape((slot_total,) + (1,) * (values.ndim - 1))
        picked = jnp.where(keep_rows, picked, jnp.zeros((), values.dtype))
        return picked.reshape((patches, capacity) + values.shape[1:])

    pieces = lax.all_to_all(
        pack_slots(matched_home), "patch", split_axis=0, concat_axis=0, tiled=True
    )
    weights = lax.all_to_all(
        pack_slots(cell_weight), "patch", split_axis=0, concat_axis=0, tiled=True
    )
    flat_weights = weights.reshape(slot_total, CELLS)
    flat_matched = pieces.reshape(slot_total, side_len * side_len)
    numerator = jnp.einsum(
        "sc,sk->ck", flat_weights, flat_matched, preferred_element_type=jnp.float32
    ).reshape(CELLS, side_len, side_len)
    weight_sum = jnp.sum(flat_weights.astype(jnp.float32), axis=0)
    numerator_part = lax.psum_scatter(numerator, "visit", scatter_dimension=1, tiled=True)
    weight_sum = lax.psum(weight_sum, "visit")
    coadd_part = numerator_part / jnp.maximum(weight_sum, 1.0)[:, None, None]
    template = lax.all_gather(coadd_part.astype(jnp.bfloat16), "visit", axis=1, tiled=True)
    live_slots = (flat_weights > 0).astype(jnp.bfloat16)
    slot_template = jnp.einsum(
        "sc,ck->sk",
        live_slots,
        template.reshape(CELLS, side_len * side_len),
        preferred_element_type=jnp.float32,
    )
    difference_slots = (flat_matched.astype(jnp.float32) - slot_template).astype(jnp.bfloat16)
    returned = lax.all_to_all(
        difference_slots.reshape(patches, capacity, side_len, side_len),
        "patch",
        split_axis=0,
        concat_axis=0,
        tiled=True,
    )
    difference = returned.reshape(slot_total, side_len, side_len)[slot_of_block]
    return (coadd_part, difference)


def solution(mesh):
    placed = (
        P(("visit", "patch"), None, None),
        P(("visit", "patch"), None, None),
        P(("visit", "patch")),
        P(("visit", "patch")),
        P(("visit", "patch")),
        P(("visit", "patch")),
        P(),
    )
    return jax.shard_map(
        shards,
        mesh=mesh,
        in_specs=placed,
        out_specs=(P("patch", "visit", None), P(("visit", "patch"), None, None)),
        check_vma=False,
    )
```

time: 755 us -> 481 us (0.64)
  local copies, waits for them, and re-layouts: 166 us -> 65.9 us
  matrix products: 115 us -> 20.7 us
  other arithmetic: 89.4 us -> 20.8 us
  Pallas kernels: 0 us -> 10.8 us
  starting transfers between devices: 31.1 us -> 23.5 us
    dot_general x33 -> x0, matrix products: 94.8 us -> none  [the longest x16 78.8 us: match_group(): jnp.einsum('nisp,npsj->nij', left_bands, columns, preferred_element_type=...]
    psum x1 -> x0, waiting for transfers between devices: 81.7 us -> none  [shards(): numerator, weight_sum = lax.psum((numerator, weight_sum), 'visit')]
    reshape x16 -> x1, local copies, waits for them, and re-layouts: 74.8 us -> 0.72 us  [match_blocks(): coefficients.reshape(-1)]
    reduce_scatter x0 -> x1, waiting for transfers between devices: none -> 35.6 us  [shards(): lax.psum_scatter(numerator, 'visit', scatter_dimension=1, tiled=True)]
    mul x16 -> x0, other arithmetic: 32.3 us -> none  [match_group(): coefficients[:, 3 * sigma_pos, None, None] * even_band]
    all_gather x0 -> x1, waiting for transfers between devices: none -> 30.7 us  [shards(): lax.all_gather(coadd_part.astype(jnp.bfloat16), 'visit', axis=1, tiled=True)]
    dynamic_slice x17 -> x0, local copies, waits for them, and re-layouts: 25.1 us -> none  [the longest x16 23.8 us: match_blocks(): lax.map(one_batch, (blocks.reshape(rounds, batch_blocks, side_len, side_l...]
    while x80 -> x0, other arithmetic: 19.4 us -> none
  transfers between devices with their start and end apart: 5 -> 5, of which waited for: 3 -> 4; matrix products, arithmetic and copies ran while one was open for 5% -> 6% of each run, Pallas kernels for 0% -> 2%
where the time goes in v1:
time: 481 us; the launch traced here: 479 us
  waiting for transfers between devices  313 us (65%)
  local copies, waits for them, and re-layouts  65.9 us (14%)
  starting transfers between devices  23.5 us (5%)
  other arithmetic  20.8 us (4%)
  matrix products  20.7 us (4%)
  between operations  14.2 us (3%)
  Pallas kernels  10.8 us (2%)
  blocking collectives  10.7 us (2%)
    all_to_all x1, waiting for transfers between devices, shards(): lax.all_to_all(pack_slots(matched_home), 'patch', split_axis=0, concat_ax...  124 us
    all_to_all x1, waiting for transfers between devices, shards(): lax.all_to_all(difference_slots.reshape(patches, capacity, side_len, side...  123 us
    reduce_scatter x1, waiting for transfers between devices, shards(): lax.psum_scatter(numerator, 'visit', scatter_dimension=1, tiled=True)  35.6 us
    all_gather x1, waiting for transfers between devices, shards(): lax.all_gather(coadd_part.astype(jnp.bfloat16), 'visit', axis=1, tiled=True)  30.7 us
    unnamed x7, local copies, waits for them, and re-layouts  26.4 us
    dot_general x1, matrix products, shards(): jnp.einsum('sc,ck->sk', live_slots, template.reshape(CELLS, side_len * si...  12.7 us
    dot_general x1, local copies, waits for them, and re-layouts, shards(): jnp.einsum('sc,sk->ck', flat_weights, flat_matched, preferred_element_typ...  11.9 us
    pallas_call x1, Pallas kernels, match_blocks(): pl.pallas_call(match_kernel, out_shape=jax.ShapeDtypeStruct(pixels.shape,...  10.8 us
  transfers between devices with their start and end apart: 5, of which 4 were waited for; matrix products, arithmetic and copies ran while one was open for 6% of the time, Pallas kernels for 2%

profile of v1, /device:TPU:32, one launch (start us, length us, event | category | flops | bytes accessed | tf_op | source)
XLA Modules:
  0.0 479.5 jit_solution(14961207492031495308)
XLA Ops:
  8.0 0.8 select_reduce_fusion.1
  11.9 0.9 gather_fusion
  13.5 8.2 %all-to-all-start = ((bf16[32,2,256]{2,1,0:T(2,128)(2,1)}), bf16[32,2,256]{2,1,0:T(2,128)(2,1)S(1)}, u32[]{:S(2)}, u32[]{:S(2)}) async-start(bf16[32,2,256]{2,1,0:T(2,128)(2,1)} %reshape.415), calls=%async_computation | async-start | bytes 65536 | tf_op jit(solution)/shard_map/all_to_all | solution.py:121
  27.5 0.8 fusion.23.tab_ref
  28.3 0.8 copy.29.right_ref
  29.1 0.8 copy.28
  31.2 10.8 %shard_map.86 = bf16[64,128,128]{2,1,0:T(8,128)(2,1)} custom-call(f32[576]{0:T(1024)} %reshape.375.coef_ref, bf16[64,128,128]{2,1,0:T(8,128)(2,1)} %pix_ref.1, s32[64,128,128]{2,1,0:T(8,128)} %mask_ref.1, f32[6,128,128]{2,1,0:T(8,128)} %copy-done, bf16[128,768]{1,0:T(8,128)(2,1)} %copy.29.right_ref), custom_call_target="tpu_custom_call" | custom-call | flops 3221225472 | bytes 8388608 | tf_op jit(solution)/shard_map/pallas_call | solution.py:70
  42.0 9.9 %gather_fusion.2 = bf16[256,128,128]{2,1,0:T(8,128)(2,1)} fusion(bf16[64,128,128]{2,1,0:T(8,128)(2,1)} %shard_map.86, s32[1024]{0:T(1024)S(1)} %get-tuple-element.15), kind=kCustom, calls=%fused_computation.2 | custom fusion | bytes 16778240 | tf_op jit(solution)/shard_map/gather | solution.py:113
  52.0 7.2 %broadcast_select_fusion = bf16[32,8,128,128]{3,2,1,0:T(8,128)(2,1)} fusion(bf16[32,8,128,128]{3,2,1,0:T(8,128)(2,1)} %bitcast.39, pred[32,8]{1,0:T(8,128)(4,1)S(1)} %broadcast_in_dim.75), kind=kLoop, calls=%fused_computation.7 | loop fusion | flops 4194304 | bytes 16777472 | tf_op jit(solution)/shard_map/jit(_where)/select_n | solution.py:115
  59.2 7.5 %all-to-all-start.1 = ((bf16[32,8,128,128]{3,2,1,0:T(8,128)(2,1)}), bf16[32,8,128,128]{3,2,1,0:T(8,128)(2,1)}, u32[]{:S(2)}, u32[]{:S(2)}) async-start(bf16[32,8,128,128]{3,2,1,0:T(8,128)(2,1)} %broadcast_select_fusion), calls=%async_computation.1 | async-start | bytes 16777216 | tf_op jit(solution)/shard_map/all_to_all | solution.py:118
  67.0 123.9 %all-to-all-done.1 = bf16[32,8,128,128]{3,2,1,0:T(8,128)(2,1)} async-done(((bf16[32,8,128,128]{3,2,1,0:T(8,128)(2,1)}), bf16[32,8,128,128]{3,2,1,0:T(8,128)(2,1)}, u32[]{:S(2)}, u32[]{:S(2)}) %all-to-all-start.1) | async-done | bytes 8388640 | tf_op jit(solution)/shard_map/all_to_all | solution.py:118
  190.9 23.2 %copy.47 = bf16[32,8,128,128]{3,1,2,0:T(8,128)(2,1)} copy(bf16[32,8,128,128]{3,2,1,0:T(8,128)(2,1)} %all-to-all-done.1) | data formatting | bytes 16777216
  214.1 11.9 %copy.30 = bf16[16384,256]{1,0:T(8,128)(2,1)} copy(bf16[16384,256]{0,1:T(8,128)(2,1)} %bitcast.41) | data formatting | bytes 16777216 | tf_op jit(solution)/shard_map/sc,sk->ck/dot_general | solution.py:126
  226.0 8.0 %fusion.24 = f32[64,128,128]{2,0,1:T(8,128)} fusion(bf16[128,128,256]{2,1,0:T(8,128)(2,1)} %bitcast.40, bf16[32,8,64]{2,1,0:T(8,128)(2,1)S(1)} %reshape.416), kind=kOutput, calls=%fused_computation.39 | convolution fusion | flops 536870912 | bytes 12615680 | tf_op jit(solution)/shard_map/sc,sk->ck/dot_general | solution.py:126
  234.1 10.7 %psum.7 = f32[64]{0:T(128)S(1)} all-reduce(f32[64]{0:T(128)S(1)} %convert_reduce_fusion), channel_id=1, replica_groups=mesh['visit'=4,'patch'=32] {'visit'}, use_global_device_ids=true, to_apply=%region_9.10 | all-reduce | flops 64 | bytes 512 | tf_op jit(solution)/shard_map/psum | solution.py:131
  244.8 35.6 %reduce-scatter.2.cloned.1.call-done = f32[64,32,128]{2,0,1:T(8,128)} async-done(((f32[64,128,128]{2,0,1:T(8,128)}), f32[64,32,128]{2,0,1:T(8,128)}) %reduce-scatter.2.cloned.1.call-update) | async-done | bytes 1048592 | tf_op jit(solution)/shard_map/reduce_scatter | solution.py:130
  280.4 2.3 fusion.34
  282.7 30.7 %all-gather.2.cloned.1.call-done = bf16[64,128,128]{2,0,1:T(8,128)(2,1)} async-done(((bf16[64,32,128]{2,0,1:T(8,128)(2,1)}), bf16[64,128,128]{2,0,1:T(8,128)(2,1)}) %all-gather.2.cloned.1.call-update) | async-done | bytes 2097168 | tf_op jit(solution)/shard_map/all_gather | solution.py:133
  313.4 12.7 %fusion.1 = bf16[32,8,128,128]{3,1,2,0:T(8,128)(2,1)} fusion(bf16[32,8,128,128]{3,2,1,0:T(8,128)(2,1)} %all-to-all-done.1, bf16[32,8,64]{2,1,0:T(8,128)(2,1)S(1)} %reshape.416, bf16[64,128,128]{2,0,1:T(8,128)(2,1)} %all-gather.2.cloned.1.call-done), kind=kOutput, calls=%fused_computation.8 | convolution fusion | flops 549470208 | bytes 18907136 | tf_op jit(solution)/shard_map/sc,ck->sk/dot_general | solution.py:135
  326.1 9.2 %copy.33 = bf16[32,8,128,128]{3,2,1,0:T(8,128)(2,1)} copy(bf16[32,8,128,128]{3,1,2,0:T(8,128)(2,1)} %fusion.1) | data formatting | bytes 16777216 | tf_op jit(solution)/shard_map/reshape | solution.py:143
  335.3 7.5 %all-to-all-start.2 = ((bf16[32,8,128,128]{3,2,1,0:T(8,128)(2,1)}), bf16[32,8,128,128]{3,2,1,0:T(8,128)(2,1)}, u32[]{:S(2)}, u32[]{:S(2)}) async-start(bf16[32,8,128,128]{3,2,1,0:T(8,128)(2,1)} %copy.33), calls=%async_computation.3 | async-start | bytes 16777216 | tf_op jit(solution)/shard_map/all_to_all | solution.py:142
  342.9 1.6 copy.34
  344.5 122.7 %all-to-all-done.2 = bf16[32,8,128,128]{3,2,1,0:T(8,128)(2,1)} async-done(((bf16[32,8,128,128]{3,2,1,0:T(8,128)(2,1)}), bf16[32,8,128,128]{3,2,1,0:T(8,128)(2,1)}, u32[]{:S(2)}, u32[]{:S(2)}) %all-to-all-start.2) | async-done | bytes 8388640 | tf_op jit(solution)/shard_map/all_to_all | solution.py:142
  467.1 5.5 %gather_fusion.3 = bf16[64,128,128]{2,1,0:T(8,128)(2,1)} fusion(bf16[256,128,128]{2,1,0:T(8,128)(2,1)} %bitcast.12, s32[1024]{0:T(1024)S(1)} %pad_clamp_fusion), kind=kCustom, calls=%fused_computation.3 | custom fusion | bytes 4194560 | tf_op jit(solution)/shard_map/gather | solution.py:149
  (36 shorter events, 12.2 us)
Async XLA Ops:
  13.5 45.7 %all-to-all-start = ((bf16[32,2,256]{2,1,0:T(2,128)(2,1)}), bf16[32,2,256]{2,1,0:T(2,128)(2,1)S(1)}, u32[]{:S(2)}, u32[]{:S(2)}) async-start(bf16[32,2,256]{2,1,0:T(2,128)(2,1)} %reshape.415), calls=%async_computation | async-start | bytes 65536 | tf_op jit(solution)/shard_map/all_to_all | solution.py:121
  28.3 3.0 copy-start
  59.2 131.7 %all-to-all-start.1 = ((bf16[32,8,128,128]{3,2,1,0:T(8,128)(2,1)}), bf16[32,8,128,128]{3,2,1,0:T(8,128)(2,1)}, u32[]{:S(2)}, u32[]{:S(2)}) async-start(bf16[32,8,128,128]{3,2,1,0:T(8,128)(2,1)} %broadcast_select_fusion), calls=%async_computation.1 | async-start | bytes 16777216 | tf_op jit(solution)/shard_map/all_to_all | solution.py:118
  66.7 213.7 %reduce-scatter.2.cloned.1.call-start = ((), (), s32[]{:S(2)}) async-start(), calls=%async_computation.4 | async-start | bytes 5242880 | tf_op jit(solution)/shard_map/reduce_scatter | solution.py:130
  234.0 79.5 %all-gather.2.cloned.1.call-start = ((), (), s32[]{:S(2)}) async-start(), calls=%async_computation.5 | async-start | bytes 2621440 | tf_op jit(solution)/shard_map/all_gather | solution.py:133
  335.3 131.8 %all-to-all-start.2 = ((bf16[32,8,128,128]{3,2,1,0:T(8,128)(2,1)}), bf16[32,8,128,128]{3,2,1,0:T(8,128)(2,1)}, u32[]{:S(2)}, u32[]{:S(2)}) async-start(bf16[32,8,128,128]{3,2,1,0:T(8,128)(2,1)} %copy.33), calls=%async_computation.3 | async-start | bytes 16777216 | tf_op jit(solution)/shard_map/all_to_all | solution.py:142
Sparse Core Ops, SparseCore 0:
  234.1 46.2 reduce-scatter.1
  282.8 30.5 all-gather.1

commit v2 on v1

--- a/solution.py
+++ b/solution.py
@@ -90,63 +90,40 @@
     side_len = pixels.shape[1]
     patches = lax.axis_size("patch")
     visits = lax.axis_size("visit")
-    capacity = 4 * blocks_here // patches
-    slot_total = patches * capacity
+    devices = patches * visits
+    segments = patches * CELLS
+    rows_here = side_len // visits
+    both = ("visit", "patch")
     tables = band_tables(side_len)
     right_bands = (
         jnp.transpose(tables, (2, 0, 1)).reshape(side_len, 6 * side_len).astype(jnp.bfloat16)
     )
     coefficients = coef_table[coef_index]
     matched_home = match_blocks(pixels, mask_bits, coefficients, tables, right_bands)
-    weight = inv_var.astype(jnp.bfloat16)
-    cell_weight = jnp.where(
-        cell[:, None] == jnp.arange(CELLS)[None, :], weight[:, None], jnp.zeros((), jnp.bfloat16)
+    by_row = jnp.transpose(matched_home, (1, 0, 2))
+    row_all = lax.all_to_all(by_row, both, split_axis=0, concat_axis=0, tiled=True)
+    row_all = row_all.reshape(devices * blocks_here, side_len)
+    weight_all = lax.all_gather(inv_var.astype(jnp.bfloat16), both, tiled=True)
+    segment_all = lax.all_gather((owner * CELLS + cell).astype(jnp.int32), both, tiled=True)
+    picks = segment_all[None, :] == jnp.arange(segments, dtype=jnp.int32)[:, None]
+    weighted = jnp.where(picks, weight_all[None, :], jnp.zeros((), jnp.bfloat16))
+    numerator = jnp.dot(weighted, row_all, preferred_element_type=jnp.float32)
+    weight_sum = jnp.sum(weighted.astype(jnp.float32), axis=1)
+    coadd_row = numerator / jnp.maximum(weight_sum, 1.0)[:, None]
+    template_row = coadd_row.astype(jnp.bfloat16)
+    difference_row = (
+        row_all.astype(jnp.float32) - template_row[segment_all].astype(jnp.float32)
+    ).astype(jnp.bfloat16)
+    returned = lax.all_to_all(
+        difference_row.reshape(devices, blocks_here, side_len),
+        both, split_axis=0, concat_axis=0, tiled=True,
     )
-    dest_onehot = (owner[:, None] == jnp.arange(patches)[None, :]).astype(jnp.int32)
-    slot_rank = jnp.sum((jnp.cumsum(dest_onehot, axis=0) - dest_onehot) * dest_onehot, axis=1)
-    slot_of_block = owner * capacity + slot_rank
-    matches = slot_of_block[None, :] == jnp.arange(slot_total)[:, None]
-    source_row = jnp.sum(jnp.where(matches, jnp.arange(blocks_here)[None, :], 0), axis=1)
-    filled = jnp.any(matches, axis=1)
-
-    def pack_slots(values):
-        picked = values[source_row]
-        keep_rows = filled.reshape((slot_total,) + (1,) * (values.ndim - 1))
-        picked = jnp.where(keep_rows, picked, jnp.zeros((), values.dtype))
-        return picked.reshape((patches, capacity) + values.shape[1:])
-
-    pieces = lax.all_to_all(
-        pack_slots(matched_home), "patch", split_axis=0, concat_axis=0, tiled=True
+    difference = jnp.transpose(returned, (1, 0, 2))
+    coadd_parts = lax.all_to_all(
+        coadd_row.reshape(patches, CELLS, 1, side_len),
+        "patch", split_axis=0, concat_axis=2, tiled=True,
     )
-    weights = lax.all_to_all(
-        pack_slots(cell_weight), "patch", split_axis=0, concat_axis=0, tiled=True
-    )
-    flat_weights = weights.reshape(slot_total, CELLS)
-    flat_matched = pieces.reshape(slot_total, side_len * side_len)
-    numerator = jnp.einsum(
-        "sc,sk->ck", flat_weights, flat_matched, preferred_element_type=jnp.float32
-    ).reshape(CELLS, side_len, side_len)
-    weight_sum = jnp.sum(flat_weights.astype(jnp.float32), axis=0)
-    numerator_part = lax.psum_scatter(numerator, "visit", scatter_dimension=1, tiled=True)
-    weight_sum = lax.psum(weight_sum, "visit")
-    coadd_part = numerator_part / jnp.maximum(weight_sum, 1.0)[:, None, None]
-    template = lax.all_gather(coadd_part.astype(jnp.bfloat16), "visit", axis=1, tiled=True)
-    live_slots = (flat_weights > 0).astype(jnp.bfloat16)
-    slot_template = jnp.einsum(
-        "sc,ck->sk",
-        live_slots,
-        template.reshape(CELLS, side_len * side_len),
-        preferred_element_type=jnp.float32,
-    )
-    difference_slots = (flat_matched.astype(jnp.float32) - slot_template).astype(jnp.bfloat16)
-    returned = lax.all_to_all(
-        difference_slots.reshape(patches, capacity, side_len, side_len),
-        "patch",
-        split_axis=0,
-        concat_axis=0,
-        tiled=True,
-    )
-    difference = returned.reshape(slot_total, side_len, side_len)[slot_of_block]
+    coadd_part = coadd_parts.reshape(CELLS, rows_here, side_len)
     return (coadd_part, difference)
 
 

time: 481 us -> 278 us (0.58)
  waiting for transfers between devices: 313 us -> 27 us
  blocking collectives: 10.7 us -> 144 us
  local copies, waits for them, and re-layouts: 65.9 us -> 37 us
  between operations: 14.2 us -> 0.83 us
  matrix products: 20.7 us -> 10.1 us
    all_to_all x3, waiting for transfers between devices: 247 us -> 27 us  [the longest x1 27 us: shards(): lax.all_to_all(difference_row.reshape(devices, blocks_here, side_len), bo...]
    unnamed x0 -> x2, blocking collectives: none -> 144 us
    reduce_scatter x1 -> x0, waiting for transfers between devices: 35.6 us -> none  [shards(): lax.psum_scatter(numerator, 'visit', scatter_dimension=1, tiled=True)]
    all_gather x1 -> x0, waiting for transfers between devices: 30.7 us -> none  [shards(): lax.all_gather(coadd_part.astype(jnp.bfloat16), 'visit', axis=1, tiled=True)]
    unnamed x7 -> x16, local copies, waits for them, and re-layouts: 26.4 us -> 6.54 us
    dot_general x1 -> x0, local copies, waits for them, and re-layouts: 11.9 us -> none  [shards(): jnp.einsum('sc,sk->ck', flat_weights, flat_matched, preferred_element_typ...]
    psum x1 -> x0, blocking collectives: 10.7 us -> none  [shards(): weight_sum = lax.psum(weight_sum, 'visit')]
    dot_general x2 -> x1, matrix products: 20.7 us -> 10.1 us  [shards(): numerator = jnp.dot(weighted, row_all, preferred_element_type=jnp.float32)]
  transfers between devices with their start and end apart: 5 -> 3, of which waited for: 4 -> 1; matrix products, arithmetic and copies ran while one was open for 6% -> 14% of each run, Pallas kernels for 2% -> 0%
where the time goes in v2:
time: 278 us; the launch traced here: 275 us
  blocking collectives  144 us (52%)
  local copies, waits for them, and re-layouts  37 us (13%)
  waiting for transfers between devices  27 us (10%)
  starting transfers between devices  25.6 us (9%)
  other arithmetic  19.5 us (7%)
  Pallas kernels  10.8 us (4%)
  matrix products  10.1 us (4%)
    unnamed x2, blocking collectives  144 us
    all_to_all x1, waiting for transfers between devices, shards(): lax.all_to_all(difference_row.reshape(devices, blocks_here, side_len), bo...  27 us
    gather x1, local copies, waits for them, and re-layouts, shards(): template_row[segment_all].astype(jnp.float32)  24 us
    pallas_call x1, Pallas kernels, match_blocks(): pl.pallas_call(match_kernel, out_shape=jax.ShapeDtypeStruct(pixels.shape,...  10.8 us
    all_to_all x1, starting transfers between devices, shards(): lax.all_to_all(by_row, both, split_axis=0, concat_axis=0, tiled=True)  10.2 us
    dot_general x1, matrix products, shards(): numerator = jnp.dot(weighted, row_all, preferred_element_type=jnp.float32)  10.1 us
    all_to_all x1, starting transfers between devices, shards(): lax.all_to_all(difference_row.reshape(devices, blocks_here, side_len), bo...  9.07 us
    reduce_sum x1, other arithmetic, shards(): weight_sum = jnp.sum(weighted.astype(jnp.float32), axis=1)  8.35 us
  transfers between devices with their start and end apart: 3, of which 1 were waited for; matrix products, arithmetic and copies ran while one was open for 14% of the time, Pallas kernels for 0%

profile of v2, /device:TPU:32, one launch (start us, length us, event | category | flops | bytes accessed | tf_op | source)
XLA Modules:
  0.0 275.1 jit_solution(3187513888200616000)
XLA Ops:
  1.9 0.7 exponential_reduce_fusion
  3.2 0.8 copy.23
  4.6 0.7 reshape.342.coef_ref
  5.3 0.7 fusion.31
  6.1 0.7 fusion.23
  6.8 0.7 fusion.30
  7.6 0.7 fusion.25
  8.3 0.8 fusion.29
  9.1 0.8 fusion.27.tab_ref
  10.0 0.8 copy.24.right_ref
  10.8 10.8 %shard_map.86 = bf16[64,128,128]{2,1,0:T(8,128)(2,1)} custom-call(f32[576]{0:T(1024)} %reshape.342.coef_ref, bf16[64,128,128]{2,1,0:T(8,128)(2,1)} %pix_ref.1, s32[64,128,128]{2,1,0:T(8,128)} %mask_ref.1, f32[6,128,128]{2,1,0:T(8,128)} %copy-done.1, bf16[128,768]{1,0:T(8,128)(2,1)} %copy.24.right_ref), custom_call_target="tpu_custom_call" | custom-call | flops 3221225472 | bytes 8388608 | tf_op jit(solution)/shard_map/pallas_call | solution.py:70
  21.6 4.3 %copy.25 = bf16[128,64,128]{2,1,0:T(8,128)(2,1)} copy(bf16[128,64,128]{2,0,1:T(8,128)(2,1)} %bitcast.20) | data formatting | bytes 4194304 | tf_op jit(solution)/shard_map/transpose | solution.py:103
  25.9 10.2 %all-to-all-start = ((bf16[128,64,128]{2,1,0:T(8,128)(2,1)}), bf16[128,64,128]{2,1,0:T(8,128)(2,1)S(1)}, u32[]{:S(2)}, u32[]{:S(2)}) async-start(bf16[128,64,128]{2,1,0:T(8,128)(2,1)} %copy.25), calls=%async_computation | async-start | bytes 4194304 | tf_op jit(solution)/shard_map/all_to_all | solution.py:104
  36.4 81.4 %all-reduce.1 = bf16[8192]{0:T(1024)(128)(2,1)S(1)} all-reduce(bf16[8192]{0:T(1024)(128)(2,1)S(1)} %dynamic-update-slice.1), channel_id=1, replica_groups=mesh['visit'=4,'patch'=32] {'visit','patch'}, use_global_device_ids=true, to_apply=%add.1 | all-reduce | flops 8192 | bytes 32768
  118.0 62.9 %all-reduce = s32[8192]{0:T(1024)S(1)} all-reduce(s32[8192]{0:T(1024)S(1)} %add_dynamic-update-slice_fusion), channel_id=1, replica_groups=mesh['visit'=4,'patch'=32] {'visit','patch'}, use_global_device_ids=true, to_apply=%add | all-reduce | flops 8192 | bytes 65536
  180.9 8.4 %convert_reduce_fusion = f32[2048]{0:T(1024)S(1)} fusion(s32[8192]{0:T(1024)S(1)} %all-reduce, bf16[8192]{0:T(1024)(128)(2,1)S(1)} %all-reduce.1), kind=kLoop, calls=%fused_computation.2 | loop fusion | flops 67106816 | bytes 57344 | tf_op jit(solution)/shard_map/reduce_sum | solution.py:111
  189.3 10.1 %fusion.33 = (bf16[2048,128]{1,0:T(8,128)(2,1)S(1)}, f32[2048,128]{1,0:T(8,128)}) fusion(f32[2048]{0:T(1024)S(1)} %broadcast_maximum_fusion, bf16[8192,128]{1,0:T(8,128)(2,1)S(1)} %bitcast.18, s32[8192]{0:T(1024)S(1)} %all-reduce, bf16[8192]{0:T(1024)(128)(2,1)S(1)} %all-reduce.1), kind=kOutput, calls=%fused_computation.51 | convolution fusion | flops 4329046016 | bytes 3727360 | tf_op jit(solution)/shard_map/dot_general | solution.py:110
  199.4 6.3 %all-to-all-start.1 = ((f32[32,64,1,128]{3,1,2,0:T(8,128)}), f32[32,64,1,128]{3,1,2,0:T(8,128)}, u32[]{:S(2)}, u32[]{:S(2)}) async-start(f32[32,64,1,128]{3,1,2,0:T(8,128)} %bitcast.21), calls=%async_computation.1 | async-start | bytes 2097152 | tf_op jit(solution)/shard_map/all_to_all | solution.py:122
  205.7 24.0 %gather_fusion.1 = bf16[8192,128]{1,0:T(8,128)(2,1)S(1)} fusion(bf16[2048,128]{1,0:T(8,128)(2,1)S(1)} %get-tuple-element.6, s32[8192]{0:T(1024)S(1)} %fusion.28), kind=kCustom, calls=%fused_computation.1 | custom fusion | bytes 4227072 | tf_op jit(solution)/shard_map/gather | solution.py:115
  229.7 3.9 %fusion.6 = bf16[128,64,128]{2,1,0:T(8,128)(2,1)} fusion(bf16[128,64,128]{2,1,0:T(8,128)(2,1)S(1)} %bitcast.17, bf16[128,64,128]{2,1,0:T(8,128)(2,1)} %copy-done), kind=kLoop, calls=%fused_computation.10 | loop fusion | flops 4194304 | bytes 6291456 | tf_op jit(solution)/shard_map/convert_element_type | solution.py:116
  233.6 9.1 %all-to-all-start.2 = ((bf16[128,64,128]{2,1,0:T(8,128)(2,1)}), bf16[128,64,128]{2,1,0:T(8,128)(2,1)S(1)}, u32[]{:S(2)}, u32[]{:S(2)}) async-start(bf16[128,64,128]{2,1,0:T(8,128)(2,1)} %fusion.6), calls=%async_computation.2 | async-start | bytes 4194304 | tf_op jit(solution)/shard_map/all_to_all | solution.py:117
  242.7 2.8 %copy.27 = f32[64,32,128]{2,1,0:T(8,128)} copy(f32[64,32,128]{2,0,1:T(8,128)} %bitcast.8) | data formatting | bytes 2097152
  245.5 27.0 %all-to-all-done.2 = bf16[128,64,128]{2,1,0:T(8,128)(2,1)S(1)} async-done(((bf16[128,64,128]{2,1,0:T(8,128)(2,1)}), bf16[128,64,128]{2,1,0:T(8,128)(2,1)S(1)}, u32[]{:S(2)}, u32[]{:S(2)}) %all-to-all-start.2) | async-done | bytes 2097184 | tf_op jit(solution)/shard_map/all_to_all | solution.py:117
  272.4 2.7 copy.28
  (26 shorter events, 3.0 us)
Async XLA Ops:
  9.9 0.9 copy-start.1
  21.6 14.6 %copy-start.4 = (f32[64]{0:T(128)S(1)}, f32[64]{0:T(128)}, u32[]{:S(2)}) copy-start(f32[64]{0:T(128)} %param.9) | copy-start | bytes 772
  21.6 96.3 %copy-start.2 = (s32[64]{0:T(128)S(1)}, s32[64]{0:T(128)}, u32[]{:S(2)}) copy-start(s32[64]{0:T(128)} %param.11) | copy-start | bytes 772
  21.6 96.3 %copy-start.3 = (s32[64]{0:T(128)S(1)}, s32[64]{0:T(128)}, u32[]{:S(2)}) copy-start(s32[64]{0:T(128)} %param.10) | copy-start | bytes 772
  25.9 163.4 %all-to-all-start = ((bf16[128,64,128]{2,1,0:T(8,128)(2,1)}), bf16[128,64,128]{2,1,0:T(8,128)(2,1)S(1)}, u32[]{:S(2)}, u32[]{:S(2)}) async-start(bf16[128,64,128]{2,1,0:T(8,128)(2,1)} %copy.25), calls=%async_computation | async-start | bytes 4194304 | tf_op jit(solution)/shard_map/all_to_all | solution.py:104
  189.3 10.1 %copy-start = (bf16[128,64,128]{2,1,0:T(8,128)(2,1)}, bf16[128,64,128]{2,1,0:T(8,128)(2,1)S(1)}, u32[]{:S(2)}) copy-start(bf16[128,64,128]{2,1,0:T(8,128)(2,1)S(1)} %all-to-all-done) | copy-start | bytes 6291460
  199.4 34.2 %all-to-all-start.1 = ((f32[32,64,1,128]{3,1,2,0:T(8,128)}), f32[32,64,1,128]{3,1,2,0:T(8,128)}, u32[]{:S(2)}, u32[]{:S(2)}) async-start(f32[32,64,1,128]{3,1,2,0:T(8,128)} %bitcast.21), calls=%async_computation.1 | async-start | bytes 2097152 | tf_op jit(solution)/shard_map/all_to_all | solution.py:122
  233.6 38.9 %all-to-all-start.2 = ((bf16[128,64,128]{2,1,0:T(8,128)(2,1)}), bf16[128,64,128]{2,1,0:T(8,128)(2,1)S(1)}, u32[]{:S(2)}, u32[]{:S(2)}) async-start(bf16[128,64,128]{2,1,0:T(8,128)(2,1)} %fusion.6), calls=%async_computation.2 | async-start | bytes 4194304 | tf_op jit(solution)/shard_map/all_to_all | solution.py:117

commit v3 on v2

--- a/solution.py
+++ b/solution.py
@@ -103,17 +103,38 @@
     by_row = jnp.transpose(matched_home, (1, 0, 2))
     row_all = lax.all_to_all(by_row, both, split_axis=0, concat_axis=0, tiled=True)
     row_all = row_all.reshape(devices * blocks_here, side_len)
-    weight_all = lax.all_gather(inv_var.astype(jnp.bfloat16), both, tiled=True)
-    segment_all = lax.all_gather((owner * CELLS + cell).astype(jnp.int32), both, tiled=True)
+    meta = jnp.stack([
+        inv_var.astype(jnp.bfloat16).astype(jnp.float32),
+        owner.astype(jnp.float32),
+        cell.astype(jnp.float32),
+    ])
+    meta = jnp.pad(meta, ((0, 8 - meta.shape[0]), (0, side_len - blocks_here)))
+    meta_all = lax.all_gather(meta, both, axis=0, tiled=True).reshape(devices, 8, side_len)
+    weight_all = meta_all[:, 0, :blocks_here].reshape(-1).astype(jnp.bfloat16)
+    owner_all = meta_all[:, 1, :blocks_here].reshape(-1).astype(jnp.int32)
+    cell_all = meta_all[:, 2, :blocks_here].reshape(-1).astype(jnp.int32)
+    segment_all = owner_all * CELLS + cell_all
     picks = segment_all[None, :] == jnp.arange(segments, dtype=jnp.int32)[:, None]
     weighted = jnp.where(picks, weight_all[None, :], jnp.zeros((), jnp.bfloat16))
     numerator = jnp.dot(weighted, row_all, preferred_element_type=jnp.float32)
-    weight_sum = jnp.sum(weighted.astype(jnp.float32), axis=1)
+    owner_pick = (owner_all[None, :] == jnp.arange(patches, dtype=jnp.int32)[:, None]).astype(
+        jnp.bfloat16
+    )
+    cell_pick = jnp.where(
+        cell_all[None, :] == jnp.arange(CELLS, dtype=jnp.int32)[:, None],
+        weight_all[None, :],
+        jnp.zeros((), jnp.bfloat16),
+    )
+    weight_sum = lax.dot_general(
+        owner_pick, cell_pick, (((1,), (1,)), ((), ())), preferred_element_type=jnp.float32
+    ).reshape(segments)
     coadd_row = numerator / jnp.maximum(weight_sum, 1.0)[:, None]
     template_row = coadd_row.astype(jnp.bfloat16)
-    difference_row = (
-        row_all.astype(jnp.float32) - template_row[segment_all].astype(jnp.float32)
+    block_pick = (
+        segment_all[:, None] == jnp.arange(segments, dtype=jnp.int32)[None, :]
     ).astype(jnp.bfloat16)
+    block_template = jnp.dot(block_pick, template_row, preferred_element_type=jnp.float32)
+    difference_row = (row_all.astype(jnp.float32) - block_template).astype(jnp.bfloat16)
     returned = lax.all_to_all(
         difference_row.reshape(devices, blocks_here, side_len),
         both, split_axis=0, concat_axis=0, tiled=True,

time: 278 us -> 163 us (0.59)
  blocking collectives: 144 us -> 52 us
  local copies, waits for them, and re-layouts: 37 us -> 12 us
  matrix products: 10.1 us -> 24.8 us
  other arithmetic: 19.5 us -> 6.99 us
    unnamed x2 -> x0, blocking collectives: 144 us -> none
    all_gather x0 -> x1, blocking collectives: none -> 52 us  [shards(): lax.all_gather(meta, both, axis=0, tiled=True).reshape(devices, 8, side_len)]
    gather x1 -> x0, local copies, waits for them, and re-layouts: 24 us -> none  [shards(): template_row[segment_all].astype(jnp.float32)]
    dot_general x0 -> x2, matrix products: none -> 14.7 us  [the longest x1 14.3 us: shards(): jnp.dot(block_pick, template_row, preferred_element_type=jnp.float32)]
    reduce_sum x1 -> x0, other arithmetic: 8.35 us -> none  [shards(): weight_sum = jnp.sum(weighted.astype(jnp.float32), axis=1)]
    convert_element_type x2, other arithmetic: 3.86 us -> 0.02 us  [the longest x1 0.01 us: shards(): owner_all = meta_all[:, 1, :blocks_here].reshape(-1).astype(jnp.int32)]
    unnamed x16 -> x12, local copies, waits for them, and re-layouts: 6.54 us -> 5.06 us
  transfers between devices with their start and end apart: 3 -> 3, of which waited for: 1 -> 2; matrix products, arithmetic and copies ran while one was open for 14% -> 10% of each run, Pallas kernels for 0% -> 0%
where the time goes in v3:
time: 163 us; the launch traced here: 160 us
  blocking collectives  52 us (32%)
  waiting for transfers between devices  29.5 us (18%)
  matrix products  24.8 us (15%)
  starting transfers between devices  23.5 us (14%)
  local copies, waits for them, and re-layouts  12 us (7%)
  Pallas kernels  10.8 us (7%)
  other arithmetic  6.99 us (4%)
    all_gather x1, blocking collectives, shards(): lax.all_gather(meta, both, axis=0, tiled=True).reshape(devices, 8, side_len)  52 us
    all_to_all x1, waiting for transfers between devices, shards(): lax.all_to_all(difference_row.reshape(devices, blocks_here, side_len), bo...  28.2 us
    dot_general x1, matrix products, shards(): jnp.dot(block_pick, template_row, preferred_element_type=jnp.float32)  14.3 us
    pallas_call x1, Pallas kernels, match_blocks(): pl.pallas_call(match_kernel, out_shape=jax.ShapeDtypeStruct(pixels.shape,...  10.8 us
    all_to_all x1, starting transfers between devices, shards(): lax.all_to_all(by_row, both, split_axis=0, concat_axis=0, tiled=True)  10.2 us
    dot_general x1, matrix products, shards(): numerator = jnp.dot(weighted, row_all, preferred_element_type=jnp.float32)  10.1 us
    all_to_all x1, starting transfers between devices, shards(): lax.all_to_all(difference_row.reshape(devices, blocks_here, side_len), bo...  7.31 us
    all_to_all x1, starting transfers between devices, shards(): lax.all_to_all(coadd_row.reshape(patches, CELLS, 1, side_len), 'patch', s...  5.97 us
  transfers between devices with their start and end apart: 3, of which 2 were waited for; matrix products, arithmetic and copies ran while one was open for 10% of the time, Pallas kernels for 0%

profile of v3, /device:TPU:32, one launch (start us, length us, event | category | flops | bytes accessed | tf_op | source)
XLA Modules:
  0.0 160.3 jit_solution(15551296918472623169)
XLA Ops:
  0.6 0.6 exponential_reduce_fusion.2
  1.9 0.6 exponential_reduce_fusion
  2.5 0.7 compare_select_fusion
  3.2 0.8 copy.24
  4.6 0.7 reshape.386.coef_ref
  5.3 0.7 fusion.40
  6.0 0.7 fusion.33
  6.8 0.7 fusion.39
  7.5 0.7 fusion.35
  8.3 0.7 fusion.38
  9.0 0.7 fusion.37.tab_ref
  9.7 0.8 copy.25.right_ref
  10.6 10.8 %shard_map.86 = bf16[64,128,128]{2,1,0:T(8,128)(2,1)} custom-call(f32[576]{0:T(1024)} %reshape.386.coef_ref, bf16[64,128,128]{2,1,0:T(8,128)(2,1)} %pix_ref.1, s32[64,128,128]{2,1,0:T(8,128)} %mask_ref.1, f32[6,128,128]{2,1,0:T(8,128)} %copy-done, bf16[128,768]{1,0:T(8,128)(2,1)} %copy.25.right_ref), custom_call_target="tpu_custom_call" | custom-call | flops 3221225472 | bytes 8388608 | tf_op jit(solution)/shard_map/pallas_call | solution.py:70
  21.4 4.3 %copy.26 = bf16[128,64,128]{2,1,0:T(8,128)(2,1)} copy(bf16[128,64,128]{2,0,1:T(8,128)(2,1)} %bitcast.35) | data formatting | bytes 4194304 | tf_op jit(solution)/shard_map/transpose | solution.py:103
  25.7 10.2 %all-to-all-start = ((bf16[128,64,128]{2,1,0:T(8,128)(2,1)}), bf16[128,64,128]{2,1,0:T(8,128)(2,1)S(1)}, u32[]{:S(2)}, u32[]{:S(2)}) async-start(bf16[128,64,128]{2,1,0:T(8,128)(2,1)} %copy.26), calls=%async_computation | async-start | bytes 4194304 | tf_op jit(solution)/shard_map/all_to_all | solution.py:104
  36.0 52.0 %all_gather.3 = f32[1024,128]{1,0:T(8,128)S(1)} all-gather(f32[8,128]{1,0:T(8,128)S(1)} %select_maximum_fusion), channel_id=1, replica_groups=mesh['visit'=4,'patch'=32] {'visit','patch'}, dimensions={0}, use_global_device_ids=true | all-gather | bytes 528384 | tf_op jit(solution)/shard_map/all_gather | solution.py:112
  88.9 10.1 %fusion.11 = f32[2048,128]{1,0:T(8,128)} fusion(bf16[8192,128]{1,0:T(8,128)(2,1)S(1)} %bitcast.32, s32[8192]{0:T(1024)S(1)} %multiply_add_fusion, bf16[8192]{0:T(1024)(128)(2,1)S(1)} %convert_element_type.113, f32[2048]{0:T(1024)S(1)} %max.15), kind=kOutput, calls=%fused_computation.14 | convolution fusion | flops 4328783872 | bytes 3203072 | tf_op jit(solution)/shard_map/dot_general | solution.py:119
  99.0 6.0 %all-to-all-start.1 = ((f32[32,64,1,128]{3,1,2,0:T(8,128)}), f32[32,64,1,128]{3,1,2,0:T(8,128)S(1)}, u32[]{:S(2)}, u32[]{:S(2)}) async-start(f32[32,64,1,128]{3,1,2,0:T(8,128)} %bitcast.36), calls=%async_computation.1 | async-start | bytes 2097152 | tf_op jit(solution)/shard_map/all_to_all | solution.py:143
  104.9 14.3 %fusion.9 = bf16[8192,128]{1,0:T(8,128)(2,1)} fusion(s32[8192]{0:T(1024)S(1)} %multiply_add_fusion, bf16[8192,128]{1,0:T(8,128)(2,1)S(1)} %bitcast.33, f32[2048,128]{1,0:T(8,128)} %fusion.11), kind=kOutput, calls=%fused_computation.11 | convolution fusion | flops 4315152384 | bytes 5275648 | tf_op jit(solution)/shard_map/dot_general | solution.py:136
  119.2 1.3 all-to-all-done.1
  120.5 7.3 %all-to-all-start.2 = ((bf16[128,64,128]{2,1,0:T(8,128)(2,1)}), bf16[128,64,128]{2,1,0:T(8,128)(2,1)S(1)}, u32[]{:S(2)}, u32[]{:S(2)}) async-start(bf16[128,64,128]{2,1,0:T(8,128)(2,1)} %bitcast.34), calls=%async_computation.2 | async-start | bytes 4194304 | tf_op jit(solution)/shard_map/all_to_all | solution.py:138
  127.8 1.6 copy.28
  129.4 28.2 %all-to-all-done.2 = bf16[128,64,128]{2,1,0:T(8,128)(2,1)S(1)} async-done(((bf16[128,64,128]{2,1,0:T(8,128)(2,1)}), bf16[128,64,128]{2,1,0:T(8,128)(2,1)S(1)}, u32[]{:S(2)}, u32[]{:S(2)}) %all-to-all-start.2) | async-done | bytes 2097184 | tf_op jit(solution)/shard_map/all_to_all | solution.py:138
  157.6 2.7 %copy.29 = bf16[64,128,128]{2,1,0:T(8,128)(2,1)} copy(bf16[64,128,128]{2,0,1:T(8,128)(2,1)S(1)} %bitcast.30) | data formatting | bytes 4194304
  (28 shorter events, 2.2 us)
Async XLA Ops:
  9.7 0.9 copy-start
  21.4 14.6 %copy-start.3 = (f32[64]{0:T(128)S(1)}, f32[64]{0:T(128)}, u32[]{:S(2)}) copy-start(f32[64]{0:T(128)} %param.9) | copy-start | bytes 772
  21.4 14.6 %copy-start.1 = (s32[64]{0:T(128)S(1)}, s32[64]{0:T(128)}, u32[]{:S(2)}) copy-start(s32[64]{0:T(128)} %param.11) | copy-start | bytes 772
  21.4 14.6 %copy-start.2 = (s32[64]{0:T(128)S(1)}, s32[64]{0:T(128)}, u32[]{:S(2)}) copy-start(s32[64]{0:T(128)} %param.10) | copy-start | bytes 772
  25.7 63.2 %all-to-all-start = ((bf16[128,64,128]{2,1,0:T(8,128)(2,1)}), bf16[128,64,128]{2,1,0:T(8,128)(2,1)S(1)}, u32[]{:S(2)}, u32[]{:S(2)}) async-start(bf16[128,64,128]{2,1,0:T(8,128)(2,1)} %copy.26), calls=%async_computation | async-start | bytes 4194304 | tf_op jit(solution)/shard_map/all_to_all | solution.py:104
  99.0 21.5 %all-to-all-start.1 = ((f32[32,64,1,128]{3,1,2,0:T(8,128)}), f32[32,64,1,128]{3,1,2,0:T(8,128)S(1)}, u32[]{:S(2)}, u32[]{:S(2)}) async-start(f32[32,64,1,128]{3,1,2,0:T(8,128)} %bitcast.36), calls=%async_computation.1 | async-start | bytes 2097152 | tf_op jit(solution)/shard_map/all_to_all | solution.py:143
  120.5 37.1 %all-to-all-start.2 = ((bf16[128,64,128]{2,1,0:T(8,128)(2,1)}), bf16[128,64,128]{2,1,0:T(8,128)(2,1)S(1)}, u32[]{:S(2)}, u32[]{:S(2)}) async-start(bf16[128,64,128]{2,1,0:T(8,128)(2,1)} %bitcast.34), calls=%async_computation.2 | async-start | bytes 4194304 | tf_op jit(solution)/shard_map/all_to_all | solution.py:138

commit v4 on v3

--- a/solution.py
+++ b/solution.py
@@ -101,18 +101,20 @@
     coefficients = coef_table[coef_index]
     matched_home = match_blocks(pixels, mask_bits, coefficients, tables, right_bands)
     by_row = jnp.transpose(matched_home, (1, 0, 2))
-    row_all = lax.all_to_all(by_row, both, split_axis=0, concat_axis=0, tiled=True)
-    row_all = row_all.reshape(devices * blocks_here, side_len)
-    meta = jnp.stack([
-        inv_var.astype(jnp.bfloat16).astype(jnp.float32),
-        owner.astype(jnp.float32),
-        cell.astype(jnp.float32),
+    weight = inv_var.astype(jnp.bfloat16)
+    meta = jnp.concatenate([
+        jnp.concatenate([weight, owner.astype(jnp.bfloat16)])[None, :],
+        jnp.concatenate([cell.astype(jnp.bfloat16), jnp.zeros_like(weight)])[None, :],
+        jnp.zeros((14, side_len), jnp.bfloat16),
     ])
-    meta = jnp.pad(meta, ((0, 8 - meta.shape[0]), (0, side_len - blocks_here)))
-    meta_all = lax.all_gather(meta, both, axis=0, tiled=True).reshape(devices, 8, side_len)
-    weight_all = meta_all[:, 0, :blocks_here].reshape(-1).astype(jnp.bfloat16)
-    owner_all = meta_all[:, 1, :blocks_here].reshape(-1).astype(jnp.int32)
-    cell_all = meta_all[:, 2, :blocks_here].reshape(-1).astype(jnp.int32)
+    payload = jnp.concatenate(
+        [by_row, jnp.broadcast_to(meta[None], (devices,) + meta.shape)], axis=1
+    )
+    received = lax.all_to_all(payload, both, split_axis=0, concat_axis=0, tiled=True)
+    row_all = received[:, :blocks_here].reshape(devices * blocks_here, side_len)
+    weight_all = received[:, blocks_here, :blocks_here].reshape(-1)
+    owner_all = received[:, blocks_here, blocks_here:].reshape(-1).astype(jnp.int32)
+    cell_all = received[:, blocks_here + 1, :blocks_here].reshape(-1).astype(jnp.int32)
     segment_all = owner_all * CELLS + cell_all
     picks = segment_all[None, :] == jnp.arange(segments, dtype=jnp.int32)[:, None]
     weighted = jnp.where(picks, weight_all[None, :], jnp.zeros((), jnp.bfloat16))

time: 163 us -> 147 us (0.902)
  starting transfers between devices: 23.5 us -> 11.7 us
  blocking collectives: 52 us -> 45.4 us
  other arithmetic: 6.99 us -> 11.6 us
  local copies, waits for them, and re-layouts: 12 us -> 9.82 us
    all_gather x1 -> x0, blocking collectives: 52 us -> none  [shards(): lax.all_gather(meta, both, axis=0, tiled=True).reshape(devices, 8, side_len)]
    all_to_all x0 -> x1, blocking collectives: none -> 45.4 us  [shards(): lax.all_to_all(payload, both, split_axis=0, concat_axis=0, tiled=True)]
    all_to_all x1 -> x0, starting transfers between devices: 10.2 us -> none  [shards(): lax.all_to_all(by_row, both, split_axis=0, concat_axis=0, tiled=True)]
    transpose x1 -> x0, local copies, waits for them, and re-layouts: 4.3 us -> none  [shards(): by_row = jnp.transpose(matched_home, (1, 0, 2))]
    convert_element_type x2 -> x4, other arithmetic: 0.02 us -> 2.49 us  [the longest x1 0.66 us: shards(): owner.astype(jnp.bfloat16)]
    concatenate x0 -> x2, other arithmetic: none -> 1.9 us  [the longest x1 1.82 us: shards(): jnp.concatenate([by_row, jnp.broadcast_to(meta[None], (devices,) + meta.s...]
    concatenate x0 -> x2, local copies, waits for them, and re-layouts: none -> 1.77 us  [the longest x1 1.69 us: shards(): jnp.concatenate([by_row, jnp.broadcast_to(meta[None], (devices,) + meta.s...]
    unnamed x12 -> x7, local copies, waits for them, and re-layouts: 5.06 us -> 5.05 us
  transfers between devices with their start and end apart: 3 -> 2, of which waited for: 2 -> 2; matrix products, arithmetic and copies ran while one was open for 10% -> 11% of each run, Pallas kernels for 0% -> 0%
where the time goes in v4:
time: 147 us; the launch traced here: 144 us
  blocking collectives  45.4 us (31%)
  waiting for transfers between devices  29.5 us (20%)
  matrix products  24.8 us (17%)
  starting transfers between devices  11.7 us (8%)
  other arithmetic  11.6 us (8%)
  Pallas kernels  10.8 us (7%)
  local copies, waits for them, and re-layouts  9.82 us (7%)
    all_to_all x1, blocking collectives, shards(): lax.all_to_all(payload, both, split_axis=0, concat_axis=0, tiled=True)  45.4 us
    all_to_all x1, waiting for transfers between devices, shards(): lax.all_to_all(difference_row.reshape(devices, blocks_here, side_len), bo...  28.2 us
    dot_general x1, matrix products, shards(): jnp.dot(block_pick, template_row, preferred_element_type=jnp.float32)  14.3 us
    pallas_call x1, Pallas kernels, match_blocks(): pl.pallas_call(match_kernel, out_shape=jax.ShapeDtypeStruct(pixels.shape,...  10.8 us
    dot_general x1, matrix products, shards(): numerator = jnp.dot(weighted, row_all, preferred_element_type=jnp.float32)  10.1 us
    all_to_all x1, starting transfers between devices, shards(): lax.all_to_all(difference_row.reshape(devices, blocks_here, side_len), bo...  6.3 us
    all_to_all x1, starting transfers between devices, shards(): lax.all_to_all(coadd_row.reshape(patches, CELLS, 1, side_len), 'patch', s...  5.39 us
    unnamed x7, local copies, waits for them, and re-layouts  5.05 us
  transfers between devices with their start and end apart: 2, of which 2 were waited for; matrix products, arithmetic and copies ran while one was open for 11% of the time, Pallas kernels for 0%

profile of v4, /device:TPU:32, one launch (start us, length us, event | category | flops | bytes accessed | tf_op | source)
XLA Modules:
  0.0 144.4 jit_solution(13235543581263397551)
XLA Ops:
  1.9 0.7 exponential_reduce_fusion
  3.2 0.7 convert_element_type.101
  3.9 0.7 convert_element_type.102
  5.2 0.8 copy.18
  6.6 0.7 reshape.380.coef_ref
  7.3 0.7 fusion.42
  8.0 0.7 fusion.33
  8.8 0.7 fusion.41
  9.5 0.7 fusion.35
  10.3 0.8 fusion.40
  11.1 0.8 fusion.37.tab_ref
  11.9 0.8 copy.19.right_ref
  13.0 10.8 %shard_map.86 = bf16[64,128,128]{2,1,0:T(8,128)(2,1)} custom-call(f32[576]{0:T(1024)} %reshape.380.coef_ref, bf16[64,128,128]{2,1,0:T(8,128)(2,1)} %pix_ref.1, s32[64,128,128]{2,1,0:T(8,128)} %mask_ref.1, f32[6,128,128]{2,1,0:T(8,128)} %copy-done.1, bf16[128,768]{1,0:T(8,128)(2,1)} %copy.19.right_ref), custom_call_target="tpu_custom_call" | custom-call | flops 3221225472 | bytes 8388608 | tf_op jit(solution)/shard_map/pallas_call | solution.py:70
  23.9 1.8 %pad_maximum_fusion = bf16[128,80,128]{2,0,1:T(8,128)(2,1)S(1)} fusion(bf16[128,16,128]{2,0,1:T(8,128)(2,1)S(1)} %broadcast_in_dim.67, bf16[128,64,128]{2,0,1:T(8,128)(2,1)} %bitcast.25), kind=kLoop, calls=%fused_computation.12 | loop fusion | flops 1310720 | bytes 5242880 | tf_op jit(solution)/shard_map/concatenate | solution.py:110
  25.7 1.7 %copy.20 = bf16[128,80,128]{2,1,0:T(8,128)(2,1)S(1)} copy(bf16[128,80,128]{2,0,1:T(8,128)(2,1)S(1)} %pad_maximum_fusion) | data formatting | bytes 5242880 | tf_op jit(solution)/shard_map/concatenate | solution.py:110
  27.4 45.4 %all_to_all.25 = bf16[128,80,128]{2,1,0:T(8,128)(2,1)S(1)} all-to-all(bf16[128,80,128]{2,1,0:T(8,128)(2,1)S(1)} %copy.20), channel_id=1, replica_groups=mesh['visit'=4,'patch'=32] {'visit','patch'}, dimensions={0} | all-to-all | bytes 5242880 | tf_op jit(solution)/shard_map/all_to_all | solution.py:113
  74.5 10.1 %fusion.11 = f32[2048,128]{1,0:T(8,128)} fusion(bf16[8192,128]{1,0:T(8,128)(2,1)S(1)} %bitcast.23, s32[8192]{0:T(1024)S(1)} %multiply_add_fusion, bf16[8192]{0:T(1024)(128)(2,1)S(1)} %broadcast_in_dim.68, f32[2048]{0:T(1024)S(1)} %max.15), kind=kOutput, calls=%fused_computation.15 | convolution fusion | flops 4328783872 | bytes 3203072 | tf_op jit(solution)/shard_map/dot_general | solution.py:121
  84.6 5.4 %all-to-all-start.1 = ((f32[32,64,1,128]{3,1,2,0:T(8,128)}), f32[32,64,1,128]{3,1,2,0:T(8,128)S(1)}, u32[]{:S(2)}, u32[]{:S(2)}) async-start(f32[32,64,1,128]{3,1,2,0:T(8,128)} %bitcast.7), calls=%async_computation.1 | async-start | bytes 2097152 | tf_op jit(solution)/shard_map/all_to_all | solution.py:145
  90.0 14.3 %fusion.9 = bf16[8192,128]{1,0:T(8,128)(2,1)} fusion(s32[8192]{0:T(1024)S(1)} %multiply_add_fusion, bf16[8192,128]{1,0:T(8,128)(2,1)} %bitcast.24, f32[2048,128]{1,0:T(8,128)} %fusion.11), kind=kOutput, calls=%fused_computation.11 | convolution fusion | flops 4315152384 | bytes 5275648 | tf_op jit(solution)/shard_map/dot_general | solution.py:138
  104.4 1.3 all-to-all-done.1
  105.7 6.3 %all-to-all-start.2 = ((bf16[128,64,128]{2,1,0:T(8,128)(2,1)}), bf16[128,64,128]{2,1,0:T(8,128)(2,1)S(1)}, u32[]{:S(2)}, u32[]{:S(2)}) async-start(bf16[128,64,128]{2,1,0:T(8,128)(2,1)} %bitcast.22), calls=%async_computation.2 | async-start | bytes 4194304 | tf_op jit(solution)/shard_map/all_to_all | solution.py:140
  112.0 1.6 %copy.22 = f32[64,32,128]{2,1,0:T(8,128)} copy(f32[64,32,128]{2,0,1:T(8,128)S(1)} %bitcast.21) | data formatting | bytes 2097152
  113.6 28.2 %all-to-all-done.2 = bf16[128,64,128]{2,1,0:T(8,128)(2,1)S(1)} async-done(((bf16[128,64,128]{2,1,0:T(8,128)(2,1)}), bf16[128,64,128]{2,1,0:T(8,128)(2,1)S(1)}, u32[]{:S(2)}, u32[]{:S(2)}) %all-to-all-start.2) | async-done | bytes 2097184 | tf_op jit(solution)/shard_map/all_to_all | solution.py:140
  141.8 2.7 %copy.23 = bf16[64,128,128]{2,1,0:T(8,128)(2,1)} copy(bf16[64,128,128]{2,0,1:T(8,128)(2,1)S(1)} %bitcast.20) | data formatting | bytes 4194304
  (26 shorter events, 5.2 us)
Async XLA Ops:
  11.9 1.1 copy-start.1
  74.5 10.1 %copy-start = (bf16[128,64,128]{2,1,0:T(8,128)(2,1)}, bf16[128,64,128]{2,1,0:T(8,128)(2,1)S(1)}, u32[]{:S(2)}) copy-start(bf16[128,64,128]{2,1,0:T(8,128)(2,1)S(1)} %slice.21) | copy-start | bytes 6291460
  84.6 21.1 %all-to-all-start.1 = ((f32[32,64,1,128]{3,1,2,0:T(8,128)}), f32[32,64,1,128]{3,1,2,0:T(8,128)S(1)}, u32[]{:S(2)}, u32[]{:S(2)}) async-start(f32[32,64,1,128]{3,1,2,0:T(8,128)} %bitcast.7), calls=%async_computation.1 | async-start | bytes 2097152 | tf_op jit(solution)/shard_map/all_to_all | solution.py:145
  105.7 36.1 %all-to-all-start.2 = ((bf16[128,64,128]{2,1,0:T(8,128)(2,1)}), bf16[128,64,128]{2,1,0:T(8,128)(2,1)S(1)}, u32[]{:S(2)}, u32[]{:S(2)}) async-start(bf16[128,64,128]{2,1,0:T(8,128)(2,1)} %bitcast.22), calls=%async_computation.2 | async-start | bytes 4194304 | tf_op jit(solution)/shard_map/all_to_all | solution.py:140

commit v5 on v4

--- a/solution.py
+++ b/solution.py
@@ -1,7 +1,6 @@
-import functools
-
 import jax
 import jax.numpy as jnp
+import numpy as np
 from jax import lax
 from jax.experimental import pallas as pl
 from jax.experimental.pallas import tpu as pltpu
@@ -17,19 +16,20 @@
 
 def band_tables(side_len):
     tap_reach = KSIZE // 2
-    position = jnp.arange(side_len).astype(jnp.float32)
+    position = np.arange(side_len).astype(np.float32)
     offset = position[:, None] - position[None, :]
-    inside = jnp.abs(offset) <= tap_reach
-    tap_offsets = jnp.arange(-tap_reach, tap_reach + 1).astype(jnp.float32)
+    inside = np.abs(offset) <= tap_reach
+    tap_offsets = np.arange(-tap_reach, tap_reach + 1).astype(np.float32)
     tables = []
     for spread in gauss_widths:
-        profile_sum = jnp.sum(jnp.exp(-tap_offsets * tap_offsets / (2.0 * spread * spread)))
-        even_band = jnp.where(
-            inside, jnp.exp(-offset * offset / (2.0 * spread * spread)) / profile_sum, 0.0
-        )
+        spread = np.float32(spread)
+        width = np.float32(2.0) * spread * spread
+        profile_sum = np.sum(np.exp(-tap_offsets * tap_offsets / width), dtype=np.float32)
+        even_band = np.where(inside, np.exp(-offset * offset / width) / profile_sum, 0.0)
+        even_band = even_band.astype(np.float32)
         tables.append(even_band)
-        tables.append(even_band * offset / spread)
-    return jnp.stack(tables)
+        tables.append((even_band * offset / spread).astype(np.float32))
+    return np.stack(tables)
 
 
 def match_kernel(coef_ref, pix_ref, mask_ref, tab_ref, right_ref, out_ref):
@@ -95,9 +95,10 @@
     rows_here = side_len // visits
     both = ("visit", "patch")
     tables = band_tables(side_len)
-    right_bands = (
-        jnp.transpose(tables, (2, 0, 1)).reshape(side_len, 6 * side_len).astype(jnp.bfloat16)
+    right_bands = jnp.asarray(
+        np.transpose(tables, (2, 0, 1)).reshape(side_len, 6 * side_len), jnp.bfloat16
     )
+    tables = jnp.asarray(tables)
     coefficients = coef_table[coef_index]
     matched_home = match_blocks(pixels, mask_bits, coefficients, tables, right_bands)
     by_row = jnp.transpose(matched_home, (1, 0, 2))
@@ -132,16 +133,23 @@
     ).reshape(segments)
     coadd_row = numerator / jnp.maximum(weight_sum, 1.0)[:, None]
     template_row = coadd_row.astype(jnp.bfloat16)
-    block_pick = (
-        segment_all[:, None] == jnp.arange(segments, dtype=jnp.int32)[None, :]
-    ).astype(jnp.bfloat16)
-    block_template = jnp.dot(block_pick, template_row, preferred_element_type=jnp.float32)
-    difference_row = (row_all.astype(jnp.float32) - block_template).astype(jnp.bfloat16)
-    returned = lax.all_to_all(
-        difference_row.reshape(devices, blocks_here, side_len),
-        both, split_axis=0, concat_axis=0, tiled=True,
-    )
-    difference = jnp.transpose(returned, (1, 0, 2))
+    row_blocks = row_all.reshape(devices, blocks_here, side_len)
+    segment_blocks = segment_all.reshape(devices, blocks_here)
+    half = blocks_here // 2
+    returned = []
+    for part in range(2):
+        part_rows = row_blocks[:, part * half:(part + 1) * half].reshape(-1, side_len)
+        part_segments = segment_blocks[:, part * half:(part + 1) * half].reshape(-1)
+        block_pick = (
+            part_segments[:, None] == jnp.arange(segments, dtype=jnp.int32)[None, :]
+        ).astype(jnp.bfloat16)
+        block_template = jnp.dot(block_pick, template_row, preferred_element_type=jnp.float32)
+        part_difference = (part_rows.astype(jnp.float32) - block_template).astype(jnp.bfloat16)
+        returned.append(lax.all_to_all(
+            part_difference.reshape(devices, half, side_len),
+            both, split_axis=0, concat_axis=0, tiled=True,
+        ))
+    difference = jnp.transpose(jnp.concatenate(returned, axis=1), (1, 0, 2))
     coadd_parts = lax.all_to_all(
         coadd_row.reshape(patches, CELLS, 1, side_len),
         "patch", split_axis=0, concat_axis=2, tiled=True,

time: 147 us -> 153 us (1.041)
  other arithmetic: 11.6 us -> 5.4 us
  starting transfers between devices: 11.7 us -> 17 us
  waiting for transfers between devices: 29.5 us -> 34.8 us
  local copies, waits for them, and re-layouts: 9.82 us -> 11.8 us
    all_to_all x1, waiting for transfers between devices: 1.33 us -> 7.5 us  [shards(): lax.all_to_all(coadd_row.reshape(patches, CELLS, 1, side_len), 'patch', s...]
    all_to_all x1 -> x2, starting transfers between devices: 6.3 us -> 10.9 us  [shards(): lax.all_to_all(part_difference.reshape(devices, half, side_len), both, sp...]
    unnamed x5 -> x0, other arithmetic: 3.75 us -> none
    reduce_sum x3 -> x0, other arithmetic: 1.92 us -> none  [band_tables(): jnp.sum(jnp.exp(-tap_offsets * tap_offsets / (2.0 * spread * spread)))]
    unnamed x7 -> x9, local copies, waits for them, and re-layouts: 5.05 us -> 6.28 us
    all_to_all x1 -> x2, waiting for transfers between devices: 28.2 us -> 27.3 us  [shards(): lax.all_to_all(part_difference.reshape(devices, half, side_len), both, sp...]
    dot_general x1 -> x2, matrix products: 14.3 us -> 13.7 us  [shards(): jnp.dot(block_pick, template_row, preferred_element_type=jnp.float32)]
  transfers between devices with their start and end apart: 2 -> 3, of which waited for: 2 -> 3; matrix products, arithmetic and copies ran while one was open for 11% -> 12% of each run, Pallas kernels for 0% -> 0%
where the time goes in v5:
time: 153 us; the launch traced here: 150 us
  blocking collectives  45.4 us (30%)
  waiting for transfers between devices  34.8 us (23%)
  matrix products  24.2 us (16%)
  starting transfers between devices  17 us (11%)
  local copies, waits for them, and re-layouts  11.8 us (8%)
  Pallas kernels  10.8 us (7%)
  other arithmetic  5.4 us (4%)
    all_to_all x1, blocking collectives, shards(): lax.all_to_all(payload, both, split_axis=0, concat_axis=0, tiled=True)  45.4 us
    all_to_all x2, waiting for transfers between devices, shards(): lax.all_to_all(part_difference.reshape(devices, half, side_len), both, sp...  27.3 us
    dot_general x2, matrix products, shards(): jnp.dot(block_pick, template_row, preferred_element_type=jnp.float32)  13.7 us
    all_to_all x2, starting transfers between devices, shards(): lax.all_to_all(part_difference.reshape(devices, half, side_len), both, sp...  10.9 us
    pallas_call x1, Pallas kernels, match_blocks(): pl.pallas_call(match_kernel, out_shape=jax.ShapeDtypeStruct(pixels.shape,...  10.8 us
    dot_general x1, matrix products, shards(): numerator = jnp.dot(weighted, row_all, preferred_element_type=jnp.float32)  10.1 us
    all_to_all x1, waiting for transfers between devices, shards(): lax.all_to_all(coadd_row.reshape(patches, CELLS, 1, side_len), 'patch', s...  7.5 us
    unnamed x9, local copies, waits for them, and re-layouts  6.28 us
  transfers between devices with their start and end apart: 3, of which 3 were waited for; matrix products, arithmetic and copies ran while one was open for 12% of the time, Pallas kernels for 0%

profile of v5, /device:TPU:32, one launch (start us, length us, event | category | flops | bytes accessed | tf_op | source)
XLA Modules:
  0.0 150.1 jit_solution(13722975007696736973)
XLA Ops:
  0.6 0.7 convert_element_type.67
  1.3 0.7 convert_element_type.68
  1.9 0.7 convert_element_type.69
  2.6 0.8 copy.22
  3.4 0.7 compare_select_fusion
  4.1 0.6 gather_fusion
  4.7 0.7 reshape.71.coef_ref
  5.6 10.8 %shard_map.104 = bf16[64,128,128]{2,1,0:T(8,128)(2,1)} custom-call(f32[576]{0:T(1024)} %reshape.71.coef_ref, bf16[64,128,128]{2,1,0:T(8,128)(2,1)} %pix_ref.1, s32[64,128,128]{2,1,0:T(8,128)} %mask_ref.1, f32[6,128,128]{2,1,0:T(8,128)} %constant.4.clone.tab_ref, bf16[128,768]{1,0:T(8,128)(2,1)} %constant.3.clone.right_ref), custom_call_target="tpu_custom_call" | custom-call | flops 3221225472 | bytes 8388608 | tf_op jit(solution)/shard_map/pallas_call | solution.py:70
  16.5 1.8 %pad_maximum_fusion = bf16[128,80,128]{2,0,1:T(8,128)(2,1)S(1)} fusion(bf16[128,16,128]{2,0,1:T(8,128)(2,1)S(1)} %broadcast_in_dim.58, bf16[128,64,128]{2,0,1:T(8,128)(2,1)} %bitcast.24), kind=kLoop, calls=%fused_computation.17 | loop fusion | flops 1310720 | bytes 5242880 | tf_op jit(solution)/shard_map/concatenate | solution.py:111
  18.3 1.7 %copy.23 = bf16[128,80,128]{2,1,0:T(8,128)(2,1)S(1)} copy(bf16[128,80,128]{2,0,1:T(8,128)(2,1)S(1)} %pad_maximum_fusion) | data formatting | bytes 5242880 | tf_op jit(solution)/shard_map/concatenate | solution.py:111
  20.0 45.4 %all_to_all.30 = bf16[128,80,128]{2,1,0:T(8,128)(2,1)S(1)} all-to-all(bf16[128,80,128]{2,1,0:T(8,128)(2,1)S(1)} %copy.23), channel_id=1, replica_groups=mesh['visit'=4,'patch'=32] {'visit','patch'}, dimensions={0} | all-to-all | bytes 5242880 | tf_op jit(solution)/shard_map/all_to_all | solution.py:114
  65.4 0.5 fusion.25
  67.3 10.1 %fusion.15 = f32[2048,128]{1,0:T(8,128)} fusion(bf16[8192,128]{1,0:T(8,128)(2,1)S(1)} %bitcast.25, s32[8192]{0:T(1024)S(1)} %multiply_add_fusion.1, bf16[8192]{0:T(1024)(128)(2,1)S(1)} %broadcast_in_dim.59, f32[2048]{0:T(1024)S(1)} %max.15), kind=kOutput, calls=%fused_computation.21 | convolution fusion | flops 4328783872 | bytes 3203072 | tf_op jit(solution)/shard_map/dot_general | solution.py:122
  77.4 6.1 %all-to-all-start.1 = ((f32[32,64,1,128]{3,1,2,0:T(8,128)}), f32[32,64,1,128]{3,1,2,0:T(8,128)}, u32[]{:S(2)}, u32[]{:S(2)}) async-start(f32[32,64,1,128]{3,1,2,0:T(8,128)} %bitcast.26), calls=%async_computation.1 | async-start | bytes 2097152 | tf_op jit(solution)/shard_map/all_to_all | solution.py:153
  83.5 1.3 fusion.29
  84.8 6.8 %fusion.12 = bf16[4096,128]{1,0:T(8,128)(2,1)} fusion(s32[4096]{0:T(1024)S(1)} %eq.78, bf16[4096,128]{1,0:T(8,128)(2,1)S(1)} %bitcast.28, f32[2048,128]{1,0:T(8,128)S(1)} %copy-done), kind=kOutput, calls=%fused_computation.15 | convolution fusion | flops 2157707264 | bytes 3162112 | tf_op jit(solution)/shard_map/dot_general | solution.py:146
  91.7 7.5 %all-to-all-done.1 = f32[32,64,1,128]{3,1,2,0:T(8,128)} async-done(((f32[32,64,1,128]{3,1,2,0:T(8,128)}), f32[32,64,1,128]{3,1,2,0:T(8,128)}, u32[]{:S(2)}, u32[]{:S(2)}) %all-to-all-start.1) | async-done | bytes 1048608 | tf_op jit(solution)/shard_map/all_to_all | solution.py:153
  99.2 5.4 %all-to-all-start.2 = ((bf16[128,32,128]{2,1,0:T(8,128)(2,1)}), bf16[128,32,128]{2,1,0:T(8,128)(2,1)S(1)}, u32[]{:S(2)}, u32[]{:S(2)}) async-start(bf16[128,32,128]{2,1,0:T(8,128)(2,1)} %bitcast.11), calls=%async_computation.2 | async-start | bytes 2097152 | tf_op jit(solution)/shard_map/all_to_all | solution.py:148
  104.7 6.8 %fusion.13 = bf16[4096,128]{1,0:T(8,128)(2,1)} fusion(s32[4096]{0:T(1024)S(1)} %eq.82, bf16[4096,128]{1,0:T(8,128)(2,1)S(1)} %bitcast.27, f32[2048,128]{1,0:T(8,128)S(1)} %copy-done.1), kind=kOutput, calls=%fused_computation.16 | convolution fusion | flops 2157707264 | bytes 3162112 | tf_op jit(solution)/shard_map/dot_general | solution.py:146
  111.6 11.6 %all-to-all-done.2 = bf16[128,32,128]{2,1,0:T(8,128)(2,1)S(1)} async-done(((bf16[128,32,128]{2,1,0:T(8,128)(2,1)}), bf16[128,32,128]{2,1,0:T(8,128)(2,1)S(1)}, u32[]{:S(2)}, u32[]{:S(2)}) %all-to-all-start.2) | async-done | bytes 1048608 | tf_op jit(solution)/shard_map/all_to_all | solution.py:148
  123.1 5.5 %all-to-all-start.3 = ((bf16[128,32,128]{2,1,0:T(8,128)(2,1)}), bf16[128,32,128]{2,1,0:T(8,128)(2,1)S(1)}, u32[]{:S(2)}, u32[]{:S(2)}) async-start(bf16[128,32,128]{2,1,0:T(8,128)(2,1)} %bitcast.13), calls=%async_computation.3 | async-start | bytes 2097152 | tf_op jit(solution)/shard_map/all_to_all | solution.py:148
  128.6 2.8 %copy.25 = f32[64,32,128]{2,1,0:T(8,128)} copy(f32[64,32,128]{2,0,1:T(8,128)} %bitcast.8) | data formatting | bytes 2097152
  131.4 15.7 %all-to-all-done.3 = bf16[128,32,128]{2,1,0:T(8,128)(2,1)S(1)} async-done(((bf16[128,32,128]{2,1,0:T(8,128)(2,1)}), bf16[128,32,128]{2,1,0:T(8,128)(2,1)S(1)}, u32[]{:S(2)}, u32[]{:S(2)}) %all-to-all-start.3) | async-done | bytes 1048608 | tf_op jit(solution)/shard_map/all_to_all | solution.py:148
  147.4 2.7 %copy.26 = bf16[64,128,128]{2,1,0:T(8,128)(2,1)} copy(bf16[64,128,128]{2,0,1:T(8,128)(2,1)S(1)} %maximum_bitcast_fusion) | data formatting | bytes 4194304
  (24 shorter events, 2.0 us)
Async XLA Ops:
  77.4 21.8 %all-to-all-start.1 = ((f32[32,64,1,128]{3,1,2,0:T(8,128)}), f32[32,64,1,128]{3,1,2,0:T(8,128)}, u32[]{:S(2)}, u32[]{:S(2)}) async-start(f32[32,64,1,128]{3,1,2,0:T(8,128)} %bitcast.26), calls=%async_computation.1 | async-start | bytes 2097152 | tf_op jit(solution)/shard_map/all_to_all | solution.py:153
  83.5 1.3 copy-start
  84.8 19.9 %copy-start.1 = (f32[2048,128]{1,0:T(8,128)S(1)}, f32[2048,128]{1,0:T(8,128)}, u32[]{:S(2)}) copy-start(f32[2048,128]{1,0:T(8,128)} %fusion.15) | copy-start | bytes 3145732
  84.8 19.9 %copy-start.2 = (bf16[128,32,128]{2,1,0:T(8,128)(2,1)S(1)}, bf16[128,32,128]{2,1,0:T(8,128)(2,1)}, u32[]{:S(2)}) copy-start(bf16[128,32,128]{2,1,0:T(8,128)(2,1)} %get-tuple-element.7) | copy-start | bytes 3145732
  99.2 23.9 %all-to-all-start.2 = ((bf16[128,32,128]{2,1,0:T(8,128)(2,1)}), bf16[128,32,128]{2,1,0:T(8,128)(2,1)S(1)}, u32[]{:S(2)}, u32[]{:S(2)}) async-start(bf16[128,32,128]{2,1,0:T(8,128)(2,1)} %bitcast.11), calls=%async_computation.2 | async-start | bytes 2097152 | tf_op jit(solution)/shard_map/all_to_all | solution.py:148
  123.1 24.0 %all-to-all-start.3 = ((bf16[128,32,128]{2,1,0:T(8,128)(2,1)}), bf16[128,32,128]{2,1,0:T(8,128)(2,1)S(1)}, u32[]{:S(2)}, u32[]{:S(2)}) async-start(bf16[128,32,128]{2,1,0:T(8,128)(2,1)} %bitcast.13), calls=%async_computation.3 | async-start | bytes 2097152 | tf_op jit(solution)/shard_map/all_to_all | solution.py:148

commit v6 on v4

--- a/solution.py
+++ b/solution.py
@@ -1,7 +1,6 @@
-import functools
-
 import jax
 import jax.numpy as jnp
+import numpy as np
 from jax import lax
 from jax.experimental import pallas as pl
 from jax.experimental.pallas import tpu as pltpu
@@ -17,19 +16,20 @@
 
 def band_tables(side_len):
     tap_reach = KSIZE // 2
-    position = jnp.arange(side_len).astype(jnp.float32)
+    position = np.arange(side_len).astype(np.float32)
     offset = position[:, None] - position[None, :]
-    inside = jnp.abs(offset) <= tap_reach
-    tap_offsets = jnp.arange(-tap_reach, tap_reach + 1).astype(jnp.float32)
+    inside = np.abs(offset) <= tap_reach
+    tap_offsets = np.arange(-tap_reach, tap_reach + 1).astype(np.float32)
     tables = []
     for spread in gauss_widths:
-        profile_sum = jnp.sum(jnp.exp(-tap_offsets * tap_offsets / (2.0 * spread * spread)))
-        even_band = jnp.where(
-            inside, jnp.exp(-offset * offset / (2.0 * spread * spread)) / profile_sum, 0.0
-        )
+        spread = np.float32(spread)
+        width = np.float32(2.0) * spread * spread
+        profile_sum = np.sum(np.exp(-tap_offsets * tap_offsets / width), dtype=np.float32)
+        even_band = np.where(inside, np.exp(-offset * offset / width) / profile_sum, 0.0)
+        even_band = even_band.astype(np.float32)
         tables.append(even_band)
-        tables.append(even_band * offset / spread)
-    return jnp.stack(tables)
+        tables.append((even_band * offset / spread).astype(np.float32))
+    return np.stack(tables)
 
 
 def match_kernel(coef_ref, pix_ref, mask_ref, tab_ref, right_ref, out_ref):
@@ -95,9 +95,10 @@
     rows_here = side_len // visits
     both = ("visit", "patch")
     tables = band_tables(side_len)
-    right_bands = (
-        jnp.transpose(tables, (2, 0, 1)).reshape(side_len, 6 * side_len).astype(jnp.bfloat16)
+    right_bands = jnp.asarray(
+        np.transpose(tables, (2, 0, 1)).reshape(side_len, 6 * side_len), jnp.bfloat16
     )
+    tables = jnp.asarray(tables)
     coefficients = coef_table[coef_index]
     matched_home = match_blocks(pixels, mask_bits, coefficients, tables, right_bands)
     by_row = jnp.transpose(matched_home, (1, 0, 2))

time: 147 us -> 140 us (0.952)
  other arithmetic: 11.6 us -> 5.14 us
    unnamed x5 -> x0, other arithmetic: 3.75 us -> none
    reduce_sum x3 -> x0, other arithmetic: 1.92 us -> none  [band_tables(): jnp.sum(jnp.exp(-tap_offsets * tap_offsets / (2.0 * spread * spread)))]
    unnamed x7 -> x5, local copies, waits for them, and re-layouts: 5.05 us -> 5.04 us
  transfers between devices with their start and end apart: 2 -> 2, of which waited for: 2 -> 2; matrix products, arithmetic and copies ran while one was open for 11% -> 12% of each run, Pallas kernels for 0% -> 0%
where the time goes in v6:
time: 140 us; the launch traced here: 137 us
  blocking collectives  45.4 us (32%)
  waiting for transfers between devices  29.5 us (21%)
  matrix products  24.8 us (18%)
  starting transfers between devices  11.7 us (8%)
  Pallas kernels  10.8 us (8%)
  local copies, waits for them, and re-layouts  9 us (6%)
  other arithmetic  5.14 us (4%)
    all_to_all x1, blocking collectives, shards(): lax.all_to_all(payload, both, split_axis=0, concat_axis=0, tiled=True)  45.4 us
    all_to_all x1, waiting for transfers between devices, shards(): lax.all_to_all(difference_row.reshape(devices, blocks_here, side_len), bo...  28.2 us
    dot_general x1, matrix products, shards(): jnp.dot(block_pick, template_row, preferred_element_type=jnp.float32)  14.3 us
    pallas_call x1, Pallas kernels, match_blocks(): pl.pallas_call(match_kernel, out_shape=jax.ShapeDtypeStruct(pixels.shape,...  10.8 us
    dot_general x1, matrix products, shards(): numerator = jnp.dot(weighted, row_all, preferred_element_type=jnp.float32)  10.1 us
    all_to_all x1, starting transfers between devices, shards(): lax.all_to_all(difference_row.reshape(devices, blocks_here, side_len), bo...  6.3 us
    all_to_all x1, starting transfers between devices, shards(): lax.all_to_all(coadd_row.reshape(patches, CELLS, 1, side_len), 'patch', s...  5.39 us
    unnamed x5, local copies, waits for them, and re-layouts  5.04 us
  transfers between devices with their start and end apart: 2, of which 2 were waited for; matrix products, arithmetic and copies ran while one was open for 12% of the time, Pallas kernels for 0%

profile of v6, /device:TPU:32, one launch (start us, length us, event | category | flops | bytes accessed | tf_op | source)
XLA Modules:
  0.0 137.1 jit_solution(9053750392233483686)
XLA Ops:
  0.6 0.7 convert_element_type.54
  1.3 0.7 convert_element_type.55
  1.9 0.7 convert_element_type.56
  2.6 0.7 compare_select_fusion
  3.3 0.8 copy.18
  4.1 0.6 gather_fusion
  4.7 0.7 reshape.64.coef_ref
  5.6 10.8 %shard_map.104 = bf16[64,128,128]{2,1,0:T(8,128)(2,1)} custom-call(f32[576]{0:T(1024)} %reshape.64.coef_ref, bf16[64,128,128]{2,1,0:T(8,128)(2,1)} %pix_ref.1, s32[64,128,128]{2,1,0:T(8,128)} %mask_ref.1, f32[6,128,128]{2,1,0:T(8,128)} %constant.4.clone.tab_ref, bf16[128,768]{1,0:T(8,128)(2,1)} %constant.3.clone.right_ref), custom_call_target="tpu_custom_call" | custom-call | flops 3221225472 | bytes 8388608 | tf_op jit(solution)/shard_map/pallas_call | solution.py:70
  16.5 1.8 %pad_maximum_fusion = bf16[128,80,128]{2,0,1:T(8,128)(2,1)S(1)} fusion(bf16[128,16,128]{2,0,1:T(8,128)(2,1)S(1)} %broadcast_in_dim.58, bf16[128,64,128]{2,0,1:T(8,128)(2,1)} %bitcast.22), kind=kLoop, calls=%fused_computation.12 | loop fusion | flops 1310720 | bytes 5242880 | tf_op jit(solution)/shard_map/concatenate | solution.py:111
  18.3 1.7 %copy.19 = bf16[128,80,128]{2,1,0:T(8,128)(2,1)S(1)} copy(bf16[128,80,128]{2,0,1:T(8,128)(2,1)S(1)} %pad_maximum_fusion) | data formatting | bytes 5242880 | tf_op jit(solution)/shard_map/concatenate | solution.py:111
  20.0 45.4 %all_to_all.25 = bf16[128,80,128]{2,1,0:T(8,128)(2,1)S(1)} all-to-all(bf16[128,80,128]{2,1,0:T(8,128)(2,1)S(1)} %copy.19), channel_id=1, replica_groups=mesh['visit'=4,'patch'=32] {'visit','patch'}, dimensions={0} | all-to-all | bytes 5242880 | tf_op jit(solution)/shard_map/all_to_all | solution.py:114
  65.4 0.2 slice_reduce_fusion
  65.6 0.1 broadcast_in_dim.59
  65.7 0.5 fusion.21
  66.4 0.4 convolution_maximum_fusion
  66.8 0.3 slice.21
  67.2 10.1 %fusion.11 = f32[2048,128]{1,0:T(8,128)} fusion(bf16[8192,128]{1,0:T(8,128)(2,1)S(1)} %bitcast.20, s32[8192]{0:T(1024)S(1)} %multiply_add_fusion, bf16[8192]{0:T(1024)(128)(2,1)S(1)} %broadcast_in_dim.59, f32[2048]{0:T(1024)S(1)} %max.15), kind=kOutput, calls=%fused_computation.15 | convolution fusion | flops 4328783872 | bytes 3203072 | tf_op jit(solution)/shard_map/dot_general | solution.py:122
  77.3 5.4 %all-to-all-start.1 = ((f32[32,64,1,128]{3,1,2,0:T(8,128)}), f32[32,64,1,128]{3,1,2,0:T(8,128)S(1)}, u32[]{:S(2)}, u32[]{:S(2)}) async-start(f32[32,64,1,128]{3,1,2,0:T(8,128)} %bitcast.5), calls=%async_computation.1 | async-start | bytes 2097152 | tf_op jit(solution)/shard_map/all_to_all | solution.py:146
  82.7 14.3 %fusion.9 = bf16[8192,128]{1,0:T(8,128)(2,1)} fusion(s32[8192]{0:T(1024)S(1)} %multiply_add_fusion, bf16[8192,128]{1,0:T(8,128)(2,1)} %bitcast.21, f32[2048,128]{1,0:T(8,128)} %fusion.11), kind=kOutput, calls=%fused_computation.11 | convolution fusion | flops 4315152384 | bytes 5275648 | tf_op jit(solution)/shard_map/dot_general | solution.py:139
  97.0 1.3 all-to-all-done.1
  98.3 6.3 %all-to-all-start.2 = ((bf16[128,64,128]{2,1,0:T(8,128)(2,1)}), bf16[128,64,128]{2,1,0:T(8,128)(2,1)S(1)}, u32[]{:S(2)}, u32[]{:S(2)}) async-start(bf16[128,64,128]{2,1,0:T(8,128)(2,1)} %bitcast.19), calls=%async_computation.2 | async-start | bytes 4194304 | tf_op jit(solution)/shard_map/all_to_all | solution.py:141
  104.6 1.6 %copy.21 = f32[64,32,128]{2,1,0:T(8,128)} copy(f32[64,32,128]{2,0,1:T(8,128)S(1)} %bitcast.18) | data formatting | bytes 2097152
  106.2 28.2 %all-to-all-done.2 = bf16[128,64,128]{2,1,0:T(8,128)(2,1)S(1)} async-done(((bf16[128,64,128]{2,1,0:T(8,128)(2,1)}), bf16[128,64,128]{2,1,0:T(8,128)(2,1)S(1)}, u32[]{:S(2)}, u32[]{:S(2)}) %all-to-all-start.2) | async-done | bytes 2097184 | tf_op jit(solution)/shard_map/all_to_all | solution.py:141
  134.4 2.7 %copy.22 = bf16[64,128,128]{2,1,0:T(8,128)(2,1)} copy(bf16[64,128,128]{2,0,1:T(8,128)(2,1)S(1)} %bitcast.17) | data formatting | bytes 4194304
  (12 shorter events, 0.5 us)
Async XLA Ops:
  67.1 10.1 %copy-start = (bf16[128,64,128]{2,1,0:T(8,128)(2,1)}, bf16[128,64,128]{2,1,0:T(8,128)(2,1)S(1)}, u32[]{:S(2)}) copy-start(bf16[128,64,128]{2,1,0:T(8,128)(2,1)S(1)} %slice.21) | copy-start | bytes 6291460
  77.3 21.1 %all-to-all-start.1 = ((f32[32,64,1,128]{3,1,2,0:T(8,128)}), f32[32,64,1,128]{3,1,2,0:T(8,128)S(1)}, u32[]{:S(2)}, u32[]{:S(2)}) async-start(f32[32,64,1,128]{3,1,2,0:T(8,128)} %bitcast.5), calls=%async_computation.1 | async-start | bytes 2097152 | tf_op jit(solution)/shard_map/all_to_all | solution.py:146
  98.3 36.1 %all-to-all-start.2 = ((bf16[128,64,128]{2,1,0:T(8,128)(2,1)}), bf16[128,64,128]{2,1,0:T(8,128)(2,1)S(1)}, u32[]{:S(2)}, u32[]{:S(2)}) async-start(bf16[128,64,128]{2,1,0:T(8,128)(2,1)} %bitcast.19), calls=%async_computation.2 | async-start | bytes 4194304 | tf_op jit(solution)/shard_map/all_to_all | solution.py:141

commit v7 on v6

--- a/solution.py
+++ b/solution.py
@@ -101,21 +101,22 @@
     tables = jnp.asarray(tables)
     coefficients = coef_table[coef_index]
     matched_home = match_blocks(pixels, mask_bits, coefficients, tables, right_bands)
-    by_row = jnp.transpose(matched_home, (1, 0, 2))
     weight = inv_var.astype(jnp.bfloat16)
     meta = jnp.concatenate([
         jnp.concatenate([weight, owner.astype(jnp.bfloat16)])[None, :],
         jnp.concatenate([cell.astype(jnp.bfloat16), jnp.zeros_like(weight)])[None, :],
         jnp.zeros((14, side_len), jnp.bfloat16),
     ])
-    payload = jnp.concatenate(
-        [by_row, jnp.broadcast_to(meta[None], (devices,) + meta.shape)], axis=1
+    by_row = jnp.transpose(matched_home, (1, 0, 2))
+    meta_all = lax.all_to_all(
+        jnp.broadcast_to(meta[None], (devices,) + meta.shape), both,
+        split_axis=0, concat_axis=0, tiled=True,
     )
-    received = lax.all_to_all(payload, both, split_axis=0, concat_axis=0, tiled=True)
-    row_all = received[:, :blocks_here].reshape(devices * blocks_here, side_len)
-    weight_all = received[:, blocks_here, :blocks_here].reshape(-1)
-    owner_all = received[:, blocks_here, blocks_here:].reshape(-1).astype(jnp.int32)
-    cell_all = received[:, blocks_here + 1, :blocks_here].reshape(-1).astype(jnp.int32)
+    row_all = lax.all_to_all(by_row, both, split_axis=0, concat_axis=0, tiled=True)
+    row_all = row_all.reshape(devices * blocks_here, side_len)
+    weight_all = meta_all[:, 0, :blocks_here].reshape(-1)
+    owner_all = meta_all[:, 0, blocks_here:].reshape(-1).astype(jnp.int32)
+    cell_all = meta_all[:, 1, :blocks_here].reshape(-1).astype(jnp.int32)
     segment_all = owner_all * CELLS + cell_all
     picks = segment_all[None, :] == jnp.arange(segments, dtype=jnp.int32)[:, None]
     weighted = jnp.where(picks, weight_all[None, :], jnp.zeros((), jnp.bfloat16))

time: 140 us -> 144 us (1.029)
  blocking collectives: 45.4 us -> 0 us
  waiting for transfers between devices: 29.5 us -> 57.9 us
  starting transfers between devices: 11.7 us -> 31.6 us
  local copies, waits for them, and re-layouts: 9 us -> 12.1 us
  other arithmetic: 5.14 us -> 3.31 us
    all_to_all x1 -> x0, blocking collectives: 45.4 us -> none  [shards(): lax.all_to_all(payload, both, split_axis=0, concat_axis=0, tiled=True)]
    all_to_all x0 -> x2, waiting for transfers between devices: none -> 28.3 us  [the longest x1 28.3 us: shards(): lax.all_to_all(by_row, both, split_axis=0, concat_axis=0, tiled=True)]
    all_to_all x0 -> x2, starting transfers between devices: none -> 20 us  [the longest x1 10.2 us: shards(): lax.all_to_all(jnp.broadcast_to(meta[None], (devices,) + meta.shape), bot...]
    transpose x0 -> x1, local copies, waits for them, and re-layouts: none -> 4.28 us  [shards(): by_row = jnp.transpose(matched_home, (1, 0, 2))]
    concatenate x1 -> x0, other arithmetic: 1.82 us -> none  [shards(): jnp.concatenate([by_row, jnp.broadcast_to(meta[None], (devices,) + meta.s...]
    concatenate x1 -> x0, local copies, waits for them, and re-layouts: 1.69 us -> none  [shards(): jnp.concatenate([by_row, jnp.broadcast_to(meta[None], (devices,) + meta.s...]
    unnamed x5 -> x3, local copies, waits for them, and re-layouts: 5.04 us -> 5.04 us
  transfers between devices with their start and end apart: 2 -> 4, of which waited for: 2 -> 3; matrix products, arithmetic and copies ran while one was open for 12% -> 17% of each run, Pallas kernels for 0% -> 8%
where the time goes in v7:
time: 144 us; the launch traced here: 141 us
  waiting for transfers between devices  57.9 us (40%)
  starting transfers between devices  31.6 us (22%)
  matrix products  24.8 us (17%)
  local copies, waits for them, and re-layouts  12.1 us (8%)
  Pallas kernels  10.8 us (8%)
  other arithmetic  3.31 us (2%)
    all_to_all x1, waiting for transfers between devices, shards(): lax.all_to_all(by_row, both, split_axis=0, concat_axis=0, tiled=True)  28.3 us
    all_to_all x1, waiting for transfers between devices, shards(): lax.all_to_all(difference_row.reshape(devices, blocks_here, side_len), bo...  28.2 us
    dot_general x1, matrix products, shards(): jnp.dot(block_pick, template_row, preferred_element_type=jnp.float32)  14.3 us
    pallas_call x1, Pallas kernels, match_blocks(): pl.pallas_call(match_kernel, out_shape=jax.ShapeDtypeStruct(pixels.shape,...  10.8 us
    all_to_all x1, starting transfers between devices, shards(): lax.all_to_all(jnp.broadcast_to(meta[None], (devices,) + meta.shape), bot...  10.2 us
    dot_general x1, matrix products, shards(): numerator = jnp.dot(weighted, row_all, preferred_element_type=jnp.float32)  10.1 us
    all_to_all x1, starting transfers between devices, shards(): lax.all_to_all(by_row, both, split_axis=0, concat_axis=0, tiled=True)  9.77 us
    all_to_all x1, starting transfers between devices, shards(): lax.all_to_all(difference_row.reshape(devices, blocks_here, side_len), bo...  6.25 us
  transfers between devices with their start and end apart: 4, of which 3 were waited for; matrix products, arithmetic and copies ran while one was open for 17% of the time, Pallas kernels for 8%

profile of v7, /device:TPU:32, one launch (start us, length us, event | category | flops | bytes accessed | tf_op | source)
XLA Modules:
  0.0 141.2 jit_solution(5766194129298708506)
XLA Ops:
  0.6 0.7 convert_element_type.54
  1.3 0.7 convert_element_type.55
  1.9 0.7 convert_element_type.56
  2.8 0.9 broadcast_in_dim.57
  3.7 10.2 %all-to-all-start = ((bf16[128,16,128]{2,1,0:T(8,128)(2,1)}), bf16[128,16,128]{2,1,0:T(8,128)(2,1)S(1)}, u32[]{:S(2)}, u32[]{:S(2)}) async-start(bf16[128,16,128]{2,1,0:T(8,128)(2,1)} %broadcast_in_dim.57), calls=%async_computation | async-start | bytes 1048576 | tf_op jit(solution)/shard_map/all_to_all | solution.py:111
  13.9 0.7 compare_select_fusion
  14.6 0.8 copy.18
  15.4 0.6 gather_fusion
  16.0 0.7 reshape.64.coef_ref
  16.7 10.8 %shard_map.104 = bf16[64,128,128]{2,1,0:T(8,128)(2,1)} custom-call(f32[576]{0:T(1024)} %reshape.64.coef_ref, bf16[64,128,128]{2,1,0:T(8,128)(2,1)} %pix_ref.1, s32[64,128,128]{2,1,0:T(8,128)} %mask_ref.1, f32[6,128,128]{2,1,0:T(8,128)} %constant.4.clone.tab_ref, bf16[128,768]{1,0:T(8,128)(2,1)} %constant.3.clone.right_ref), custom_call_target="tpu_custom_call" | custom-call | flops 3221225472 | bytes 8388608 | tf_op jit(solution)/shard_map/pallas_call | solution.py:70
  27.5 4.3 %copy.19 = bf16[128,64,128]{2,1,0:T(8,128)(2,1)} copy(bf16[128,64,128]{2,0,1:T(8,128)(2,1)} %bitcast.22) | data formatting | bytes 4194304 | tf_op jit(solution)/shard_map/transpose | solution.py:110
  31.8 9.8 %all-to-all-start.1 = ((bf16[128,64,128]{2,1,0:T(8,128)(2,1)}), bf16[128,64,128]{2,1,0:T(8,128)(2,1)S(1)}, u32[]{:S(2)}, u32[]{:S(2)}) async-start(bf16[128,64,128]{2,1,0:T(8,128)(2,1)} %copy.19), calls=%async_computation.1 | async-start | bytes 4194304 | tf_op jit(solution)/shard_map/all_to_all | solution.py:115
  41.6 0.2 slice_reduce_fusion
  41.8 0.5 fusion.21
  42.5 0.4 convolution_maximum_fusion
  43.0 28.3 %all-to-all-done.1 = bf16[128,64,128]{2,1,0:T(8,128)(2,1)S(1)} async-done(((bf16[128,64,128]{2,1,0:T(8,128)(2,1)}), bf16[128,64,128]{2,1,0:T(8,128)(2,1)S(1)}, u32[]{:S(2)}, u32[]{:S(2)}) %all-to-all-start.1) | async-done | bytes 2097184 | tf_op jit(solution)/shard_map/all_to_all | solution.py:115
  71.3 10.1 %fusion.11 = f32[2048,128]{1,0:T(8,128)} fusion(bf16[8192,128]{1,0:T(8,128)(2,1)S(1)} %bitcast.19, s32[8192]{0:T(1024)S(1)} %multiply_add_fusion, bf16[8192]{0:T(1024)(128)(2,1)S(1)} %broadcast_in_dim.58, f32[2048]{0:T(1024)S(1)} %max.15), kind=kOutput, calls=%fused_computation.14 | convolution fusion | flops 4328783872 | bytes 3203072 | tf_op jit(solution)/shard_map/dot_general | solution.py:123
  81.4 5.4 %all-to-all-start.2 = ((f32[32,64,1,128]{3,1,2,0:T(8,128)}), f32[32,64,1,128]{3,1,2,0:T(8,128)S(1)}, u32[]{:S(2)}, u32[]{:S(2)}) async-start(f32[32,64,1,128]{3,1,2,0:T(8,128)} %bitcast.23), calls=%async_computation.2 | async-start | bytes 2097152 | tf_op jit(solution)/shard_map/all_to_all | solution.py:147
  86.8 14.3 %fusion.9 = bf16[8192,128]{1,0:T(8,128)(2,1)} fusion(s32[8192]{0:T(1024)S(1)} %multiply_add_fusion, bf16[8192,128]{1,0:T(8,128)(2,1)S(1)} %bitcast.20, f32[2048,128]{1,0:T(8,128)} %fusion.11), kind=kOutput, calls=%fused_computation.11 | convolution fusion | flops 4315152384 | bytes 5275648 | tf_op jit(solution)/shard_map/dot_general | solution.py:140
  101.1 1.4 all-to-all-done.2
  102.5 6.3 %all-to-all-start.3 = ((bf16[128,64,128]{2,1,0:T(8,128)(2,1)}), bf16[128,64,128]{2,1,0:T(8,128)(2,1)S(1)}, u32[]{:S(2)}, u32[]{:S(2)}) async-start(bf16[128,64,128]{2,1,0:T(8,128)(2,1)} %bitcast.21), calls=%async_computation.3 | async-start | bytes 4194304 | tf_op jit(solution)/shard_map/all_to_all | solution.py:142
  108.7 1.6 %copy.21 = f32[64,32,128]{2,1,0:T(8,128)} copy(f32[64,32,128]{2,0,1:T(8,128)S(1)} %bitcast.18) | data formatting | bytes 2097152
  110.3 28.2 %all-to-all-done.3 = bf16[128,64,128]{2,1,0:T(8,128)(2,1)S(1)} async-done(((bf16[128,64,128]{2,1,0:T(8,128)(2,1)}), bf16[128,64,128]{2,1,0:T(8,128)(2,1)S(1)}, u32[]{:S(2)}, u32[]{:S(2)}) %all-to-all-start.3) | async-done | bytes 2097184 | tf_op jit(solution)/shard_map/all_to_all | solution.py:142
  138.5 2.7 %copy.22 = bf16[64,128,128]{2,1,0:T(8,128)(2,1)} copy(bf16[64,128,128]{2,0,1:T(8,128)(2,1)S(1)} %bitcast.17) | data formatting | bytes 4194304
  (11 shorter events, 0.6 us)
Async XLA Ops:
  3.7 28.1 %all-to-all-start = ((bf16[128,16,128]{2,1,0:T(8,128)(2,1)}), bf16[128,16,128]{2,1,0:T(8,128)(2,1)S(1)}, u32[]{:S(2)}, u32[]{:S(2)}) async-start(bf16[128,16,128]{2,1,0:T(8,128)(2,1)} %broadcast_in_dim.57), calls=%async_computation | async-start | bytes 1048576 | tf_op jit(solution)/shard_map/all_to_all | solution.py:111
  31.8 39.5 %all-to-all-start.1 = ((bf16[128,64,128]{2,1,0:T(8,128)(2,1)}), bf16[128,64,128]{2,1,0:T(8,128)(2,1)S(1)}, u32[]{:S(2)}, u32[]{:S(2)}) async-start(bf16[128,64,128]{2,1,0:T(8,128)(2,1)} %copy.19), calls=%async_computation.1 | async-start | bytes 4194304 | tf_op jit(solution)/shard_map/all_to_all | solution.py:115
  81.4 21.0 %all-to-all-start.2 = ((f32[32,64,1,128]{3,1,2,0:T(8,128)}), f32[32,64,1,128]{3,1,2,0:T(8,128)S(1)}, u32[]{:S(2)}, u32[]{:S(2)}) async-start(f32[32,64,1,128]{3,1,2,0:T(8,128)} %bitcast.23), calls=%async_computation.2 | async-start | bytes 2097152 | tf_op jit(solution)/shard_map/all_to_all | solution.py:147
  102.5 36.0 %all-to-all-start.3 = ((bf16[128,64,128]{2,1,0:T(8,128)(2,1)}), bf16[128,64,128]{2,1,0:T(8,128)(2,1)S(1)}, u32[]{:S(2)}, u32[]{:S(2)}) async-start(bf16[128,64,128]{2,1,0:T(8,128)(2,1)} %bitcast.21), calls=%async_computation.3 | async-start | bytes 4194304 | tf_op jit(solution)/shard_map/all_to_all | solution.py:142

commit v8 on v6

--- a/solution.py
+++ b/solution.py
@@ -45,22 +45,20 @@
     for g in range(group):
         base = (step * group + g) * 9
         rows = columns[g * side_len:(g + 1) * side_len]
-        acc = jnp.zeros((side_len, side_len), jnp.float32)
+        stacked = jnp.concatenate(
+            [rows[:, s * side_len:(s + 1) * side_len] for s in range(6)], axis=0
+        )
+        lefts = []
         for m in range(3):
             even_band = tab_ref[2 * m]
             odd_band = tab_ref[2 * m + 1]
-            left_a = (coef_ref[base + 3 * m] * even_band
-                      + coef_ref[base + 3 * m + 1] * odd_band).astype(jnp.bfloat16)
-            left_b = (coef_ref[base + 3 * m + 2] * even_band).astype(jnp.bfloat16)
-            acc = acc + jnp.dot(
-                left_a, rows[:, (2 * m) * side_len:(2 * m + 1) * side_len],
-                preferred_element_type=jnp.float32,
-            )
-            acc = acc + jnp.dot(
-                left_b, rows[:, (2 * m + 1) * side_len:(2 * m + 2) * side_len],
-                preferred_element_type=jnp.float32,
-            )
-        out_ref[g] = acc.astype(jnp.bfloat16)
+            lefts.append((coef_ref[base + 3 * m] * even_band
+                          + coef_ref[base + 3 * m + 1] * odd_band).astype(jnp.bfloat16))
+            lefts.append((coef_ref[base + 3 * m + 2] * even_band).astype(jnp.bfloat16))
+        left = jnp.concatenate(lefts, axis=1)
+        out_ref[g] = jnp.dot(left, stacked, preferred_element_type=jnp.float32).astype(
+            jnp.bfloat16
+        )
 
 
 def match_blocks(pixels, mask_bits, coefficients, tables, right_bands):

time: 140 us -> 140 us (level)
  no operation moved by 1% of the time
where the time goes in v8:
time: 140 us; the launch traced here: 137 us
  blocking collectives  45.4 us (32%)
  waiting for transfers between devices  29.5 us (21%)
  matrix products  24.8 us (18%)
  starting transfers between devices  11.7 us (8%)
  Pallas kernels  11.1 us (8%)
  local copies, waits for them, and re-layouts  9 us (6%)
  other arithmetic  5.14 us (4%)
    all_to_all x1, blocking collectives, shards(): lax.all_to_all(payload, both, split_axis=0, concat_axis=0, tiled=True)  45.4 us
    all_to_all x1, waiting for transfers between devices, shards(): lax.all_to_all(difference_row.reshape(devices, blocks_here, side_len), bo...  28.2 us
    dot_general x1, matrix products, shards(): jnp.dot(block_pick, template_row, preferred_element_type=jnp.float32)  14.3 us
    pallas_call x1, Pallas kernels, match_blocks(): pl.pallas_call(match_kernel, out_shape=jax.ShapeDtypeStruct(pixels.shape,...  11.1 us
    dot_general x1, matrix products, shards(): numerator = jnp.dot(weighted, row_all, preferred_element_type=jnp.float32)  10.1 us
    all_to_all x1, starting transfers between devices, shards(): lax.all_to_all(difference_row.reshape(devices, blocks_here, side_len), bo...  6.3 us
    all_to_all x1, starting transfers between devices, shards(): lax.all_to_all(coadd_row.reshape(patches, CELLS, 1, side_len), 'patch', s...  5.39 us
    unnamed x5, local copies, waits for them, and re-layouts  5.04 us
  transfers between devices with their start and end apart: 2, of which 2 were waited for; matrix products, arithmetic and copies ran while one was open for 12% of the time, Pallas kernels for 0%

profile of v8, /device:TPU:32, one launch (start us, length us, event | category | flops | bytes accessed | tf_op | source)
XLA Modules:
  0.0 137.4 jit_solution(601289907010213710)
XLA Ops:
  0.6 0.7 convert_element_type.54
  1.3 0.7 convert_element_type.55
  1.9 0.7 convert_element_type.56
  2.6 0.7 compare_select_fusion
  3.3 0.8 copy.18
  4.1 0.6 gather_fusion
  4.7 0.7 reshape.64.coef_ref
  5.6 11.1 %shard_map.104 = bf16[64,128,128]{2,1,0:T(8,128)(2,1)} custom-call(f32[576]{0:T(1024)} %reshape.64.coef_ref, bf16[64,128,128]{2,1,0:T(8,128)(2,1)} %pix_ref.1, s32[64,128,128]{2,1,0:T(8,128)} %mask_ref.1, f32[6,128,128]{2,1,0:T(8,128)} %constant.4.clone.tab_ref, bf16[128,768]{1,0:T(8,128)(2,1)} %constant.3.clone.right_ref), custom_call_target="tpu_custom_call" | custom-call | flops 3221225472 | bytes 8388608 | tf_op jit(solution)/shard_map/pallas_call | solution.py:68
  16.8 1.8 %pad_maximum_fusion = bf16[128,80,128]{2,0,1:T(8,128)(2,1)S(1)} fusion(bf16[128,16,128]{2,0,1:T(8,128)(2,1)S(1)} %broadcast_in_dim.58, bf16[128,64,128]{2,0,1:T(8,128)(2,1)} %bitcast.22), kind=kLoop, calls=%fused_computation.12 | loop fusion | flops 1310720 | bytes 5242880 | tf_op jit(solution)/shard_map/concatenate | solution.py:109
  18.6 1.7 %copy.19 = bf16[128,80,128]{2,1,0:T(8,128)(2,1)S(1)} copy(bf16[128,80,128]{2,0,1:T(8,128)(2,1)S(1)} %pad_maximum_fusion) | data formatting | bytes 5242880 | tf_op jit(solution)/shard_map/concatenate | solution.py:109
  20.3 45.4 %all_to_all.25 = bf16[128,80,128]{2,1,0:T(8,128)(2,1)S(1)} all-to-all(bf16[128,80,128]{2,1,0:T(8,128)(2,1)S(1)} %copy.19), channel_id=1, replica_groups=mesh['visit'=4,'patch'=32] {'visit','patch'}, dimensions={0} | all-to-all | bytes 5242880 | tf_op jit(solution)/shard_map/all_to_all | solution.py:112
  65.8 0.2 slice_reduce_fusion
  65.9 0.1 broadcast_in_dim.59
  66.0 0.5 fusion.21
  66.7 0.4 convolution_maximum_fusion
  67.2 0.3 slice.21
  67.5 10.1 %fusion.11 = f32[2048,128]{1,0:T(8,128)} fusion(bf16[8192,128]{1,0:T(8,128)(2,1)S(1)} %bitcast.20, s32[8192]{0:T(1024)S(1)} %multiply_add_fusion, bf16[8192]{0:T(1024)(128)(2,1)S(1)} %broadcast_in_dim.59, f32[2048]{0:T(1024)S(1)} %max.15), kind=kOutput, calls=%fused_computation.15 | convolution fusion | flops 4328783872 | bytes 3203072 | tf_op jit(solution)/shard_map/dot_general | solution.py:120
  77.6 5.4 %all-to-all-start.1 = ((f32[32,64,1,128]{3,1,2,0:T(8,128)}), f32[32,64,1,128]{3,1,2,0:T(8,128)S(1)}, u32[]{:S(2)}, u32[]{:S(2)}) async-start(f32[32,64,1,128]{3,1,2,0:T(8,128)} %bitcast.5), calls=%async_computation.1 | async-start | bytes 2097152 | tf_op jit(solution)/shard_map/all_to_all | solution.py:144
  83.0 14.3 %fusion.9 = bf16[8192,128]{1,0:T(8,128)(2,1)} fusion(s32[8192]{0:T(1024)S(1)} %multiply_add_fusion, bf16[8192,128]{1,0:T(8,128)(2,1)} %bitcast.21, f32[2048,128]{1,0:T(8,128)} %fusion.11), kind=kOutput, calls=%fused_computation.11 | convolution fusion | flops 4315152384 | bytes 5275648 | tf_op jit(solution)/shard_map/dot_general | solution.py:137
  97.3 1.3 all-to-all-done.1
  98.6 6.3 %all-to-all-start.2 = ((bf16[128,64,128]{2,1,0:T(8,128)(2,1)}), bf16[128,64,128]{2,1,0:T(8,128)(2,1)S(1)}, u32[]{:S(2)}, u32[]{:S(2)}) async-start(bf16[128,64,128]{2,1,0:T(8,128)(2,1)} %bitcast.19), calls=%async_computation.2 | async-start | bytes 4194304 | tf_op jit(solution)/shard_map/all_to_all | solution.py:139
  105.0 1.6 %copy.21 = f32[64,32,128]{2,1,0:T(8,128)} copy(f32[64,32,128]{2,0,1:T(8,128)S(1)} %bitcast.18) | data formatting | bytes 2097152
  106.5 28.2 %all-to-all-done.2 = bf16[128,64,128]{2,1,0:T(8,128)(2,1)S(1)} async-done(((bf16[128,64,128]{2,1,0:T(8,128)(2,1)}), bf16[128,64,128]{2,1,0:T(8,128)(2,1)S(1)}, u32[]{:S(2)}, u32[]{:S(2)}) %all-to-all-start.2) | async-done | bytes 2097184 | tf_op jit(solution)/shard_map/all_to_all | solution.py:139
  134.7 2.7 %copy.22 = bf16[64,128,128]{2,1,0:T(8,128)(2,1)} copy(bf16[64,128,128]{2,0,1:T(8,128)(2,1)S(1)} %bitcast.17) | data formatting | bytes 4194304
  (12 shorter events, 0.5 us)
Async XLA Ops:
  67.5 10.1 %copy-start = (bf16[128,64,128]{2,1,0:T(8,128)(2,1)}, bf16[128,64,128]{2,1,0:T(8,128)(2,1)S(1)}, u32[]{:S(2)}) copy-start(bf16[128,64,128]{2,1,0:T(8,128)(2,1)S(1)} %slice.21) | copy-start | bytes 6291460
  77.6 21.1 %all-to-all-start.1 = ((f32[32,64,1,128]{3,1,2,0:T(8,128)}), f32[32,64,1,128]{3,1,2,0:T(8,128)S(1)}, u32[]{:S(2)}, u32[]{:S(2)}) async-start(f32[32,64,1,128]{3,1,2,0:T(8,128)} %bitcast.5), calls=%async_computation.1 | async-start | bytes 2097152 | tf_op jit(solution)/shard_map/all_to_all | solution.py:144
  98.6 36.1 %all-to-all-start.2 = ((bf16[128,64,128]{2,1,0:T(8,128)(2,1)}), bf16[128,64,128]{2,1,0:T(8,128)(2,1)S(1)}, u32[]{:S(2)}, u32[]{:S(2)}) async-start(bf16[128,64,128]{2,1,0:T(8,128)(2,1)} %bitcast.19), calls=%async_computation.2 | async-start | bytes 4194304 | tf_op jit(solution)/shard_map/all_to_all | solution.py:139

commit v9 on v6

--- a/solution.py
+++ b/solution.py
@@ -32,7 +32,7 @@
     return np.stack(tables)
 
 
-def match_kernel(coef_ref, pix_ref, mask_ref, tab_ref, right_ref, out_ref):
+def match_kernel(index_ref, coef_ref, pix_ref, mask_ref, tab_ref, right_ref, out_ref):
     step = pl.program_id(0)
     group, side_len, _ = pix_ref.shape
     bits = mask_ref[...]
@@ -43,7 +43,8 @@
         preferred_element_type=jnp.float32,
     ).astype(jnp.bfloat16)
     for g in range(group):
-        base = (step * group + g) * 9
+        chosen = jnp.minimum(jnp.maximum(index_ref[step * group + g], 0), coef_ref.shape[0] // 9 - 1)
+        base = chosen * 9
         rows = columns[g * side_len:(g + 1) * side_len]
         acc = jnp.zeros((side_len, side_len), jnp.float32)
         for m in range(3):
@@ -63,7 +64,7 @@
         out_ref[g] = acc.astype(jnp.bfloat16)
 
 
-def match_blocks(pixels, mask_bits, coefficients, tables, right_bands):
+def match_blocks(pixels, mask_bits, coef_index, coef_table, tables, right_bands):
     number, side_len, _ = pixels.shape
     steps = number // GROUP
     flops = number * 4 * side_len * side_len * 6 * side_len
@@ -72,6 +73,7 @@
         out_shape=jax.ShapeDtypeStruct(pixels.shape, jnp.bfloat16),
         grid=(steps,),
         in_specs=[
+            pl.BlockSpec(memory_space=pltpu.SMEM),
             pl.BlockSpec(memory_space=pltpu.SMEM),
             pl.BlockSpec((GROUP, side_len, side_len), lambda i: (i, 0, 0)),
             pl.BlockSpec((GROUP, side_len, side_len), lambda i: (i, 0, 0)),
@@ -82,7 +84,7 @@
         cost_estimate=pl.CostEstimate(
             flops=flops, transcendentals=0, bytes_accessed=number * side_len * side_len * 8
         ),
-    )(coefficients.reshape(-1), pixels, mask_bits, tables, right_bands)
+    )(coef_index, coef_table.reshape(-1), pixels, mask_bits, tables, right_bands)
 
 
 def shards(pixels, mask_bits, inv_var, owner, cell, coef_index, coef_table):
@@ -99,18 +101,16 @@
         np.transpose(tables, (2, 0, 1)).reshape(side_len, 6 * side_len), jnp.bfloat16
     )
     tables = jnp.asarray(tables)
-    coefficients = coef_table[coef_index]
-    matched_home = match_blocks(pixels, mask_bits, coefficients, tables, right_bands)
-    by_row = jnp.transpose(matched_home, (1, 0, 2))
-    weight = inv_var.astype(jnp.bfloat16)
-    meta = jnp.concatenate([
-        jnp.concatenate([weight, owner.astype(jnp.bfloat16)])[None, :],
-        jnp.concatenate([cell.astype(jnp.bfloat16), jnp.zeros_like(weight)])[None, :],
-        jnp.zeros((14, side_len), jnp.bfloat16),
-    ])
-    payload = jnp.concatenate(
-        [by_row, jnp.broadcast_to(meta[None], (devices,) + meta.shape)], axis=1
-    )
+    matched_home = match_blocks(pixels, mask_bits, coef_index, coef_table, tables, right_bands)
+    meta = jnp.stack([
+        inv_var,
+        owner.astype(jnp.float32),
+        cell.astype(jnp.float32),
+        jnp.zeros_like(inv_var),
+    ]).astype(jnp.bfloat16).reshape(2, 2 * blocks_here)
+    meta = jnp.pad(meta, ((0, 14), (0, side_len - 2 * blocks_here)))
+    meta_blocks = jnp.broadcast_to(meta[:, None, :], (16, side_len, side_len))
+    payload = jnp.transpose(jnp.concatenate([matched_home, meta_blocks], axis=0), (1, 0, 2))
     received = lax.all_to_all(payload, both, split_axis=0, concat_axis=0, tiled=True)
     row_all = received[:, :blocks_here].reshape(devices * blocks_here, side_len)
     weight_all = received[:, blocks_here, :blocks_here].reshape(-1)

time: 140 us -> 138 us (0.986)
    convert_element_type x3 -> x0, other arithmetic: 1.97 us -> none  [the longest x1 0.66 us: shards(): weight = inv_var.astype(jnp.bfloat16)]
    concatenate x2 -> x0, other arithmetic: 1.9 us -> none  [the longest x1 1.82 us: shards(): jnp.concatenate([by_row, jnp.broadcast_to(meta[None], (devices,) + meta.s...]
    transpose x0 -> x1, other arithmetic: none -> 1.82 us  [shards(): jnp.transpose(jnp.concatenate([matched_home, meta_blocks], axis=0), (1, 0...]
    concatenate x2 -> x0, local copies, waits for them, and re-layouts: 1.77 us -> none  [the longest x1 1.69 us: shards(): jnp.concatenate([by_row, jnp.broadcast_to(meta[None], (devices,) + meta.s...]
    transpose x0 -> x1, local copies, waits for them, and re-layouts: none -> 1.69 us  [shards(): jnp.transpose(jnp.concatenate([matched_home, meta_blocks], axis=0), (1, 0...]
    another operation x0 -> x3, other arithmetic: none -> 1.41 us  [shards(): jnp.stack([inv_var, owner.astype(jnp.float32), cell.astype(jnp.float32),...]
where the time goes in v9:
time: 138 us; the launch traced here: 135 us
  blocking collectives  45.4 us (33%)
  waiting for transfers between devices  29.5 us (21%)
  matrix products  24.8 us (18%)
  starting transfers between devices  11.7 us (8%)
  Pallas kernels  10.8 us (8%)
  local copies, waits for them, and re-layouts  8.49 us (6%)
  other arithmetic  3.75 us (3%)
    all_to_all x1, blocking collectives, shards(): lax.all_to_all(payload, both, split_axis=0, concat_axis=0, tiled=True)  45.4 us
    all_to_all x1, waiting for transfers between devices, shards(): lax.all_to_all(difference_row.reshape(devices, blocks_here, side_len), bo...  28.2 us
    dot_general x1, matrix products, shards(): jnp.dot(block_pick, template_row, preferred_element_type=jnp.float32)  14.3 us
    pallas_call x1, Pallas kernels, match_blocks(): pl.pallas_call(match_kernel, out_shape=jax.ShapeDtypeStruct(pixels.shape,...  10.8 us
    dot_general x1, matrix products, shards(): numerator = jnp.dot(weighted, row_all, preferred_element_type=jnp.float32)  10.1 us
    all_to_all x1, starting transfers between devices, shards(): lax.all_to_all(difference_row.reshape(devices, blocks_here, side_len), bo...  6.3 us
    all_to_all x1, starting transfers between devices, shards(): lax.all_to_all(coadd_row.reshape(patches, CELLS, 1, side_len), 'patch', s...  5.39 us
    unnamed x5, local copies, waits for them, and re-layouts  5.04 us
  transfers between devices with their start and end apart: 2, of which 2 were waited for; matrix products, arithmetic and copies ran while one was open for 12% of the time, Pallas kernels for 0%

profile of v9, /device:TPU:32, one launch (start us, length us, event | category | flops | bytes accessed | tf_op | source)
XLA Modules:
  0.0 135.2 jit_solution(16064482584533833946)
XLA Ops:
  0.6 0.7 convert_bitcast_fusion.2
  1.3 0.1 pad.10.clone
  1.4 0.7 convert_bitcast_fusion
  2.1 0.1 convert_element_type.60
  2.2 0.8 copy.17
  3.0 0.7 reshape.67.coef_ref
  3.7 10.8 %shard_map.104 = bf16[64,128,128]{2,1,0:T(8,128)(2,1)} custom-call(s32[64]{0:T(128)} %index_ref.1, f32[576]{0:T(1024)} %reshape.67.coef_ref, bf16[64,128,128]{2,1,0:T(8,128)(2,1)} %pix_ref.1, s32[64,128,128]{2,1,0:T(8,128)} %mask_ref.1, f32[6,128,128]{2,1,0:T(8,128)} %constant.15.clone.tab_ref, bf16[128,768]{1,0:T(8,128)(2,1)} %constant.14.clone.right_ref), custom_call_target="tpu_custom_call" | custom-call | flops 3221225472 | bytes 8388608 | tf_op jit(solution)/shard_map/pallas_call | solution.py:71
  14.6 1.8 %maximum_bitcast_fusion = bf16[128,80,128]{2,0,1:T(8,128)(2,1)S(1)} fusion(bf16[16,128,128]{2,1,0:T(8,128)(2,1)S(1)} %broadcast_in_dim.28, bf16[64,128,128]{2,1,0:T(8,128)(2,1)} %shard_map.104), kind=kLoop, calls=%fused_computation.11 | loop fusion | flops 1310720 | bytes 5242880 | tf_op jit(solution)/shard_map/transpose | solution.py:113
  16.4 1.7 %copy.18 = bf16[128,80,128]{2,1,0:T(8,128)(2,1)S(1)} copy(bf16[128,80,128]{2,0,1:T(8,128)(2,1)S(1)} %maximum_bitcast_fusion) | data formatting | bytes 5242880 | tf_op jit(solution)/shard_map/transpose | solution.py:113
  18.1 45.4 %all_to_all.25 = bf16[128,80,128]{2,1,0:T(8,128)(2,1)S(1)} all-to-all(bf16[128,80,128]{2,1,0:T(8,128)(2,1)S(1)} %copy.18), channel_id=1, replica_groups=mesh['visit'=4,'patch'=32] {'visit','patch'}, dimensions={0} | all-to-all | bytes 5242880 | tf_op jit(solution)/shard_map/all_to_all | solution.py:114
  63.5 0.2 slice_reduce_fusion
  63.7 0.1 broadcast_in_dim.42
  63.8 0.5 fusion.21
  64.3 0.1 reshape.72
  64.5 0.4 convolution_maximum_fusion
  64.9 0.3 slice.19
  65.3 10.1 %fusion.11 = f32[2048,128]{1,0:T(8,128)} fusion(bf16[8192,128]{1,0:T(8,128)(2,1)S(1)} %bitcast.24, s32[8192]{0:T(1024)S(1)} %multiply_add_fusion, bf16[8192]{0:T(1024)(128)(2,1)S(1)} %broadcast_in_dim.42, f32[2048]{0:T(1024)S(1)} %max.15), kind=kOutput, calls=%fused_computation.14 | convolution fusion | flops 4328783872 | bytes 3203072 | tf_op jit(solution)/shard_map/dot_general | solution.py:122
  75.3 5.4 %all-to-all-start.1 = ((f32[32,64,1,128]{3,1,2,0:T(8,128)}), f32[32,64,1,128]{3,1,2,0:T(8,128)S(1)}, u32[]{:S(2)}, u32[]{:S(2)}) async-start(f32[32,64,1,128]{3,1,2,0:T(8,128)} %bitcast.6), calls=%async_computation.1 | async-start | bytes 2097152 | tf_op jit(solution)/shard_map/all_to_all | solution.py:146
  80.7 14.3 %fusion.9 = bf16[8192,128]{1,0:T(8,128)(2,1)} fusion(s32[8192]{0:T(1024)S(1)} %multiply_add_fusion, bf16[8192,128]{1,0:T(8,128)(2,1)} %bitcast.25, f32[2048,128]{1,0:T(8,128)} %fusion.11), kind=kOutput, calls=%fused_computation.10 | convolution fusion | flops 4315152384 | bytes 5275648 | tf_op jit(solution)/shard_map/dot_general | solution.py:139
  95.1 1.3 all-to-all-done.1
  96.4 6.3 %all-to-all-start.2 = ((bf16[128,64,128]{2,1,0:T(8,128)(2,1)}), bf16[128,64,128]{2,1,0:T(8,128)(2,1)S(1)}, u32[]{:S(2)}, u32[]{:S(2)}) async-start(bf16[128,64,128]{2,1,0:T(8,128)(2,1)} %bitcast.23), calls=%async_computation.2 | async-start | bytes 4194304 | tf_op jit(solution)/shard_map/all_to_all | solution.py:141
  102.7 1.6 %copy.20 = f32[64,32,128]{2,1,0:T(8,128)} copy(f32[64,32,128]{2,0,1:T(8,128)S(1)} %bitcast.22) | data formatting | bytes 2097152
  104.3 28.2 %all-to-all-done.2 = bf16[128,64,128]{2,1,0:T(8,128)(2,1)S(1)} async-done(((bf16[128,64,128]{2,1,0:T(8,128)(2,1)}), bf16[128,64,128]{2,1,0:T(8,128)(2,1)S(1)}, u32[]{:S(2)}, u32[]{:S(2)}) %all-to-all-start.2) | async-done | bytes 2097184 | tf_op jit(solution)/shard_map/all_to_all | solution.py:141
  132.5 2.7 %copy.21 = bf16[64,128,128]{2,1,0:T(8,128)(2,1)} copy(bf16[64,128,128]{2,0,1:T(8,128)(2,1)S(1)} %bitcast.21) | data formatting | bytes 4194304
  (8 shorter events, 0.3 us)
Async XLA Ops:
  65.2 10.1 %copy-start = (bf16[128,64,128]{2,1,0:T(8,128)(2,1)}, bf16[128,64,128]{2,1,0:T(8,128)(2,1)S(1)}, u32[]{:S(2)}) copy-start(bf16[128,64,128]{2,1,0:T(8,128)(2,1)S(1)} %slice.19) | copy-start | bytes 6291460
  75.3 21.1 %all-to-all-start.1 = ((f32[32,64,1,128]{3,1,2,0:T(8,128)}), f32[32,64,1,128]{3,1,2,0:T(8,128)S(1)}, u32[]{:S(2)}, u32[]{:S(2)}) async-start(f32[32,64,1,128]{3,1,2,0:T(8,128)} %bitcast.6), calls=%async_computation.1 | async-start | bytes 2097152 | tf_op jit(solution)/shard_map/all_to_all | solution.py:146
  96.4 36.1 %all-to-all-start.2 = ((bf16[128,64,128]{2,1,0:T(8,128)(2,1)}), bf16[128,64,128]{2,1,0:T(8,128)(2,1)S(1)}, u32[]{:S(2)}, u32[]{:S(2)}) async-start(bf16[128,64,128]{2,1,0:T(8,128)(2,1)} %bitcast.23), calls=%async_computation.2 | async-start | bytes 4194304 | tf_op jit(solution)/shard_map/all_to_all | solution.py:141

commit v10 on v9

--- a/solution.py
+++ b/solution.py
@@ -32,59 +32,76 @@
     return np.stack(tables)
 
 
-def match_kernel(index_ref, coef_ref, pix_ref, mask_ref, tab_ref, right_ref, out_ref):
+def match_kernel(index_ref, coef_ref, pix_ref, mask_ref, tab_ref, right_ref, meta_ref, out_ref):
     step = pl.program_id(0)
     group, side_len, _ = pix_ref.shape
-    bits = mask_ref[...]
-    masked = jnp.where((bits & 7) == 0, pix_ref[...], jnp.zeros((), jnp.bfloat16))
-    columns = jnp.dot(
-        masked.reshape(group * side_len, side_len),
-        right_ref[...],
-        preferred_element_type=jnp.float32,
-    ).astype(jnp.bfloat16)
-    for g in range(group):
-        chosen = jnp.minimum(jnp.maximum(index_ref[step * group + g], 0), coef_ref.shape[0] // 9 - 1)
-        base = chosen * 9
-        rows = columns[g * side_len:(g + 1) * side_len]
-        acc = jnp.zeros((side_len, side_len), jnp.float32)
-        for m in range(3):
-            even_band = tab_ref[2 * m]
-            odd_band = tab_ref[2 * m + 1]
-            left_a = (coef_ref[base + 3 * m] * even_band
-                      + coef_ref[base + 3 * m + 1] * odd_band).astype(jnp.bfloat16)
-            left_b = (coef_ref[base + 3 * m + 2] * even_band).astype(jnp.bfloat16)
-            acc = acc + jnp.dot(
-                left_a, rows[:, (2 * m) * side_len:(2 * m + 1) * side_len],
-                preferred_element_type=jnp.float32,
+    blocks = index_ref.shape[0]
+
+    @pl.when(step * group < blocks)
+    def _():
+        bits = mask_ref[...]
+        masked = jnp.where((bits & 7) == 0, pix_ref[...], jnp.zeros((), jnp.bfloat16))
+        columns = jnp.dot(
+            masked.reshape(group * side_len, side_len),
+            right_ref[...],
+            preferred_element_type=jnp.float32,
+        ).astype(jnp.bfloat16)
+        for g in range(group):
+            chosen = jnp.minimum(
+                jnp.maximum(index_ref[step * group + g], 0), coef_ref.shape[0] - 1
             )
-            acc = acc + jnp.dot(
-                left_b, rows[:, (2 * m + 1) * side_len:(2 * m + 2) * side_len],
-                preferred_element_type=jnp.float32,
-            )
-        out_ref[g] = acc.astype(jnp.bfloat16)
+            rows = columns[g * side_len:(g + 1) * side_len]
+            acc = jnp.zeros((side_len, side_len), jnp.float32)
+            for m in range(3):
+                even_band = tab_ref[2 * m]
+                odd_band = tab_ref[2 * m + 1]
+                left_a = (coef_ref[chosen, 3 * m] * even_band
+                          + coef_ref[chosen, 3 * m + 1] * odd_band).astype(jnp.bfloat16)
+                left_b = (coef_ref[chosen, 3 * m + 2] * even_band).astype(jnp.bfloat16)
+                acc = acc + jnp.dot(
+                    left_a, rows[:, (2 * m) * side_len:(2 * m + 1) * side_len],
+                    preferred_element_type=jnp.float32,
+                )
+                acc = acc + jnp.dot(
+                    left_b, rows[:, (2 * m + 1) * side_len:(2 * m + 2) * side_len],
+                    preferred_element_type=jnp.float32,
+                )
+            out_ref[g] = acc.astype(jnp.bfloat16)
+
+    @pl.when(step * group >= blocks)
+    def _():
+        for g in range(group):
+            line = meta_ref[g:g + 1, :].astype(jnp.bfloat16)
+            out_ref[g] = jnp.broadcast_to(line, (side_len, side_len))
 
 
-def match_blocks(pixels, mask_bits, coef_index, coef_table, tables, right_bands):
+def match_blocks(pixels, mask_bits, coef_index, coef_table, tables, right_bands, meta):
     number, side_len, _ = pixels.shape
     steps = number // GROUP
+    extra = meta.shape[0] // GROUP
     flops = number * 4 * side_len * side_len * 6 * side_len
+
+    def block_at(i):
+        return (jnp.minimum(i, steps - 1), 0, 0)
+
     return pl.pallas_call(
         match_kernel,
-        out_shape=jax.ShapeDtypeStruct(pixels.shape, jnp.bfloat16),
-        grid=(steps,),
+        out_shape=jax.ShapeDtypeStruct((number + meta.shape[0], side_len, side_len), jnp.bfloat16),
+        grid=(steps + extra,),
         in_specs=[
             pl.BlockSpec(memory_space=pltpu.SMEM),
             pl.BlockSpec(memory_space=pltpu.SMEM),
-            pl.BlockSpec((GROUP, side_len, side_len), lambda i: (i, 0, 0)),
-            pl.BlockSpec((GROUP, side_len, side_len), lambda i: (i, 0, 0)),
+            pl.BlockSpec((GROUP, side_len, side_len), block_at),
+            pl.BlockSpec((GROUP, side_len, side_len), block_at),
             pl.BlockSpec(tables.shape, lambda i: (0, 0, 0)),
             pl.BlockSpec(right_bands.shape, lambda i: (0, 0)),
+            pl.BlockSpec((GROUP, side_len), lambda i: (jnp.maximum(i - steps, 0), 0)),
         ],
         out_specs=pl.BlockSpec((GROUP, side_len, side_len), lambda i: (i, 0, 0)),
         cost_estimate=pl.CostEstimate(
             flops=flops, transcendentals=0, bytes_accessed=number * side_len * side_len * 8
         ),
-    )(coef_index, coef_table.reshape(-1), pixels, mask_bits, tables, right_bands)
+    )(coef_index, coef_table, pixels, mask_bits, tables, right_bands, meta)
 
 
 def shards(pixels, mask_bits, inv_var, owner, cell, coef_index, coef_table):
@@ -101,16 +118,17 @@
         np.transpose(tables, (2, 0, 1)).reshape(side_len, 6 * side_len), jnp.bfloat16
     )
     tables = jnp.asarray(tables)
-    matched_home = match_blocks(pixels, mask_bits, coef_index, coef_table, tables, right_bands)
     meta = jnp.stack([
-        inv_var,
+        inv_var.astype(jnp.bfloat16).astype(jnp.float32),
         owner.astype(jnp.float32),
         cell.astype(jnp.float32),
         jnp.zeros_like(inv_var),
-    ]).astype(jnp.bfloat16).reshape(2, 2 * blocks_here)
+    ]).reshape(2, 2 * blocks_here)
     meta = jnp.pad(meta, ((0, 14), (0, side_len - 2 * blocks_here)))
-    meta_blocks = jnp.broadcast_to(meta[:, None, :], (16, side_len, side_len))
-    payload = jnp.transpose(jnp.concatenate([matched_home, meta_blocks], axis=0), (1, 0, 2))
+    matched_home = match_blocks(
+        pixels, mask_bits, coef_index, coef_table, tables, right_bands, meta
+    )
+    payload = jnp.transpose(matched_home, (1, 0, 2))
     received = lax.all_to_all(payload, both, split_axis=0, concat_axis=0, tiled=True)
     row_all = received[:, :blocks_here].reshape(devices * blocks_here, side_len)
     weight_all = received[:, blocks_here, :blocks_here].reshape(-1)

time: 138 us -> 139 us (level)
  local copies, waits for them, and re-layouts: 8.49 us -> 10.6 us
  other arithmetic: 3.75 us -> 1.92 us
    transpose x1 -> x0, other arithmetic: 1.82 us -> none  [shards(): jnp.transpose(jnp.concatenate([matched_home, meta_blocks], axis=0), (1, 0...]
    transpose x1, local copies, waits for them, and re-layouts: 1.69 us -> 3.43 us  [shards(): payload = jnp.transpose(matched_home, (1, 0, 2))]
where the time goes in v10:
time: 139 us; the launch traced here: 136 us
  blocking collectives  45.4 us (33%)
  waiting for transfers between devices  29.5 us (21%)
  matrix products  24.8 us (18%)
  Pallas kernels  11.8 us (8%)
  starting transfers between devices  11.7 us (8%)
  local copies, waits for them, and re-layouts  10.6 us (8%)
  other arithmetic  1.92 us (1%)
    all_to_all x1, blocking collectives, shards(): lax.all_to_all(payload, both, split_axis=0, concat_axis=0, tiled=True)  45.4 us
    all_to_all x1, waiting for transfers between devices, shards(): lax.all_to_all(difference_row.reshape(devices, blocks_here, side_len), bo...  28.2 us
    dot_general x1, matrix products, shards(): jnp.dot(block_pick, template_row, preferred_element_type=jnp.float32)  14.3 us
    pallas_call x1, Pallas kernels, match_blocks(): pl.pallas_call(match_kernel, out_shape=jax.ShapeDtypeStruct((number + met...  11.8 us
    dot_general x1, matrix products, shards(): numerator = jnp.dot(weighted, row_all, preferred_element_type=jnp.float32)  10.1 us
    all_to_all x1, starting transfers between devices, shards(): lax.all_to_all(difference_row.reshape(devices, blocks_here, side_len), bo...  6.3 us
    unnamed x5, local copies, waits for them, and re-layouts  5.66 us
    all_to_all x1, starting transfers between devices, shards(): lax.all_to_all(coadd_row.reshape(patches, CELLS, 1, side_len), 'patch', s...  5.39 us
  transfers between devices with their start and end apart: 2, of which 2 were waited for; matrix products, arithmetic and copies ran while one was open for 12% of the time, Pallas kernels for 0%

profile of v10, /device:TPU:32, one launch (start us, length us, event | category | flops | bytes accessed | tf_op | source)
XLA Modules:
  0.0 136.5 jit_solution(5476563036236163225)
XLA Ops:
  0.6 0.7 bitcast_convert_fusion
  1.3 0.1 pad.8.clone
  1.4 0.7 convert_bitcast_fusion
  2.1 0.1 reshape.63
  2.2 0.6 pad.4.meta_ref
  2.8 1.4 %copy.18.coef_ref = f32[64,9]{1,0:T(8,128)} copy(f32[64,9]{0,1:T(8,128)} %param.15) | data formatting | bytes 4608 | tf_op args[6]
  4.2 11.8 %shard_map.104 = bf16[80,128,128]{2,1,0:T(8,128)(2,1)} custom-call(s32[64]{0:T(128)} %index_ref.1, f32[64,9]{1,0:T(8,128)} %copy.18.coef_ref, bf16[64,128,128]{2,1,0:T(8,128)(2,1)} %pix_ref.1, s32[64,128,128]{2,1,0:T(8,128)} %mask_ref.1, f32[6,128,128]{2,1,0:T(8,128)} %constant.15.clone.tab_ref, bf16[128,768]{1,0:T(8,128)(2,1)} %constant.14.clone.right_ref, ...), custom_call_target="tpu_custom_call" | custom-call | flops 3221225472 | bytes 8388608 | tf_op jit(solution)/shard_map/pallas_call | solution.py:87
  16.0 3.4 %copy.19 = bf16[128,80,128]{2,1,0:T(8,128)(2,1)S(1)} copy(bf16[128,80,128]{2,0,1:T(8,128)(2,1)} %bitcast.23) | data formatting | bytes 5242880 | tf_op jit(solution)/shard_map/transpose | solution.py:131
  19.4 45.4 %all_to_all.25 = bf16[128,80,128]{2,1,0:T(8,128)(2,1)S(1)} all-to-all(bf16[128,80,128]{2,1,0:T(8,128)(2,1)S(1)} %copy.19), channel_id=1, replica_groups=mesh['visit'=4,'patch'=32] {'visit','patch'}, dimensions={0} | all-to-all | bytes 5242880 | tf_op jit(solution)/shard_map/all_to_all | solution.py:132
  64.8 0.2 slice_reduce_fusion
  65.0 0.1 broadcast_in_dim.35
  65.1 0.5 fusion.21
  65.6 0.1 reshape.69
  65.7 0.1 reshape.70
  65.8 0.4 convolution_maximum_fusion
  66.2 0.3 slice.19
  66.6 10.1 %fusion.11 = f32[2048,128]{1,0:T(8,128)} fusion(bf16[8192,128]{1,0:T(8,128)(2,1)S(1)} %bitcast.25, s32[8192]{0:T(1024)S(1)} %multiply_add_fusion, bf16[8192]{0:T(1024)(128)(2,1)S(1)} %broadcast_in_dim.35, f32[2048]{0:T(1024)S(1)} %max.15), kind=kOutput, calls=%fused_computation.13 | convolution fusion | flops 4328783872 | bytes 3203072 | tf_op jit(solution)/shard_map/dot_general | solution.py:140
  76.6 5.4 %all-to-all-start.1 = ((f32[32,64,1,128]{3,1,2,0:T(8,128)}), f32[32,64,1,128]{3,1,2,0:T(8,128)S(1)}, u32[]{:S(2)}, u32[]{:S(2)}) async-start(f32[32,64,1,128]{3,1,2,0:T(8,128)} %bitcast.6), calls=%async_computation.1 | async-start | bytes 2097152 | tf_op jit(solution)/shard_map/all_to_all | solution.py:164
  82.0 14.3 %fusion.9 = bf16[8192,128]{1,0:T(8,128)(2,1)} fusion(s32[8192]{0:T(1024)S(1)} %multiply_add_fusion, bf16[8192,128]{1,0:T(8,128)(2,1)} %bitcast.26, f32[2048,128]{1,0:T(8,128)} %fusion.11), kind=kOutput, calls=%fused_computation.10 | convolution fusion | flops 4315152384 | bytes 5275648 | tf_op jit(solution)/shard_map/dot_general | solution.py:157
  96.4 1.3 all-to-all-done.1
  97.7 6.3 %all-to-all-start.2 = ((bf16[128,64,128]{2,1,0:T(8,128)(2,1)}), bf16[128,64,128]{2,1,0:T(8,128)(2,1)S(1)}, u32[]{:S(2)}, u32[]{:S(2)}) async-start(bf16[128,64,128]{2,1,0:T(8,128)(2,1)} %bitcast.24), calls=%async_computation.2 | async-start | bytes 4194304 | tf_op jit(solution)/shard_map/all_to_all | solution.py:159
  104.0 1.6 %copy.21 = f32[64,32,128]{2,1,0:T(8,128)} copy(f32[64,32,128]{2,0,1:T(8,128)S(1)} %bitcast.22) | data formatting | bytes 2097152
  105.6 28.2 %all-to-all-done.2 = bf16[128,64,128]{2,1,0:T(8,128)(2,1)S(1)} async-done(((bf16[128,64,128]{2,1,0:T(8,128)(2,1)}), bf16[128,64,128]{2,1,0:T(8,128)(2,1)S(1)}, u32[]{:S(2)}, u32[]{:S(2)}) %all-to-all-start.2) | async-done | bytes 2097184 | tf_op jit(solution)/shard_map/all_to_all | solution.py:159
  133.8 2.7 %copy.22 = bf16[64,128,128]{2,1,0:T(8,128)(2,1)} copy(bf16[64,128,128]{2,0,1:T(8,128)(2,1)S(1)} %bitcast.21) | data formatting | bytes 4194304
  (5 shorter events, 0.2 us)
Async XLA Ops:
  66.5 10.1 %copy-start = (bf16[128,64,128]{2,1,0:T(8,128)(2,1)}, bf16[128,64,128]{2,1,0:T(8,128)(2,1)S(1)}, u32[]{:S(2)}) copy-start(bf16[128,64,128]{2,1,0:T(8,128)(2,1)S(1)} %slice.19) | copy-start | bytes 6291460
  76.6 21.1 %all-to-all-start.1 = ((f32[32,64,1,128]{3,1,2,0:T(8,128)}), f32[32,64,1,128]{3,1,2,0:T(8,128)S(1)}, u32[]{:S(2)}, u32[]{:S(2)}) async-start(f32[32,64,1,128]{3,1,2,0:T(8,128)} %bitcast.6), calls=%async_computation.1 | async-start | bytes 2097152 | tf_op jit(solution)/shard_map/all_to_all | solution.py:164
  97.7 36.1 %all-to-all-start.2 = ((bf16[128,64,128]{2,1,0:T(8,128)(2,1)}), bf16[128,64,128]{2,1,0:T(8,128)(2,1)S(1)}, u32[]{:S(2)}, u32[]{:S(2)}) async-start(bf16[128,64,128]{2,1,0:T(8,128)(2,1)} %bitcast.24), calls=%async_computation.2 | async-start | bytes 4194304 | tf_op jit(solution)/shard_map/all_to_all | solution.py:159

commit v11 on v9

--- a/solution.py
+++ b/solution.py
@@ -133,10 +133,10 @@
     ).reshape(segments)
     coadd_row = numerator / jnp.maximum(weight_sum, 1.0)[:, None]
     template_row = coadd_row.astype(jnp.bfloat16)
-    block_pick = (
-        segment_all[:, None] == jnp.arange(segments, dtype=jnp.int32)[None, :]
-    ).astype(jnp.bfloat16)
-    block_template = jnp.dot(block_pick, template_row, preferred_element_type=jnp.float32)
+    block_template = lax.dot_general(
+        picks.astype(jnp.bfloat16), template_row, (((0,), (0,)), ((), ())),
+        preferred_element_type=jnp.float32,
+    )
     difference_row = (row_all.astype(jnp.float32) - block_template).astype(jnp.bfloat16)
     returned = lax.all_to_all(
         difference_row.reshape(devices, blocks_here, side_len),

time: 138 us -> 144 us (1.043)
  matrix products: 24.8 us -> 31.3 us
    dot_general x1, matrix products: 14.3 us -> 20.8 us  [shards(): lax.dot_general(picks.astype(jnp.bfloat16), template_row, (((0,), (0,)),...]
  transfers between devices with their start and end apart: 2 -> 2, of which waited for: 2 -> 1; matrix products, arithmetic and copies ran while one was open for 12% -> 16% of each run, Pallas kernels for 0% -> 0%
where the time goes in v11:
time: 144 us; the launch traced here: 142 us
  blocking collectives  45.4 us (32%)
  matrix products  31.3 us (22%)
  waiting for transfers between devices  28.2 us (20%)
  starting transfers between devices  13 us (9%)
  Pallas kernels  10.8 us (8%)
  local copies, waits for them, and re-layouts  8.49 us (6%)
  other arithmetic  3.75 us (3%)
    all_to_all x1, blocking collectives, shards(): lax.all_to_all(payload, both, split_axis=0, concat_axis=0, tiled=True)  45.4 us
    all_to_all x1, waiting for transfers between devices, shards(): lax.all_to_all(difference_row.reshape(devices, blocks_here, side_len), bo...  28.2 us
    dot_general x1, matrix products, shards(): lax.dot_general(picks.astype(jnp.bfloat16), template_row, (((0,), (0,)),...  20.8 us
    pallas_call x1, Pallas kernels, match_blocks(): pl.pallas_call(match_kernel, out_shape=jax.ShapeDtypeStruct(pixels.shape,...  10.8 us
    dot_general x1, matrix products, shards(): numerator = jnp.dot(weighted, row_all, preferred_element_type=jnp.float32)  10.1 us
    all_to_all x1, starting transfers between devices, shards(): lax.all_to_all(difference_row.reshape(devices, blocks_here, side_len), bo...  7.63 us
    all_to_all x1, starting transfers between devices, shards(): lax.all_to_all(coadd_row.reshape(patches, CELLS, 1, side_len), 'patch', s...  5.4 us
    unnamed x5, local copies, waits for them, and re-layouts  5.04 us
  transfers between devices with their start and end apart: 2, of which 1 were waited for; matrix products, arithmetic and copies ran while one was open for 16% of the time, Pallas kernels for 0%

profile of v11, /device:TPU:32, one launch (start us, length us, event | category | flops | bytes accessed | tf_op | source)
XLA Modules:
  0.0 141.7 jit_solution(2176667717227781835)
XLA Ops:
  0.6 0.7 convert_bitcast_fusion.2
  1.3 0.1 pad.10.clone
  1.4 0.7 convert_bitcast_fusion
  2.1 0.1 convert_element_type.52
  2.2 0.8 copy.17
  3.0 0.7 reshape.55.coef_ref
  3.7 10.8 %shard_map.104 = bf16[64,128,128]{2,1,0:T(8,128)(2,1)} custom-call(s32[64]{0:T(128)} %index_ref.1, f32[576]{0:T(1024)} %reshape.55.coef_ref, bf16[64,128,128]{2,1,0:T(8,128)(2,1)} %pix_ref.1, s32[64,128,128]{2,1,0:T(8,128)} %mask_ref.1, f32[6,128,128]{2,1,0:T(8,128)} %constant.15.clone.tab_ref, bf16[128,768]{1,0:T(8,128)(2,1)} %constant.14.clone.right_ref), custom_call_target="tpu_custom_call" | custom-call | flops 3221225472 | bytes 8388608 | tf_op jit(solution)/shard_map/pallas_call | solution.py:71
  14.6 1.8 %maximum_bitcast_fusion = bf16[128,80,128]{2,0,1:T(8,128)(2,1)S(1)} fusion(bf16[16,128,128]{2,1,0:T(8,128)(2,1)S(1)} %broadcast_in_dim.39, bf16[64,128,128]{2,1,0:T(8,128)(2,1)} %shard_map.104), kind=kLoop, calls=%fused_computation.10 | loop fusion | flops 1310720 | bytes 5242880 | tf_op jit(solution)/shard_map/transpose | solution.py:113
  16.4 1.7 %copy.18 = bf16[128,80,128]{2,1,0:T(8,128)(2,1)S(1)} copy(bf16[128,80,128]{2,0,1:T(8,128)(2,1)S(1)} %maximum_bitcast_fusion) | data formatting | bytes 5242880 | tf_op jit(solution)/shard_map/transpose | solution.py:113
  18.1 45.4 %all_to_all.25 = bf16[128,80,128]{2,1,0:T(8,128)(2,1)S(1)} all-to-all(bf16[128,80,128]{2,1,0:T(8,128)(2,1)S(1)} %copy.18), channel_id=1, replica_groups=mesh['visit'=4,'patch'=32] {'visit','patch'}, dimensions={0} | all-to-all | bytes 5242880 | tf_op jit(solution)/shard_map/all_to_all | solution.py:114
  63.5 0.2 slice_reduce_fusion
  63.7 0.1 broadcast_in_dim.40
  63.8 0.5 fusion.21
  64.3 0.1 reshape.60
  64.4 0.1 reshape.61
  64.5 0.4 convolution_maximum_fusion
  64.9 0.3 slice.19
  65.3 10.1 %fusion.11 = f32[2048,128]{1,0:T(8,128)} fusion(bf16[8192,128]{1,0:T(8,128)(2,1)S(1)} %bitcast.24, s32[8192]{0:T(1024)S(1)} %multiply_add_fusion, bf16[8192]{0:T(1024)(128)(2,1)S(1)} %broadcast_in_dim.40, f32[2048]{0:T(1024)S(1)} %max.15), kind=kOutput, calls=%fused_computation.13 | convolution fusion | flops 4328783872 | bytes 3203072 | tf_op jit(solution)/shard_map/dot_general | solution.py:122
  75.3 5.4 %all-to-all-start.1 = ((f32[32,64,1,128]{3,1,2,0:T(8,128)}), f32[32,64,1,128]{3,1,2,0:T(8,128)S(1)}, u32[]{:S(2)}, u32[]{:S(2)}) async-start(f32[32,64,1,128]{3,1,2,0:T(8,128)} %bitcast.6), calls=%async_computation.1 | async-start | bytes 2097152 | tf_op jit(solution)/shard_map/all_to_all | solution.py:146
  80.7 20.8 %fusion.9 = bf16[8192,128]{1,0:T(8,128)(2,1)} fusion(s32[8192]{0:T(1024)S(1)} %multiply_add_fusion, bf16[8192,128]{1,0:T(8,128)(2,1)} %bitcast.25, f32[2048,128]{1,0:T(8,128)} %fusion.11), kind=kOutput, calls=%fused_computation.9 | convolution fusion | flops 4315152384 | bytes 5275648 | tf_op jit(solution)/shard_map/dot_general | solution.py:136
  101.6 7.6 %all-to-all-start.2 = ((bf16[128,64,128]{2,1,0:T(8,128)(2,1)}), bf16[128,64,128]{2,1,0:T(8,128)(2,1)S(1)}, u32[]{:S(2)}, u32[]{:S(2)}) async-start(bf16[128,64,128]{2,1,0:T(8,128)(2,1)} %bitcast.23), calls=%async_computation.2 | async-start | bytes 4194304 | tf_op jit(solution)/shard_map/all_to_all | solution.py:141
  109.2 1.6 %copy.20 = f32[64,32,128]{2,1,0:T(8,128)} copy(f32[64,32,128]{2,0,1:T(8,128)S(1)} %bitcast.22) | data formatting | bytes 2097152
  110.8 28.2 %all-to-all-done.2 = bf16[128,64,128]{2,1,0:T(8,128)(2,1)S(1)} async-done(((bf16[128,64,128]{2,1,0:T(8,128)(2,1)}), bf16[128,64,128]{2,1,0:T(8,128)(2,1)S(1)}, u32[]{:S(2)}, u32[]{:S(2)}) %all-to-all-start.2) | async-done | bytes 2097184 | tf_op jit(solution)/shard_map/all_to_all | solution.py:141
  139.0 2.7 %copy.21 = bf16[64,128,128]{2,1,0:T(8,128)(2,1)} copy(bf16[64,128,128]{2,0,1:T(8,128)(2,1)S(1)} %bitcast.21) | data formatting | bytes 4194304
  (8 shorter events, 0.2 us)
Async XLA Ops:
  65.2 10.1 %copy-start = (bf16[128,64,128]{2,1,0:T(8,128)(2,1)}, bf16[128,64,128]{2,1,0:T(8,128)(2,1)S(1)}, u32[]{:S(2)}) copy-start(bf16[128,64,128]{2,1,0:T(8,128)(2,1)S(1)} %slice.19) | copy-start | bytes 6291460
  75.3 26.3 %all-to-all-start.1 = ((f32[32,64,1,128]{3,1,2,0:T(8,128)}), f32[32,64,1,128]{3,1,2,0:T(8,128)S(1)}, u32[]{:S(2)}, u32[]{:S(2)}) async-start(f32[32,64,1,128]{3,1,2,0:T(8,128)} %bitcast.6), calls=%async_computation.1 | async-start | bytes 2097152 | tf_op jit(solution)/shard_map/all_to_all | solution.py:146
  101.6 37.4 %all-to-all-start.2 = ((bf16[128,64,128]{2,1,0:T(8,128)(2,1)}), bf16[128,64,128]{2,1,0:T(8,128)(2,1)S(1)}, u32[]{:S(2)}, u32[]{:S(2)}) async-start(bf16[128,64,128]{2,1,0:T(8,128)(2,1)} %bitcast.23), calls=%async_computation.2 | async-start | bytes 4194304 | tf_op jit(solution)/shard_map/all_to_all | solution.py:141

commit v12 on v9

--- a/solution.py
+++ b/solution.py
@@ -8,7 +8,7 @@
 
 CELLS = 64
 KSIZE = 21
-GROUP = 8
+GROUP = 16
 
 
 gauss_widths = (1.0, 2.0, 3.5)

time: 138 us -> 137 us (level)
  no operation moved by 1% of the time
where the time goes in v12:
time: 137 us; the launch traced here: 135 us
  blocking collectives  45.4 us (33%)
  waiting for transfers between devices  29.5 us (22%)
  matrix products  24.8 us (18%)
  starting transfers between devices  11.7 us (9%)
  Pallas kernels  10.2 us (7%)
  local copies, waits for them, and re-layouts  8.49 us (6%)
  other arithmetic  3.75 us (3%)
    all_to_all x1, blocking collectives, shards(): lax.all_to_all(payload, both, split_axis=0, concat_axis=0, tiled=True)  45.4 us
    all_to_all x1, waiting for transfers between devices, shards(): lax.all_to_all(difference_row.reshape(devices, blocks_here, side_len), bo...  28.2 us
    dot_general x1, matrix products, shards(): jnp.dot(block_pick, template_row, preferred_element_type=jnp.float32)  14.3 us
    pallas_call x1, Pallas kernels, match_blocks(): pl.pallas_call(match_kernel, out_shape=jax.ShapeDtypeStruct(pixels.shape,...  10.2 us
    dot_general x1, matrix products, shards(): numerator = jnp.dot(weighted, row_all, preferred_element_type=jnp.float32)  10.1 us
    all_to_all x1, starting transfers between devices, shards(): lax.all_to_all(difference_row.reshape(devices, blocks_here, side_len), bo...  6.3 us
    all_to_all x1, starting transfers between devices, shards(): lax.all_to_all(coadd_row.reshape(patches, CELLS, 1, side_len), 'patch', s...  5.39 us
    unnamed x5, local copies, waits for them, and re-layouts  5.04 us
  transfers between devices with their start and end apart: 2, of which 2 were waited for; matrix products, arithmetic and copies ran while one was open for 12% of the time, Pallas kernels for 0%

profile of v12, /device:TPU:32, one launch (start us, length us, event | category | flops | bytes accessed | tf_op | source)
XLA Modules:
  0.0 134.6 jit_solution(7722003230016443436)
XLA Ops:
  0.6 0.7 convert_bitcast_fusion.2
  1.3 0.1 pad.10.clone
  1.4 0.7 convert_bitcast_fusion
  2.1 0.1 convert_element_type.60
  2.2 0.8 copy.17
  3.0 0.7 reshape.67.coef_ref
  3.7 10.2 %shard_map.104 = bf16[64,128,128]{2,1,0:T(8,128)(2,1)} custom-call(s32[64]{0:T(128)} %index_ref.1, f32[576]{0:T(1024)} %reshape.67.coef_ref, bf16[64,128,128]{2,1,0:T(8,128)(2,1)} %pix_ref.1, s32[64,128,128]{2,1,0:T(8,128)} %mask_ref.1, f32[6,128,128]{2,1,0:T(8,128)} %constant.15.clone.tab_ref, bf16[128,768]{1,0:T(8,128)(2,1)} %constant.14.clone.right_ref), custom_call_target="tpu_custom_call" | custom-call | flops 3221225472 | bytes 8388608 | tf_op jit(solution)/shard_map/pallas_call | solution.py:71
  14.0 1.8 %maximum_bitcast_fusion = bf16[128,80,128]{2,0,1:T(8,128)(2,1)S(1)} fusion(bf16[16,128,128]{2,1,0:T(8,128)(2,1)S(1)} %broadcast_in_dim.28, bf16[64,128,128]{2,1,0:T(8,128)(2,1)} %shard_map.104), kind=kLoop, calls=%fused_computation.11 | loop fusion | flops 1310720 | bytes 5242880 | tf_op jit(solution)/shard_map/transpose | solution.py:113
  15.8 1.7 %copy.18 = bf16[128,80,128]{2,1,0:T(8,128)(2,1)S(1)} copy(bf16[128,80,128]{2,0,1:T(8,128)(2,1)S(1)} %maximum_bitcast_fusion) | data formatting | bytes 5242880 | tf_op jit(solution)/shard_map/transpose | solution.py:113
  17.5 45.4 %all_to_all.25 = bf16[128,80,128]{2,1,0:T(8,128)(2,1)S(1)} all-to-all(bf16[128,80,128]{2,1,0:T(8,128)(2,1)S(1)} %copy.18), channel_id=1, replica_groups=mesh['visit'=4,'patch'=32] {'visit','patch'}, dimensions={0} | all-to-all | bytes 5242880 | tf_op jit(solution)/shard_map/all_to_all | solution.py:114
  62.9 0.2 slice_reduce_fusion
  63.1 0.1 broadcast_in_dim.42
  63.2 0.5 fusion.21
  63.7 0.1 reshape.72
  63.9 0.4 convolution_maximum_fusion
  64.4 0.3 slice.19
  64.7 10.1 %fusion.11 = f32[2048,128]{1,0:T(8,128)} fusion(bf16[8192,128]{1,0:T(8,128)(2,1)S(1)} %bitcast.24, s32[8192]{0:T(1024)S(1)} %multiply_add_fusion, bf16[8192]{0:T(1024)(128)(2,1)S(1)} %broadcast_in_dim.42, f32[2048]{0:T(1024)S(1)} %max.15), kind=kOutput, calls=%fused_computation.14 | convolution fusion | flops 4328783872 | bytes 3203072 | tf_op jit(solution)/shard_map/dot_general | solution.py:122
  74.8 5.4 %all-to-all-start.1 = ((f32[32,64,1,128]{3,1,2,0:T(8,128)}), f32[32,64,1,128]{3,1,2,0:T(8,128)S(1)}, u32[]{:S(2)}, u32[]{:S(2)}) async-start(f32[32,64,1,128]{3,1,2,0:T(8,128)} %bitcast.6), calls=%async_computation.1 | async-start | bytes 2097152 | tf_op jit(solution)/shard_map/all_to_all | solution.py:146
  80.2 14.3 %fusion.9 = bf16[8192,128]{1,0:T(8,128)(2,1)} fusion(s32[8192]{0:T(1024)S(1)} %multiply_add_fusion, bf16[8192,128]{1,0:T(8,128)(2,1)} %bitcast.25, f32[2048,128]{1,0:T(8,128)} %fusion.11), kind=kOutput, calls=%fused_computation.10 | convolution fusion | flops 4315152384 | bytes 5275648 | tf_op jit(solution)/shard_map/dot_general | solution.py:139
  94.5 1.3 all-to-all-done.1
  95.8 6.3 %all-to-all-start.2 = ((bf16[128,64,128]{2,1,0:T(8,128)(2,1)}), bf16[128,64,128]{2,1,0:T(8,128)(2,1)S(1)}, u32[]{:S(2)}, u32[]{:S(2)}) async-start(bf16[128,64,128]{2,1,0:T(8,128)(2,1)} %bitcast.23), calls=%async_computation.2 | async-start | bytes 4194304 | tf_op jit(solution)/shard_map/all_to_all | solution.py:141
  102.1 1.6 %copy.20 = f32[64,32,128]{2,1,0:T(8,128)} copy(f32[64,32,128]{2,0,1:T(8,128)S(1)} %bitcast.22) | data formatting | bytes 2097152
  103.7 28.2 %all-to-all-done.2 = bf16[128,64,128]{2,1,0:T(8,128)(2,1)S(1)} async-done(((bf16[128,64,128]{2,1,0:T(8,128)(2,1)}), bf16[128,64,128]{2,1,0:T(8,128)(2,1)S(1)}, u32[]{:S(2)}, u32[]{:S(2)}) %all-to-all-start.2) | async-done | bytes 2097184 | tf_op jit(solution)/shard_map/all_to_all | solution.py:141
  131.9 2.7 %copy.21 = bf16[64,128,128]{2,1,0:T(8,128)(2,1)} copy(bf16[64,128,128]{2,0,1:T(8,128)(2,1)S(1)} %bitcast.21) | data formatting | bytes 4194304
  (8 shorter events, 0.3 us)
Async XLA Ops:
  64.7 10.1 %copy-start = (bf16[128,64,128]{2,1,0:T(8,128)(2,1)}, bf16[128,64,128]{2,1,0:T(8,128)(2,1)S(1)}, u32[]{:S(2)}) copy-start(bf16[128,64,128]{2,1,0:T(8,128)(2,1)S(1)} %slice.19) | copy-start | bytes 6291460
  74.8 21.1 %all-to-all-start.1 = ((f32[32,64,1,128]{3,1,2,0:T(8,128)}), f32[32,64,1,128]{3,1,2,0:T(8,128)S(1)}, u32[]{:S(2)}, u32[]{:S(2)}) async-start(f32[32,64,1,128]{3,1,2,0:T(8,128)} %bitcast.6), calls=%async_computation.1 | async-start | bytes 2097152 | tf_op jit(solution)/shard_map/all_to_all | solution.py:146
  95.8 36.1 %all-to-all-start.2 = ((bf16[128,64,128]{2,1,0:T(8,128)(2,1)}), bf16[128,64,128]{2,1,0:T(8,128)(2,1)S(1)}, u32[]{:S(2)}, u32[]{:S(2)}) async-start(bf16[128,64,128]{2,1,0:T(8,128)(2,1)} %bitcast.23), calls=%async_computation.2 | async-start | bytes 4194304 | tf_op jit(solution)/shard_map/all_to_all | solution.py:141

commit v13 on v12

--- a/solution.py
+++ b/solution.py
@@ -36,7 +36,9 @@
     step = pl.program_id(0)
     group, side_len, _ = pix_ref.shape
     bits = mask_ref[...]
-    masked = jnp.where((bits & 7) == 0, pix_ref[...], jnp.zeros((), jnp.bfloat16))
+    masked = jnp.where(
+        (bits & 7) == 0, pix_ref[...].astype(jnp.float32), jnp.zeros((), jnp.float32)
+    ).astype(jnp.bfloat16)
     columns = jnp.dot(
         masked.reshape(group * side_len, side_len),
         right_ref[...],

time: 137 us -> 137 us (level)
  no operation moved by 1% of the time
where the time goes in v13:
time: 137 us; the launch traced here: 135 us
  blocking collectives  45.4 us (33%)
  waiting for transfers between devices  29.5 us (22%)
  matrix products  24.8 us (18%)
  starting transfers between devices  11.7 us (9%)
  Pallas kernels  10.2 us (7%)
  local copies, waits for them, and re-layouts  8.49 us (6%)
  other arithmetic  3.75 us (3%)
    all_to_all x1, blocking collectives, shards(): lax.all_to_all(payload, both, split_axis=0, concat_axis=0, tiled=True)  45.4 us
    all_to_all x1, waiting for transfers between devices, shards(): lax.all_to_all(difference_row.reshape(devices, blocks_here, side_len), bo...  28.2 us
    dot_general x1, matrix products, shards(): jnp.dot(block_pick, template_row, preferred_element_type=jnp.float32)  14.3 us
    pallas_call x1, Pallas kernels, match_blocks(): pl.pallas_call(match_kernel, out_shape=jax.ShapeDtypeStruct(pixels.shape,...  10.2 us
    dot_general x1, matrix products, shards(): numerator = jnp.dot(weighted, row_all, preferred_element_type=jnp.float32)  10.1 us
    all_to_all x1, starting transfers between devices, shards(): lax.all_to_all(difference_row.reshape(devices, blocks_here, side_len), bo...  6.31 us
    all_to_all x1, starting transfers between devices, shards(): lax.all_to_all(coadd_row.reshape(patches, CELLS, 1, side_len), 'patch', s...  5.39 us
    unnamed x5, local copies, waits for them, and re-layouts  5.04 us
  transfers between devices with their start and end apart: 2, of which 2 were waited for; matrix products, arithmetic and copies ran while one was open for 12% of the time, Pallas kernels for 0%

profile of v13, /device:TPU:32, one launch (start us, length us, event | category | flops | bytes accessed | tf_op | source)
XLA Modules:
  0.0 134.6 jit_solution(10519922096945426690)
XLA Ops:
  0.6 0.7 convert_bitcast_fusion.2
  1.3 0.1 pad.10.clone
  1.4 0.7 convert_bitcast_fusion
  2.1 0.1 convert_element_type.60
  2.2 0.8 copy.17
  3.0 0.7 reshape.67.coef_ref
  3.7 10.2 %shard_map.104 = bf16[64,128,128]{2,1,0:T(8,128)(2,1)} custom-call(s32[64]{0:T(128)} %index_ref.1, f32[576]{0:T(1024)} %reshape.67.coef_ref, bf16[64,128,128]{2,1,0:T(8,128)(2,1)} %pix_ref.1, s32[64,128,128]{2,1,0:T(8,128)} %mask_ref.1, f32[6,128,128]{2,1,0:T(8,128)} %constant.15.clone.tab_ref, bf16[128,768]{1,0:T(8,128)(2,1)} %constant.14.clone.right_ref), custom_call_target="tpu_custom_call" | custom-call | flops 3221225472 | bytes 8388608 | tf_op jit(solution)/shard_map/pallas_call | solution.py:73
  14.0 1.8 %maximum_bitcast_fusion = bf16[128,80,128]{2,0,1:T(8,128)(2,1)S(1)} fusion(bf16[16,128,128]{2,1,0:T(8,128)(2,1)S(1)} %broadcast_in_dim.28, bf16[64,128,128]{2,1,0:T(8,128)(2,1)} %shard_map.104), kind=kLoop, calls=%fused_computation.11 | loop fusion | flops 1310720 | bytes 5242880 | tf_op jit(solution)/shard_map/transpose | solution.py:115
  15.8 1.7 %copy.18 = bf16[128,80,128]{2,1,0:T(8,128)(2,1)S(1)} copy(bf16[128,80,128]{2,0,1:T(8,128)(2,1)S(1)} %maximum_bitcast_fusion) | data formatting | bytes 5242880 | tf_op jit(solution)/shard_map/transpose | solution.py:115
  17.5 45.4 %all_to_all.25 = bf16[128,80,128]{2,1,0:T(8,128)(2,1)S(1)} all-to-all(bf16[128,80,128]{2,1,0:T(8,128)(2,1)S(1)} %copy.18), channel_id=1, replica_groups=mesh['visit'=4,'patch'=32] {'visit','patch'}, dimensions={0} | all-to-all | bytes 5242880 | tf_op jit(solution)/shard_map/all_to_all | solution.py:116
  62.9 0.2 slice_reduce_fusion
  63.1 0.1 broadcast_in_dim.42
  63.2 0.5 fusion.21
  63.7 0.1 reshape.72
  63.9 0.4 convolution_maximum_fusion
  64.4 0.3 slice.19
  64.7 10.1 %fusion.11 = f32[2048,128]{1,0:T(8,128)} fusion(bf16[8192,128]{1,0:T(8,128)(2,1)S(1)} %bitcast.24, s32[8192]{0:T(1024)S(1)} %multiply_add_fusion, bf16[8192]{0:T(1024)(128)(2,1)S(1)} %broadcast_in_dim.42, f32[2048]{0:T(1024)S(1)} %max.15), kind=kOutput, calls=%fused_computation.14 | convolution fusion | flops 4328783872 | bytes 3203072 | tf_op jit(solution)/shard_map/dot_general | solution.py:124
  74.8 5.4 %all-to-all-start.1 = ((f32[32,64,1,128]{3,1,2,0:T(8,128)}), f32[32,64,1,128]{3,1,2,0:T(8,128)S(1)}, u32[]{:S(2)}, u32[]{:S(2)}) async-start(f32[32,64,1,128]{3,1,2,0:T(8,128)} %bitcast.6), calls=%async_computation.1 | async-start | bytes 2097152 | tf_op jit(solution)/shard_map/all_to_all | solution.py:148
  80.2 14.3 %fusion.9 = bf16[8192,128]{1,0:T(8,128)(2,1)} fusion(s32[8192]{0:T(1024)S(1)} %multiply_add_fusion, bf16[8192,128]{1,0:T(8,128)(2,1)} %bitcast.25, f32[2048,128]{1,0:T(8,128)} %fusion.11), kind=kOutput, calls=%fused_computation.10 | convolution fusion | flops 4315152384 | bytes 5275648 | tf_op jit(solution)/shard_map/dot_general | solution.py:141
  94.5 1.3 all-to-all-done.1
  95.8 6.3 %all-to-all-start.2 = ((bf16[128,64,128]{2,1,0:T(8,128)(2,1)}), bf16[128,64,128]{2,1,0:T(8,128)(2,1)S(1)}, u32[]{:S(2)}, u32[]{:S(2)}) async-start(bf16[128,64,128]{2,1,0:T(8,128)(2,1)} %bitcast.23), calls=%async_computation.2 | async-start | bytes 4194304 | tf_op jit(solution)/shard_map/all_to_all | solution.py:143
  102.1 1.6 %copy.20 = f32[64,32,128]{2,1,0:T(8,128)} copy(f32[64,32,128]{2,0,1:T(8,128)S(1)} %bitcast.22) | data formatting | bytes 2097152
  103.7 28.2 %all-to-all-done.2 = bf16[128,64,128]{2,1,0:T(8,128)(2,1)S(1)} async-done(((bf16[128,64,128]{2,1,0:T(8,128)(2,1)}), bf16[128,64,128]{2,1,0:T(8,128)(2,1)S(1)}, u32[]{:S(2)}, u32[]{:S(2)}) %all-to-all-start.2) | async-done | bytes 2097184 | tf_op jit(solution)/shard_map/all_to_all | solution.py:143
  131.9 2.7 %copy.21 = bf16[64,128,128]{2,1,0:T(8,128)(2,1)} copy(bf16[64,128,128]{2,0,1:T(8,128)(2,1)S(1)} %bitcast.21) | data formatting | bytes 4194304
  (8 shorter events, 0.3 us)
Async XLA Ops:
  64.7 10.1 %copy-start = (bf16[128,64,128]{2,1,0:T(8,128)(2,1)}, bf16[128,64,128]{2,1,0:T(8,128)(2,1)S(1)}, u32[]{:S(2)}) copy-start(bf16[128,64,128]{2,1,0:T(8,128)(2,1)S(1)} %slice.19) | copy-start | bytes 6291460
  74.8 21.1 %all-to-all-start.1 = ((f32[32,64,1,128]{3,1,2,0:T(8,128)}), f32[32,64,1,128]{3,1,2,0:T(8,128)S(1)}, u32[]{:S(2)}, u32[]{:S(2)}) async-start(f32[32,64,1,128]{3,1,2,0:T(8,128)} %bitcast.6), calls=%async_computation.1 | async-start | bytes 2097152 | tf_op jit(solution)/shard_map/all_to_all | solution.py:148
  95.8 36.1 %all-to-all-start.2 = ((bf16[128,64,128]{2,1,0:T(8,128)(2,1)}), bf16[128,64,128]{2,1,0:T(8,128)(2,1)S(1)}, u32[]{:S(2)}, u32[]{:S(2)}) async-start(bf16[128,64,128]{2,1,0:T(8,128)(2,1)} %bitcast.23), calls=%async_computation.2 | async-start | bytes 4194304 | tf_op jit(solution)/shard_map/all_to_all | solution.py:143

commit v14 on v12

--- a/solution.py
+++ b/solution.py
@@ -61,7 +61,7 @@
                 left_b, rows[:, (2 * m + 1) * side_len:(2 * m + 2) * side_len],
                 preferred_element_type=jnp.float32,
             )
-        out_ref[g] = acc.astype(jnp.bfloat16)
+        out_ref[:, pl.ds(g, 1), :] = acc.astype(jnp.bfloat16)[:, None, :]
 
 
 def match_blocks(pixels, mask_bits, coef_index, coef_table, tables, right_bands):
@@ -70,7 +70,7 @@
     flops = number * 4 * side_len * side_len * 6 * side_len
     return pl.pallas_call(
         match_kernel,
-        out_shape=jax.ShapeDtypeStruct(pixels.shape, jnp.bfloat16),
+        out_shape=jax.ShapeDtypeStruct((side_len, number, side_len), jnp.bfloat16),
         grid=(steps,),
         in_specs=[
             pl.BlockSpec(memory_space=pltpu.SMEM),
@@ -80,7 +80,7 @@
             pl.BlockSpec(tables.shape, lambda i: (0, 0, 0)),
             pl.BlockSpec(right_bands.shape, lambda i: (0, 0)),
         ],
-        out_specs=pl.BlockSpec((GROUP, side_len, side_len), lambda i: (i, 0, 0)),
+        out_specs=pl.BlockSpec((side_len, GROUP, side_len), lambda i: (0, i, 0)),
         cost_estimate=pl.CostEstimate(
             flops=flops, transcendentals=0, bytes_accessed=number * side_len * side_len * 8
         ),
@@ -110,7 +110,7 @@
     ]).astype(jnp.bfloat16).reshape(2, 2 * blocks_here)
     meta = jnp.pad(meta, ((0, 14), (0, side_len - 2 * blocks_here)))
     meta_blocks = jnp.broadcast_to(meta[:, None, :], (16, side_len, side_len))
-    payload = jnp.transpose(jnp.concatenate([matched_home, meta_blocks], axis=0), (1, 0, 2))
+    payload = jnp.concatenate([matched_home, jnp.transpose(meta_blocks, (1, 0, 2))], axis=1)
     received = lax.all_to_all(payload, both, split_axis=0, concat_axis=0, tiled=True)
     row_all = received[:, :blocks_here].reshape(devices * blocks_here, side_len)
     weight_all = received[:, blocks_here, :blocks_here].reshape(-1)

time: 137 us -> 139 us (1.015)
  Pallas kernels: 10.2 us -> 14.3 us
  local copies, waits for them, and re-layouts: 8.49 us -> 6.8 us
    pallas_call x1, Pallas kernels: 10.2 us -> 14.3 us  [match_blocks(): pl.pallas_call(match_kernel, out_shape=jax.ShapeDtypeStruct((side_len, nu...]
    transpose x1 -> x0, other arithmetic: 1.82 us -> none  [shards(): jnp.transpose(jnp.concatenate([matched_home, meta_blocks], axis=0), (1, 0...]
    concatenate x0 -> x1, other arithmetic: none -> 1.8 us  [shards(): jnp.concatenate([matched_home, jnp.transpose(meta_blocks, (1, 0, 2))], ax...]
    transpose x1, local copies, waits for them, and re-layouts: 1.69 us -> 0.07 us  [shards(): jnp.transpose(meta_blocks, (1, 0, 2))]
where the time goes in v14:
time: 139 us; the launch traced here: 137 us
  blocking collectives  45.4 us (33%)
  waiting for transfers between devices  29.5 us (21%)
  matrix products  24.8 us (18%)
  Pallas kernels  14.3 us (10%)
  starting transfers between devices  11.7 us (8%)
  local copies, waits for them, and re-layouts  6.8 us (5%)
  other arithmetic  3.72 us (3%)
    all_to_all x1, blocking collectives, shards(): lax.all_to_all(payload, both, split_axis=0, concat_axis=0, tiled=True)  45.4 us
    all_to_all x1, waiting for transfers between devices, shards(): lax.all_to_all(difference_row.reshape(devices, blocks_here, side_len), bo...  28.2 us
    dot_general x1, matrix products, shards(): jnp.dot(block_pick, template_row, preferred_element_type=jnp.float32)  14.3 us
    pallas_call x1, Pallas kernels, match_blocks(): pl.pallas_call(match_kernel, out_shape=jax.ShapeDtypeStruct((side_len, nu...  14.3 us
    dot_general x1, matrix products, shards(): numerator = jnp.dot(weighted, row_all, preferred_element_type=jnp.float32)  10.1 us
    all_to_all x1, starting transfers between devices, shards(): lax.all_to_all(difference_row.reshape(devices, blocks_here, side_len), bo...  6.3 us
    all_to_all x1, starting transfers between devices, shards(): lax.all_to_all(coadd_row.reshape(patches, CELLS, 1, side_len), 'patch', s...  5.39 us
    unnamed x5, local copies, waits for them, and re-layouts  5.04 us
  transfers between devices with their start and end apart: 2, of which 2 were waited for; matrix products, arithmetic and copies ran while one was open for 12% of the time, Pallas kernels for 0%

profile of v14, /device:TPU:32, one launch (start us, length us, event | category | flops | bytes accessed | tf_op | source)
XLA Modules:
  0.0 136.9 jit_solution(4323337917255512546)
XLA Ops:
  0.6 0.7 convert_bitcast_fusion.2
  1.3 0.1 pad.10.clone
  1.4 0.7 convert_bitcast_fusion
  2.1 0.1 convert_element_type.60
  2.2 0.8 copy.16
  3.0 0.7 reshape.67.coef_ref
  3.7 14.3 %shard_map.104 = bf16[128,64,128]{2,1,0:T(8,128)(2,1)} custom-call(s32[64]{0:T(128)} %index_ref.1, f32[576]{0:T(1024)} %reshape.67.coef_ref, bf16[64,128,128]{2,1,0:T(8,128)(2,1)} %pix_ref.1, s32[64,128,128]{2,1,0:T(8,128)} %mask_ref.1, f32[6,128,128]{2,1,0:T(8,128)} %constant.15.clone.tab_ref, bf16[128,768]{1,0:T(8,128)(2,1)} %constant.14.clone.right_ref), custom_call_target="tpu_custom_call" | custom-call | flops 3221225472 | bytes 8388608 | tf_op jit(solution)/shard_map/pallas_call | solution.py:71
  18.1 1.8 %pad_maximum_fusion = bf16[128,80,128]{2,1,0:T(8,128)(2,1)S(1)} fusion(bf16[128,16,128]{2,1,0:T(8,128)(2,1)S(1)} %transpose.18, bf16[128,64,128]{2,1,0:T(8,128)(2,1)} %shard_map.104), kind=kLoop, calls=%fused_computation.11 | loop fusion | flops 5242880 | bytes 5242880 | tf_op jit(solution)/shard_map/concatenate | solution.py:113
  19.9 45.4 %all_to_all.25 = bf16[128,80,128]{2,1,0:T(8,128)(2,1)S(1)} all-to-all(bf16[128,80,128]{2,1,0:T(8,128)(2,1)S(1)} %pad_maximum_fusion), channel_id=1, replica_groups=mesh['visit'=4,'patch'=32] {'visit','patch'}, dimensions={0} | all-to-all | bytes 5242880 | tf_op jit(solution)/shard_map/all_to_all | solution.py:114
  65.3 0.2 slice_reduce_fusion
  65.4 0.1 broadcast_in_dim.26
  65.5 0.5 fusion.21
  66.1 0.1 reshape.72
  66.1 0.1 reshape.73
  66.2 0.4 convolution_maximum_fusion
  66.7 0.3 slice.19
  67.0 10.1 %fusion.11 = f32[2048,128]{1,0:T(8,128)} fusion(bf16[8192,128]{1,0:T(8,128)(2,1)S(1)} %bitcast.22, s32[8192]{0:T(1024)S(1)} %multiply_add_fusion, bf16[8192]{0:T(1024)(128)(2,1)S(1)} %broadcast_in_dim.26, f32[2048]{0:T(1024)S(1)} %max.15), kind=kOutput, calls=%fused_computation.14 | convolution fusion | flops 4328783872 | bytes 3203072 | tf_op jit(solution)/shard_map/dot_general | solution.py:122
  77.1 5.4 %all-to-all-start.1 = ((f32[32,64,1,128]{3,1,2,0:T(8,128)}), f32[32,64,1,128]{3,1,2,0:T(8,128)S(1)}, u32[]{:S(2)}, u32[]{:S(2)}) async-start(f32[32,64,1,128]{3,1,2,0:T(8,128)} %bitcast.5), calls=%async_computation.1 | async-start | bytes 2097152 | tf_op jit(solution)/shard_map/all_to_all | solution.py:146
  82.5 14.3 %fusion.9 = bf16[8192,128]{1,0:T(8,128)(2,1)} fusion(s32[8192]{0:T(1024)S(1)} %multiply_add_fusion, bf16[8192,128]{1,0:T(8,128)(2,1)} %bitcast.23, f32[2048,128]{1,0:T(8,128)} %fusion.11), kind=kOutput, calls=%fused_computation.10 | convolution fusion | flops 4315152384 | bytes 5275648 | tf_op jit(solution)/shard_map/dot_general | solution.py:139
  96.8 1.3 all-to-all-done.1
  98.2 6.3 %all-to-all-start.2 = ((bf16[128,64,128]{2,1,0:T(8,128)(2,1)}), bf16[128,64,128]{2,1,0:T(8,128)(2,1)S(1)}, u32[]{:S(2)}, u32[]{:S(2)}) async-start(bf16[128,64,128]{2,1,0:T(8,128)(2,1)} %bitcast.21), calls=%async_computation.2 | async-start | bytes 4194304 | tf_op jit(solution)/shard_map/all_to_all | solution.py:141
  104.5 1.6 %copy.18 = f32[64,32,128]{2,1,0:T(8,128)} copy(f32[64,32,128]{2,0,1:T(8,128)S(1)} %bitcast.20) | data formatting | bytes 2097152
  106.0 28.2 %all-to-all-done.2 = bf16[128,64,128]{2,1,0:T(8,128)(2,1)S(1)} async-done(((bf16[128,64,128]{2,1,0:T(8,128)(2,1)}), bf16[128,64,128]{2,1,0:T(8,128)(2,1)S(1)}, u32[]{:S(2)}, u32[]{:S(2)}) %all-to-all-start.2) | async-done | bytes 2097184 | tf_op jit(solution)/shard_map/all_to_all | solution.py:141
  134.2 2.7 %copy.19 = bf16[64,128,128]{2,1,0:T(8,128)(2,1)} copy(bf16[64,128,128]{2,0,1:T(8,128)(2,1)S(1)} %bitcast.19) | data formatting | bytes 4194304
  (7 shorter events, 0.2 us)
Async XLA Ops:
  67.0 10.1 %copy-start = (bf16[128,64,128]{2,1,0:T(8,128)(2,1)}, bf16[128,64,128]{2,1,0:T(8,128)(2,1)S(1)}, u32[]{:S(2)}) copy-start(bf16[128,64,128]{2,1,0:T(8,128)(2,1)S(1)} %slice.19) | copy-start | bytes 6291460
  77.1 21.1 %all-to-all-start.1 = ((f32[32,64,1,128]{3,1,2,0:T(8,128)}), f32[32,64,1,128]{3,1,2,0:T(8,128)S(1)}, u32[]{:S(2)}, u32[]{:S(2)}) async-start(f32[32,64,1,128]{3,1,2,0:T(8,128)} %bitcast.5), calls=%async_computation.1 | async-start | bytes 2097152 | tf_op jit(solution)/shard_map/all_to_all | solution.py:146
  98.2 36.1 %all-to-all-start.2 = ((bf16[128,64,128]{2,1,0:T(8,128)(2,1)}), bf16[128,64,128]{2,1,0:T(8,128)(2,1)S(1)}, u32[]{:S(2)}, u32[]{:S(2)}) async-start(bf16[128,64,128]{2,1,0:T(8,128)(2,1)} %bitcast.21), calls=%async_computation.2 | async-start | bytes 4194304 | tf_op jit(solution)/shard_map/all_to_all | solution.py:141

commit v15 on v12

--- a/solution.py
+++ b/solution.py
@@ -8,7 +8,7 @@
 
 CELLS = 64
 KSIZE = 21
-GROUP = 16
+GROUP = 32
 
 
 gauss_widths = (1.0, 2.0, 3.5)

time: 137 us -> 137 us (level)
  no operation moved by 1% of the time
where the time goes in v15:
time: 137 us; the launch traced here: 134 us
  blocking collectives  45.4 us (33%)
  waiting for transfers between devices  29.5 us (22%)
  matrix products  24.8 us (18%)
  starting transfers between devices  11.7 us (9%)
  Pallas kernels  9.89 us (7%)
  local copies, waits for them, and re-layouts  8.49 us (6%)
  other arithmetic  3.75 us (3%)
    all_to_all x1, blocking collectives, shards(): lax.all_to_all(payload, both, split_axis=0, concat_axis=0, tiled=True)  45.4 us
    all_to_all x1, waiting for transfers between devices, shards(): lax.all_to_all(difference_row.reshape(devices, blocks_here, side_len), bo...  28.2 us
    dot_general x1, matrix products, shards(): jnp.dot(block_pick, template_row, preferred_element_type=jnp.float32)  14.3 us
    dot_general x1, matrix products, shards(): numerator = jnp.dot(weighted, row_all, preferred_element_type=jnp.float32)  10.1 us
    pallas_call x1, Pallas kernels, match_blocks(): pl.pallas_call(match_kernel, out_shape=jax.ShapeDtypeStruct(pixels.shape,...  9.89 us
    all_to_all x1, starting transfers between devices, shards(): lax.all_to_all(difference_row.reshape(devices, blocks_here, side_len), bo...  6.3 us
    all_to_all x1, starting transfers between devices, shards(): lax.all_to_all(coadd_row.reshape(patches, CELLS, 1, side_len), 'patch', s...  5.39 us
    unnamed x5, local copies, waits for them, and re-layouts  5.04 us
  transfers between devices with their start and end apart: 2, of which 2 were waited for; matrix products, arithmetic and copies ran while one was open for 12% of the time, Pallas kernels for 0%

profile of v15, /device:TPU:32, one launch (start us, length us, event | category | flops | bytes accessed | tf_op | source)
XLA Modules:
  0.0 134.3 jit_solution(9080053740323192206)
XLA Ops:
  0.6 0.7 convert_bitcast_fusion.2
  1.3 0.1 pad.10.clone
  1.4 0.7 convert_bitcast_fusion
  2.1 0.1 convert_element_type.60
  2.2 0.8 copy.17
  3.0 0.7 reshape.67.coef_ref
  3.7 9.9 %shard_map.104 = bf16[64,128,128]{2,1,0:T(8,128)(2,1)} custom-call(s32[64]{0:T(128)} %index_ref.1, f32[576]{0:T(1024)} %reshape.67.coef_ref, bf16[64,128,128]{2,1,0:T(8,128)(2,1)} %pix_ref.1, s32[64,128,128]{2,1,0:T(8,128)} %mask_ref.1, f32[6,128,128]{2,1,0:T(8,128)} %constant.15.clone.tab_ref, bf16[128,768]{1,0:T(8,128)(2,1)} %constant.14.clone.right_ref), custom_call_target="tpu_custom_call" | custom-call | flops 3221225472 | bytes 8388608 | tf_op jit(solution)/shard_map/pallas_call | solution.py:71
  13.7 1.8 %maximum_bitcast_fusion = bf16[128,80,128]{2,0,1:T(8,128)(2,1)S(1)} fusion(bf16[16,128,128]{2,1,0:T(8,128)(2,1)S(1)} %broadcast_in_dim.28, bf16[64,128,128]{2,1,0:T(8,128)(2,1)} %shard_map.104), kind=kLoop, calls=%fused_computation.11 | loop fusion | flops 1310720 | bytes 5242880 | tf_op jit(solution)/shard_map/transpose | solution.py:113
  15.5 1.7 %copy.18 = bf16[128,80,128]{2,1,0:T(8,128)(2,1)S(1)} copy(bf16[128,80,128]{2,0,1:T(8,128)(2,1)S(1)} %maximum_bitcast_fusion) | data formatting | bytes 5242880 | tf_op jit(solution)/shard_map/transpose | solution.py:113
  17.2 45.4 %all_to_all.25 = bf16[128,80,128]{2,1,0:T(8,128)(2,1)S(1)} all-to-all(bf16[128,80,128]{2,1,0:T(8,128)(2,1)S(1)} %copy.18), channel_id=1, replica_groups=mesh['visit'=4,'patch'=32] {'visit','patch'}, dimensions={0} | all-to-all | bytes 5242880 | tf_op jit(solution)/shard_map/all_to_all | solution.py:114
  62.6 0.2 slice_reduce_fusion
  62.8 0.1 broadcast_in_dim.42
  62.9 0.5 fusion.21
  63.4 0.1 reshape.72
  63.6 0.4 convolution_maximum_fusion
  64.1 0.3 slice.19
  64.4 10.1 %fusion.11 = f32[2048,128]{1,0:T(8,128)} fusion(bf16[8192,128]{1,0:T(8,128)(2,1)S(1)} %bitcast.24, s32[8192]{0:T(1024)S(1)} %multiply_add_fusion, bf16[8192]{0:T(1024)(128)(2,1)S(1)} %broadcast_in_dim.42, f32[2048]{0:T(1024)S(1)} %max.15), kind=kOutput, calls=%fused_computation.14 | convolution fusion | flops 4328783872 | bytes 3203072 | tf_op jit(solution)/shard_map/dot_general | solution.py:122
  74.5 5.4 %all-to-all-start.1 = ((f32[32,64,1,128]{3,1,2,0:T(8,128)}), f32[32,64,1,128]{3,1,2,0:T(8,128)S(1)}, u32[]{:S(2)}, u32[]{:S(2)}) async-start(f32[32,64,1,128]{3,1,2,0:T(8,128)} %bitcast.6), calls=%async_computation.1 | async-start | bytes 2097152 | tf_op jit(solution)/shard_map/all_to_all | solution.py:146
  79.9 14.3 %fusion.9 = bf16[8192,128]{1,0:T(8,128)(2,1)} fusion(s32[8192]{0:T(1024)S(1)} %multiply_add_fusion, bf16[8192,128]{1,0:T(8,128)(2,1)} %bitcast.25, f32[2048,128]{1,0:T(8,128)} %fusion.11), kind=kOutput, calls=%fused_computation.10 | convolution fusion | flops 4315152384 | bytes 5275648 | tf_op jit(solution)/shard_map/dot_general | solution.py:139
  94.2 1.3 all-to-all-done.1
  95.5 6.3 %all-to-all-start.2 = ((bf16[128,64,128]{2,1,0:T(8,128)(2,1)}), bf16[128,64,128]{2,1,0:T(8,128)(2,1)S(1)}, u32[]{:S(2)}, u32[]{:S(2)}) async-start(bf16[128,64,128]{2,1,0:T(8,128)(2,1)} %bitcast.23), calls=%async_computation.2 | async-start | bytes 4194304 | tf_op jit(solution)/shard_map/all_to_all | solution.py:141
  101.8 1.6 %copy.20 = f32[64,32,128]{2,1,0:T(8,128)} copy(f32[64,32,128]{2,0,1:T(8,128)S(1)} %bitcast.22) | data formatting | bytes 2097152
  103.4 28.2 %all-to-all-done.2 = bf16[128,64,128]{2,1,0:T(8,128)(2,1)S(1)} async-done(((bf16[128,64,128]{2,1,0:T(8,128)(2,1)}), bf16[128,64,128]{2,1,0:T(8,128)(2,1)S(1)}, u32[]{:S(2)}, u32[]{:S(2)}) %all-to-all-start.2) | async-done | bytes 2097184 | tf_op jit(solution)/shard_map/all_to_all | solution.py:141
  131.6 2.7 %copy.21 = bf16[64,128,128]{2,1,0:T(8,128)(2,1)} copy(bf16[64,128,128]{2,0,1:T(8,128)(2,1)S(1)} %bitcast.21) | data formatting | bytes 4194304
  (8 shorter events, 0.3 us)
Async XLA Ops:
  64.4 10.1 %copy-start = (bf16[128,64,128]{2,1,0:T(8,128)(2,1)}, bf16[128,64,128]{2,1,0:T(8,128)(2,1)S(1)}, u32[]{:S(2)}) copy-start(bf16[128,64,128]{2,1,0:T(8,128)(2,1)S(1)} %slice.19) | copy-start | bytes 6291460
  74.5 21.1 %all-to-all-start.1 = ((f32[32,64,1,128]{3,1,2,0:T(8,128)}), f32[32,64,1,128]{3,1,2,0:T(8,128)S(1)}, u32[]{:S(2)}, u32[]{:S(2)}) async-start(f32[32,64,1,128]{3,1,2,0:T(8,128)} %bitcast.6), calls=%async_computation.1 | async-start | bytes 2097152 | tf_op jit(solution)/shard_map/all_to_all | solution.py:146
  95.5 36.1 %all-to-all-start.2 = ((bf16[128,64,128]{2,1,0:T(8,128)(2,1)}), bf16[128,64,128]{2,1,0:T(8,128)(2,1)S(1)}, u32[]{:S(2)}, u32[]{:S(2)}) async-start(bf16[128,64,128]{2,1,0:T(8,128)(2,1)} %bitcast.23), calls=%async_computation.2 | async-start | bytes 4194304 | tf_op jit(solution)/shard_map/all_to_all | solution.py:141

commit v16 on v12

--- a/solution.py
+++ b/solution.py
@@ -114,10 +114,15 @@
     received = lax.all_to_all(payload, both, split_axis=0, concat_axis=0, tiled=True)
     row_all = received[:, :blocks_here].reshape(devices * blocks_here, side_len)
     weight_all = received[:, blocks_here, :blocks_here].reshape(-1)
-    owner_all = received[:, blocks_here, blocks_here:].reshape(-1).astype(jnp.int32)
-    cell_all = received[:, blocks_here + 1, :blocks_here].reshape(-1).astype(jnp.int32)
-    segment_all = owner_all * CELLS + cell_all
-    picks = segment_all[None, :] == jnp.arange(segments, dtype=jnp.int32)[:, None]
+    owner_code = received[:, blocks_here, blocks_here:].reshape(-1)
+    cell_code = received[:, blocks_here + 1, :blocks_here].reshape(-1)
+    owner_all = owner_code.astype(jnp.int32)
+    cell_all = cell_code.astype(jnp.int32)
+    segment_owner = (jnp.arange(segments) // CELLS).astype(jnp.bfloat16)
+    segment_cell = (jnp.arange(segments) % CELLS).astype(jnp.bfloat16)
+    picks = (owner_code[None, :] == segment_owner[:, None]) & (
+        cell_code[None, :] == segment_cell[:, None]
+    )
     weighted = jnp.where(picks, weight_all[None, :], jnp.zeros((), jnp.bfloat16))
     numerator = jnp.dot(weighted, row_all, preferred_element_type=jnp.float32)
     owner_pick = (owner_all[None, :] == jnp.arange(patches, dtype=jnp.int32)[:, None]).astype(
@@ -134,7 +139,8 @@
     coadd_row = numerator / jnp.maximum(weight_sum, 1.0)[:, None]
     template_row = coadd_row.astype(jnp.bfloat16)
     block_pick = (
-        segment_all[:, None] == jnp.arange(segments, dtype=jnp.int32)[None, :]
+        (owner_code[:, None] == segment_owner[None, :])
+        & (cell_code[:, None] == segment_cell[None, :])
     ).astype(jnp.bfloat16)
     block_template = jnp.dot(block_pick, template_row, preferred_element_type=jnp.float32)
     difference_row = (row_all.astype(jnp.float32) - block_template).astype(jnp.bfloat16)

time: 137 us -> 142 us (1.036)
  blocking collectives: 45.4 us -> 0 us
  waiting for transfers between devices: 29.5 us -> 63.6 us
  starting transfers between devices: 11.7 us -> 23.2 us
  matrix products: 24.8 us -> 27.7 us
  local copies, waits for them, and re-layouts: 8.49 us -> 10.5 us
    all_to_all x1 -> x0, blocking collectives: 45.4 us -> none  [shards(): lax.all_to_all(payload, both, split_axis=0, concat_axis=0, tiled=True)]
    all_to_all x0 -> x1, waiting for transfers between devices: none -> 35.4 us  [shards(): lax.all_to_all(payload, both, split_axis=0, concat_axis=0, tiled=True)]
    all_to_all x0 -> x1, starting transfers between devices: none -> 10.2 us  [shards(): lax.all_to_all(payload, both, split_axis=0, concat_axis=0, tiled=True)]
    dot_general x1, matrix products: 14.3 us -> 17.3 us  [shards(): jnp.dot(block_pick, template_row, preferred_element_type=jnp.float32)]
    transpose x1, local copies, waits for them, and re-layouts: 1.69 us -> 3.2 us  [shards(): jnp.transpose(jnp.concatenate([matched_home, meta_blocks], axis=0), (1, 0...]
  transfers between devices with their start and end apart: 2 -> 3, of which waited for: 2 -> 2; matrix products, arithmetic and copies ran while one was open for 12% -> 14% of each run, Pallas kernels for 0% -> 0%
where the time goes in v16:
time: 142 us; the launch traced here: 139 us
  waiting for transfers between devices  63.6 us (45%)
  matrix products  27.7 us (20%)
  starting transfers between devices  23.2 us (16%)
  local copies, waits for them, and re-layouts  10.5 us (7%)
  Pallas kernels  10.2 us (7%)
  other arithmetic  3.25 us (2%)
    all_to_all x1, waiting for transfers between devices, shards(): lax.all_to_all(payload, both, split_axis=0, concat_axis=0, tiled=True)  35.4 us
    all_to_all x1, waiting for transfers between devices, shards(): lax.all_to_all(difference_row.reshape(devices, blocks_here, side_len), bo...  28.2 us
    dot_general x1, matrix products, shards(): jnp.dot(block_pick, template_row, preferred_element_type=jnp.float32)  17.3 us
    all_to_all x1, starting transfers between devices, shards(): lax.all_to_all(payload, both, split_axis=0, concat_axis=0, tiled=True)  10.2 us
    pallas_call x1, Pallas kernels, match_blocks(): pl.pallas_call(match_kernel, out_shape=jax.ShapeDtypeStruct(pixels.shape,...  10.2 us
    dot_general x1, matrix products, shards(): numerator = jnp.dot(weighted, row_all, preferred_element_type=jnp.float32)  9.98 us
    all_to_all x1, starting transfers between devices, shards(): lax.all_to_all(difference_row.reshape(devices, blocks_here, side_len), bo...  7.63 us
    all_to_all x1, starting transfers between devices, shards(): lax.all_to_all(coadd_row.reshape(patches, CELLS, 1, side_len), 'patch', s...  5.4 us
  transfers between devices with their start and end apart: 3, of which 2 were waited for; matrix products, arithmetic and copies ran while one was open for 14% of the time, Pallas kernels for 0%

profile of v16, /device:TPU:32, one launch (start us, length us, event | category | flops | bytes accessed | tf_op | source)
XLA Modules:
  0.0 139.1 jit_solution(3539705419931289890)
XLA Ops:
  0.6 0.7 convert_bitcast_fusion.2
  1.3 0.1 pad.10.clone
  1.4 0.7 convert_bitcast_fusion
  2.1 0.1 convert_element_type.66
  2.2 0.8 copy.17
  3.0 0.7 reshape.95.coef_ref
  3.7 10.2 %shard_map.104 = bf16[64,128,128]{2,1,0:T(8,128)(2,1)} custom-call(s32[64]{0:T(128)} %index_ref.1, f32[576]{0:T(1024)} %reshape.95.coef_ref, bf16[64,128,128]{2,1,0:T(8,128)(2,1)} %pix_ref.1, s32[64,128,128]{2,1,0:T(8,128)} %mask_ref.1, f32[6,128,128]{2,1,0:T(8,128)} %constant.49.clone.tab_ref, bf16[128,768]{1,0:T(8,128)(2,1)} %constant.48.clone.right_ref), custom_call_target="tpu_custom_call" | custom-call | flops 3221225472 | bytes 8388608 | tf_op jit(solution)/shard_map/pallas_call | solution.py:71
  14.0 1.8 %maximum_bitcast_fusion = bf16[128,80,128]{2,0,1:T(8,128)(2,1)S(1)} fusion(bf16[16,128,128]{2,1,0:T(8,128)(2,1)S(1)} %broadcast_in_dim.28, bf16[64,128,128]{2,1,0:T(8,128)(2,1)} %shard_map.104), kind=kLoop, calls=%fused_computation.16 | loop fusion | flops 1310720 | bytes 5242880 | tf_op jit(solution)/shard_map/transpose | solution.py:113
  15.8 3.2 %copy.18 = bf16[128,80,128]{2,1,0:T(8,128)(2,1)} copy(bf16[128,80,128]{2,0,1:T(8,128)(2,1)S(1)} %maximum_bitcast_fusion) | data formatting | bytes 5242880 | tf_op jit(solution)/shard_map/transpose | solution.py:113
  19.0 10.2 %all-to-all-start = ((bf16[128,80,128]{2,1,0:T(8,128)(2,1)}), bf16[128,80,128]{2,1,0:T(8,128)(2,1)S(1)}, u32[]{:S(2)}, u32[]{:S(2)}) async-start(bf16[128,80,128]{2,1,0:T(8,128)(2,1)} %copy.18), calls=%async_computation | async-start | bytes 5242880 | tf_op jit(solution)/shard_map/all_to_all | solution.py:114
  29.3 35.4 %all-to-all-done = bf16[128,80,128]{2,1,0:T(8,128)(2,1)S(1)} async-done(((bf16[128,80,128]{2,1,0:T(8,128)(2,1)}), bf16[128,80,128]{2,1,0:T(8,128)(2,1)S(1)}, u32[]{:S(2)}, u32[]{:S(2)}) %all-to-all-start) | async-done | bytes 2621472 | tf_op jit(solution)/shard_map/all_to_all | solution.py:114
  64.6 0.6 slice_reduce_fusion.2
  65.3 0.1 eq.42
  65.4 0.1 eq.88
  65.4 0.1 broadcast_in_dim.42
  65.6 0.4 convolution_maximum_fusion
  66.0 0.3 slice.19
  66.3 10.0 %fusion.15 = f32[2048,128]{1,0:T(8,128)} fusion(bf16[8192,128]{1,0:T(8,128)(2,1)S(1)} %bitcast.24, bf16[8192]{0:T(1024)(128)(2,1)S(1)} %broadcast_in_dim.42, bf16[8192]{0:T(1024)(128)(2,1)S(1)} %eq.88, bf16[8192]{0:T(1024)(128)(2,1)S(1)} %eq.42, bf16[2048]{0:T(1024)(128)(2,1)S(1)} %get-tuple-element.10, bf16[2048]{0:T(1024)(128)(2,1)S(1)} %get-tuple-element.9, ...), kind=kOutput, calls=%fused_computation.19 | convolution fusion | flops 4429447168 | bytes 3211264 | tf_op jit(solution)/shard_map/dot_general | solution.py:127
  76.3 5.4 %all-to-all-start.1 = ((f32[32,64,1,128]{3,1,2,0:T(8,128)}), f32[32,64,1,128]{3,1,2,0:T(8,128)S(1)}, u32[]{:S(2)}, u32[]{:S(2)}) async-start(f32[32,64,1,128]{3,1,2,0:T(8,128)} %bitcast.6), calls=%async_computation.1 | async-start | bytes 2097152 | tf_op jit(solution)/shard_map/all_to_all | solution.py:152
  81.7 17.3 %fusion.13 = bf16[8192,128]{1,0:T(8,128)(2,1)} fusion(bf16[2048]{0:T(1024)(128)(2,1)S(1)} %get-tuple-element.10, bf16[2048]{0:T(1024)(128)(2,1)S(1)} %get-tuple-element.9, bf16[8192]{0:T(1024)(128)(2,1)S(1)} %eq.88, bf16[8192]{0:T(1024)(128)(2,1)S(1)} %eq.42, bf16[8192,128]{1,0:T(8,128)(2,1)} %bitcast.25, f32[2048,128]{1,0:T(8,128)} %fusion.15), kind=kOutput, calls=%fused_computation.15 | convolution fusion | flops 4415815680 | bytes 5283840 | tf_op jit(solution)/shard_map/dot_general | solution.py:145
  99.0 7.6 %all-to-all-start.2 = ((bf16[128,64,128]{2,1,0:T(8,128)(2,1)}), bf16[128,64,128]{2,1,0:T(8,128)(2,1)S(1)}, u32[]{:S(2)}, u32[]{:S(2)}) async-start(bf16[128,64,128]{2,1,0:T(8,128)(2,1)} %bitcast.23), calls=%async_computation.2 | async-start | bytes 4194304 | tf_op jit(solution)/shard_map/all_to_all | solution.py:147
  106.7 1.6 %copy.20 = f32[64,32,128]{2,1,0:T(8,128)} copy(f32[64,32,128]{2,0,1:T(8,128)S(1)} %bitcast.22) | data formatting | bytes 2097152
  108.2 28.2 %all-to-all-done.2 = bf16[128,64,128]{2,1,0:T(8,128)(2,1)S(1)} async-done(((bf16[128,64,128]{2,1,0:T(8,128)(2,1)}), bf16[128,64,128]{2,1,0:T(8,128)(2,1)S(1)}, u32[]{:S(2)}, u32[]{:S(2)}) %all-to-all-start.2) | async-done | bytes 2097184 | tf_op jit(solution)/shard_map/all_to_all | solution.py:147
  136.4 2.7 %copy.21 = bf16[64,128,128]{2,1,0:T(8,128)(2,1)} copy(bf16[64,128,128]{2,0,1:T(8,128)(2,1)S(1)} %bitcast.21) | data formatting | bytes 4194304
  (10 shorter events, 0.3 us)
Async XLA Ops:
  19.0 45.6 %all-to-all-start = ((bf16[128,80,128]{2,1,0:T(8,128)(2,1)}), bf16[128,80,128]{2,1,0:T(8,128)(2,1)S(1)}, u32[]{:S(2)}, u32[]{:S(2)}) async-start(bf16[128,80,128]{2,1,0:T(8,128)(2,1)} %copy.18), calls=%async_computation | async-start | bytes 5242880 | tf_op jit(solution)/shard_map/all_to_all | solution.py:114
  66.3 10.0 %copy-start = (bf16[128,64,128]{2,1,0:T(8,128)(2,1)}, bf16[128,64,128]{2,1,0:T(8,128)(2,1)S(1)}, u32[]{:S(2)}) copy-start(bf16[128,64,128]{2,1,0:T(8,128)(2,1)S(1)} %slice.19) | copy-start | bytes 6291460
  76.3 22.7 %all-to-all-start.1 = ((f32[32,64,1,128]{3,1,2,0:T(8,128)}), f32[32,64,1,128]{3,1,2,0:T(8,128)S(1)}, u32[]{:S(2)}, u32[]{:S(2)}) async-start(f32[32,64,1,128]{3,1,2,0:T(8,128)} %bitcast.6), calls=%async_computation.1 | async-start | bytes 2097152 | tf_op jit(solution)/shard_map/all_to_all | solution.py:152
  99.0 37.4 %all-to-all-start.2 = ((bf16[128,64,128]{2,1,0:T(8,128)(2,1)}), bf16[128,64,128]{2,1,0:T(8,128)(2,1)S(1)}, u32[]{:S(2)}, u32[]{:S(2)}) async-start(bf16[128,64,128]{2,1,0:T(8,128)(2,1)} %bitcast.23), calls=%async_computation.2 | async-start | bytes 4194304 | tf_op jit(solution)/shard_map/all_to_all | solution.py:147
